TPU v7x, 128 devices: a whole 4x4x4 slice. The times are simulated.
128 devices in a mesh: dp: 32 (over y, x, core), blk: 4 (over z).
Axes of the slice: x: 4, y: 4, z: 4, core: 2. Of those that a mesh axis runs over, the one named last changes fastest.
Arguments:
- prod_feat: bfloat16 [32, 3072, 768], P('dp', 'blk'), may hold values from -23 to 23
- prec_feat: bfloat16 [32, 3072, 768], P('dp', 'blk'), may hold values from -23 to 23
- matched: int32 [32, 3072], P('dp', 'blk'), may hold values from 0 to 3071, each once within a row
- row_weight: float32 [32, 3072], P('dp', 'blk'), may hold values from 0.2 to 28, as said below
- proj_prod: bfloat16 [768, 1024], replicated, may hold values from -0.21875 to 0.21875
- proj_prec: bfloat16 [768, 1024], replicated, may hold values from -0.21875 to 0.21875
Outputs:
- loss_value: float32 [], replicated
- grad_prod: float32 [768, 1024], P('dp', 'blk')
- grad_prec: float32 [768, 1024], P('dp', 'blk')
Inputs may be any that keep to these rules, and one draw needn't show every extreme that they name: `matched`: in each of the 32 groups the 3072 values are a permutation of 0 to 3071. `row_weight`: positive.
All inputs are finite; a program needn't handle non-finite values.
Results may differ from a plain program's by a relative error of at most 0.0027.
Values may be sent and summed in bfloat16 or wider, within the bound.
No kernel may reach another device: no remote copies, remote signals or barrier semaphores. Data moves between devices by JAX's collectives and lax.ppermute only.
A program may use at most 128 MiB of HBM per device.

v0:
```python
import jax
import jax.numpy as jnp
from jax import lax
from jax.sharding import PartitionSpec as P

EPS = 1e-06
LOGIT_SCALE = 50.0


def passed_along(block, axis, distance):
    devices = range(lax.axis_size(axis))
    route = [((i - distance) % len(devices), i) for i in devices]
    return lax.ppermute(block, axis, route)


def embed_rows(features, weight):
    projected_raw = jnp.dot(features, weight, preferred_element_type=jnp.float32)
    radius = jnp.sqrt(jnp.sum(projected_raw * projected_raw, axis=1, keepdims=True) + EPS)
    unit_vec = projected_raw / radius
    return (unit_vec, unit_vec.astype(jnp.bfloat16), radius)


def similarity(queries, key_rows):
    return LOGIT_SCALE * lax.dot_general(
        queries, key_rows, (((1,), (1,)), ((), ())), preferred_element_type=jnp.float32
    )


def coefficient(scores, matches, weights, totals):
    probability = jnp.exp(scores - LOGIT_SCALE) / totals[:, None]
    return (weights[:, None] * (probability - matches.astype(jnp.float32))).astype(jnp.bfloat16)


def back_norm(unit_vec, radius, gradient):
    projected = jnp.sum(unit_vec * gradient, axis=1, keepdims=True)
    return ((gradient - unit_vec * projected) / radius).astype(jnp.bfloat16)


def per_device(prod_feat, prec_feat, matched, row_weight, proj_prod, proj_prec):
    feat_prod = prod_feat[0]
    feat_prec = prec_feat[0]
    targets = matched[0]
    weights = row_weight[0]
    row_count = feat_prod.shape[0]
    cycle_size = lax.axis_size("blk")
    cycle_pos = lax.axis_index("blk")
    unit_prod, unit16_prod, radius_prod = embed_rows(feat_prod, proj_prod)
    unit_prec, unit16_prec, radius_prec = embed_rows(feat_prec, proj_prec)
    shard_rows = lax.all_gather(unit16_prec, "blk", axis=0, tiled=True)
    scores = similarity(unit16_prod, shard_rows)
    columns = lax.iota(jnp.int32, shard_rows.shape[0])
    matches = targets[:, None] == columns[None, :]
    total_now = jnp.sum(jnp.exp(scores - LOGIT_SCALE), axis=1)
    positive_now = jnp.sum(jnp.where(matches, scores, 0.0), axis=1)
    losses = LOGIT_SCALE + jnp.log(total_now) - positive_now
    loss_local = jnp.sum(weights * losses)
    weight_local = jnp.sum(weights)
    loss_sum, weight_total = lax.psum((loss_local, weight_local), ("dp", "blk"))

    def cycle_turn(turn_index, cycle_state):
        tile_now, carried, prod_acc = cycle_state
        source = jnp.remainder(cycle_pos - turn_index, cycle_size)
        columns = source * row_count + lax.iota(jnp.int32, row_count)
        scores = similarity(unit16_prod, tile_now)
        matches = targets[:, None] == columns[None, :]
        coeffs = coefficient(scores, matches, weights, total_now)
        prod_acc = prod_acc + jnp.dot(coeffs, tile_now, preferred_element_type=jnp.float32)
        carried = carried + lax.dot_general(
            coeffs, unit16_prod, (((0,), (0,)), ((), ())), preferred_element_type=jnp.float32
        )
        tile_now = passed_along(tile_now, "blk", 1)
        carried = passed_along(carried, "blk", 1)
        return (tile_now, carried, prod_acc)

    zero_embed = jnp.zeros(unit_prec.shape, jnp.float32)
    final_state = lax.fori_loop(0, cycle_size, cycle_turn, (unit16_prec, zero_embed, zero_embed))
    prec_sum = final_state[1]
    prod_sum = final_state[2]
    dir_prod = back_norm(unit_prod, radius_prod, LOGIT_SCALE * prod_sum)
    dir_prec = back_norm(unit_prec, radius_prec, LOGIT_SCALE * prec_sum)
    head_prod = lax.dot_general(
        feat_prod, dir_prod, (((0,), (0,)), ((), ())), preferred_element_type=jnp.float32
    )
    head_prec = lax.dot_general(
        feat_prec, dir_prec, (((0,), (0,)), ((), ())), preferred_element_type=jnp.float32
    )
    head_prod = head_prod / weight_total
    head_prec = head_prec / weight_total
    partial_blk = (
        lax.psum_scatter(head_prod, "blk", scatter_dimension=1, tiled=True),
        lax.psum_scatter(head_prec, "blk", scatter_dimension=1, tiled=True),
    )
    summed_prod, summed_prec = (
        lax.psum_scatter(partial_blk[0], "dp", scatter_dimension=0, tiled=True),
        lax.psum_scatter(partial_blk[1], "dp", scatter_dimension=0, tiled=True),
    )
    return (loss_sum / weight_total, summed_prod, summed_prec)


def solution(mesh):
    placed = (P("dp", "blk", None), P("dp", "blk", None), P("dp", "blk"), P("dp", "blk"), P(), P())
    return jax.shard_map(
        per_device,
        mesh=mesh,
        in_specs=placed,
        out_specs=(P(), P("dp", "blk"), P("dp", "blk")),
        check_vma=False,
    )
```

profile of v0, /device:TPU:0, one launch (start us, length us, event | category | flops | bytes accessed | tf_op | source)
XLA Modules:
  0.0 872.1 jit_solution(11993308056530438230)
XLA Ops:
  8.6 2.7 multiply_reduce_fusion.2
  15.4 2.7 multiply_reduce_fusion.3
  20.2 63.0 %all-gather.2.cloned.1.call-done = bf16[3072,1024]{1,0:T(8,128)(2,1)} async-done(((bf16[768,1024]{1,0:T(8,128)(2,1)}), bf16[3072,1024]{1,0:T(8,128)(2,1)}) %all-gather.2.cloned.1.call-update) | async-done | bytes 6291472 | tf_op jit(solution)/shard_map/all_gather | solution.py:49
  83.2 9.9 %exponential_reduce_fusion = (f32[768]{0:T(1024)S(1)}, f32[768]{0:T(1024)S(1)}) fusion(s32[768]{0:T(1024)S(1)} %reduce.4, bf16[768,1024]{1,0:T(8,128)(2,1)S(1)} %fusion.14, bf16[3072,1024]{1,0:T(8,128)(2,1)} %all-gather.2.cloned.1.call-done), kind=kOutput, calls=%fused_computation.6 | convolution fusion | flops 4845991936 | bytes 7873536 | tf_op jit(solution)/shard_map/dot_general | solution.py:24
  95.2 456.2 %while.20 = (s32[]{:T(128)}, bf16[768,1024]{1,0:T(8,128)(2,1)S(1)}, f32[768,1024]{1,0:T(8,128)}, f32[768,1024]{1,0:T(8,128)}, f32[1,768]{1,0:T(1,128)S(1)}, /*in...) while((s32[]{:T(128)}, bf16[768,1024]{1,0:T(8,128)(2,1)S(1)}, ...), condition=%wide.region_9.10_spmd.clone, body=%wide.region_8.9_spmd.clone.sunk | while | flops 3630957312 | bytes 55471532 | solution.py:76
  96.4 3.8 multiply_convert_fusion.2
  100.2 5.4 convolution_add_fusion.2
  108.0 4.8 select_add_fusion.2
  112.8 97.8 %collective-permute-done = bf16[768,1024]{1,0:T(8,128)(2,1)S(1)} collective-permute-done((bf16[768,1024]{1,0:T(8,128)(2,1)}, bf16[768,1024]{1,0:T(8,128)(2,1)S(1)}, u32[]{:S(2)}, u32[]{:S(2)}) %collective-permute-start) | collective-permute-done | bytes 1572896 | tf_op jit(solution)/shard_map/while/body/eval_jaxpr/ppermute | solution.py:13
  211.8 3.8 multiply_convert_fusion.2
  215.6 5.4 convolution_add_fusion.2
  222.2 5.8 select_add_fusion.2
  228.0 97.1 %collective-permute-done = bf16[768,1024]{1,0:T(8,128)(2,1)S(1)} collective-permute-done((bf16[768,1024]{1,0:T(8,128)(2,1)}, bf16[768,1024]{1,0:T(8,128)(2,1)S(1)}, u32[]{:S(2)}, u32[]{:S(2)}) %collective-permute-start) | collective-permute-done | bytes 1572896 | tf_op jit(solution)/shard_map/while/body/eval_jaxpr/ppermute | solution.py:13
  326.4 3.8 multiply_convert_fusion.2
  330.1 5.4 convolution_add_fusion.2
  335.6 5.8 select_add_fusion.2
  341.4 97.3 %collective-permute-done = bf16[768,1024]{1,0:T(8,128)(2,1)S(1)} collective-permute-done((bf16[768,1024]{1,0:T(8,128)(2,1)}, bf16[768,1024]{1,0:T(8,128)(2,1)S(1)}, u32[]{:S(2)}, u32[]{:S(2)}) %collective-permute-start) | collective-permute-done | bytes 1572896 | tf_op jit(solution)/shard_map/while/body/eval_jaxpr/ppermute | solution.py:13
  440.0 3.8 multiply_convert_fusion.2
  443.8 5.4 convolution_add_fusion.2
  449.2 5.8 select_add_fusion.2
  455.0 96.4 %collective-permute-done = bf16[768,1024]{1,0:T(8,128)(2,1)S(1)} collective-permute-done((bf16[768,1024]{1,0:T(8,128)(2,1)}, bf16[768,1024]{1,0:T(8,128)(2,1)S(1)}, u32[]{:S(2)}, u32[]{:S(2)}) %collective-permute-start) | collective-permute-done | bytes 1572896 | tf_op jit(solution)/shard_map/while/body/eval_jaxpr/ppermute | solution.py:13
  551.4 3.5 multiply_reduce_fusion
  555.5 65.3 %all-reduce = (f32[]{:T(128)}, f32[]{:T(128)}) all-reduce(f32[]{:T(128)} %multiply_reduce_fusion.4, f32[]{:T(128)} %get-tuple-element.266), channel_id=1, replica_groups=mesh['dp'=32,'blk'=4] {'dp','blk'}, use_global_device_ids=true, to_apply=%region_5.6 | all-reduce | flops 2 | bytes 16 | tf_op jit(solution)/shard_map/psum | solution.py:58
  620.9 7.0 divide_bitcast_fusion
  628.0 3.5 multiply_reduce_fusion.1
  633.1 4.3 divide_bitcast_fusion.1
  637.4 25.1 %reduce-scatter.11.cloned.1.call-done = f32[768,256]{0,1:T(8,128)} async-done(((f32[768,1024]{0,1:T(8,128)}), f32[768,256]{0,1:T(8,128)}) %reduce-scatter.11.cloned.1.call-update) | async-done | bytes 786448 | tf_op jit(solution)/shard_map/reduce_scatter | solution.py:91
  662.5 2.3 copy.15
  664.9 38.1 %reduce-scatter.9.cloned.1.call-done = f32[768,256]{0,1:T(8,128)} async-done(((f32[768,1024]{0,1:T(8,128)}), f32[768,256]{0,1:T(8,128)}) %reduce-scatter.9.cloned.1.call-update) | async-done | bytes 786448 | tf_op jit(solution)/shard_map/reduce_scatter | solution.py:90
  703.0 2.3 copy.13
  706.7 77.1 %reduce-scatter.15.cloned.1.call-done = f32[24,256]{1,0:T(8,128)} async-done(((f32[768,256]{1,0:T(8,128)}), f32[24,256]{1,0:T(8,128)}) %reduce-scatter.15.cloned.1.call-update) | async-done | bytes 24592
  783.8 80.6 %reduce-scatter.13.cloned.1.call-done = f32[24,256]{1,0:T(8,128)} async-done(((f32[768,256]{1,0:T(8,128)}), f32[24,256]{1,0:T(8,128)}) %reduce-scatter.13.cloned.1.call-update) | async-done | bytes 24592
  (87 shorter events, 20.4 us)
Async XLA Ops:
  7.2 76.0 %all-gather.2.cloned.1.call-start = ((), (), s32[]{:S(2)}) async-start(), calls=%async_computation.4 | async-start | bytes 7864320 | tf_op jit(solution)/shard_map/all_gather | solution.py:49
  11.3 1.7 copy-start.2
  13.0 1.7 copy-start.9
  13.0 1.7 copy-start.8
  13.0 2.4 copy-start.10
  14.7 647.9 %reduce-scatter.11.cloned.1.call-start = ((), (), s32[]{:S(2)}) async-start(), calls=%async_computation.6 | async-start | bytes 3932160 | tf_op jit(solution)/shard_map/reduce_scatter | solution.py:91
  18.1 1.6 copy-start.3
  20.2 63.0 %copy-start.6 = (bf16[768,1024]{1,0:T(8,128)(2,1)}, bf16[768,1024]{1,0:T(8,128)(2,1)S(1)}, u32[]{:S(2)}) copy-start(bf16[768,1024]{1,0:T(8,128)(2,1)S(1)} %fusion.14) | copy-start | bytes 4718596
  93.1 2.1 copy-start.1
  96.4 3.8 copy-start.7
  100.2 5.5 copy-start.13
  105.6 104.9 %collective-permute-start.1 = (f32[768,1024]{1,0:T(8,128)}, f32[768,1024]{1,0:T(8,128)}, u32[]{:S(2)}, u32[]{:S(2)}) collective-permute-start(f32[768,1024]{1,0:T(8,128)} %convolution_add_fusion.2), channel_id=1, source_target_pairs={{3,0},{0,1},{1,2},{2,3},{7,4},{4,5},{5,6},{6,7},{11,8},{8,9},{9,10... | collective-permute-start | bytes 9437192 | tf_op jit(solution)/shard_map/while/body/eval_jaxpr/ppermute | solution.py:13
  106.7 103.9 %collective-permute-start = (bf16[768,1024]{1,0:T(8,128)(2,1)}, bf16[768,1024]{1,0:T(8,128)(2,1)S(1)}, u32[]{:S(2)}, u32[]{:S(2)}) collective-permute-start(bf16[768,1024]{1,0:T(8,128)(2,1)} %copy.22), channel_id=1, source_target_pairs={{3,0},{0,1},{1,2},{2,3},{7,4},{4,5},{5,6},{6,7},{11,8},{8,9},{9,10... | collective-permute-start | bytes 4718600 | tf_op jit(solution)/shard_map/while/body/eval_jaxpr/ppermute | solution.py:13
  211.8 3.8 copy-start.7
  215.6 5.5 copy-start.13
  221.1 104.1 %collective-permute-start.1 = (f32[768,1024]{1,0:T(8,128)}, f32[768,1024]{1,0:T(8,128)}, u32[]{:S(2)}, u32[]{:S(2)}) collective-permute-start(f32[768,1024]{1,0:T(8,128)} %convolution_add_fusion.2), channel_id=1, source_target_pairs={{3,0},{0,1},{1,2},{2,3},{7,4},{4,5},{5,6},{6,7},{11,8},{8,9},{9,10... | collective-permute-start | bytes 9437192 | tf_op jit(solution)/shard_map/while/body/eval_jaxpr/ppermute | solution.py:13
  221.1 104.1 %collective-permute-start = (bf16[768,1024]{1,0:T(8,128)(2,1)}, bf16[768,1024]{1,0:T(8,128)(2,1)S(1)}, u32[]{:S(2)}, u32[]{:S(2)}) collective-permute-start(bf16[768,1024]{1,0:T(8,128)(2,1)} %copy.22), channel_id=1, source_target_pairs={{3,0},{0,1},{1,2},{2,3},{7,4},{4,5},{5,6},{6,7},{11,8},{8,9},{9,10... | collective-permute-start | bytes 4718600 | tf_op jit(solution)/shard_map/while/body/eval_jaxpr/ppermute | solution.py:13
  326.4 3.8 copy-start.7
  330.1 5.5 copy-start.13
  335.6 103.1 %collective-permute-start.1 = (f32[768,1024]{1,0:T(8,128)}, f32[768,1024]{1,0:T(8,128)}, u32[]{:S(2)}, u32[]{:S(2)}) collective-permute-start(f32[768,1024]{1,0:T(8,128)} %convolution_add_fusion.2), channel_id=1, source_target_pairs={{3,0},{0,1},{1,2},{2,3},{7,4},{4,5},{5,6},{6,7},{11,8},{8,9},{9,10... | collective-permute-start | bytes 9437192 | tf_op jit(solution)/shard_map/while/body/eval_jaxpr/ppermute | solution.py:13
  335.6 103.1 %collective-permute-start = (bf16[768,1024]{1,0:T(8,128)(2,1)}, bf16[768,1024]{1,0:T(8,128)(2,1)S(1)}, u32[]{:S(2)}, u32[]{:S(2)}) collective-permute-start(bf16[768,1024]{1,0:T(8,128)(2,1)} %copy.22), channel_id=1, source_target_pairs={{3,0},{0,1},{1,2},{2,3},{7,4},{4,5},{5,6},{6,7},{11,8},{8,9},{9,10... | collective-permute-start | bytes 4718600 | tf_op jit(solution)/shard_map/while/body/eval_jaxpr/ppermute | solution.py:13
  440.0 3.8 copy-start.7
  443.7 5.5 copy-start.13
  449.2 102.2 %collective-permute-start.1 = (f32[768,1024]{1,0:T(8,128)}, f32[768,1024]{1,0:T(8,128)}, u32[]{:S(2)}, u32[]{:S(2)}) collective-permute-start(f32[768,1024]{1,0:T(8,128)} %convolution_add_fusion.2), channel_id=1, source_target_pairs={{3,0},{0,1},{1,2},{2,3},{7,4},{4,5},{5,6},{6,7},{11,8},{8,9},{9,10... | collective-permute-start | bytes 9437192 | tf_op jit(solution)/shard_map/while/body/eval_jaxpr/ppermute | solution.py:13
  449.2 102.2 %collective-permute-start = (bf16[768,1024]{1,0:T(8,128)(2,1)}, bf16[768,1024]{1,0:T(8,128)(2,1)S(1)}, u32[]{:S(2)}, u32[]{:S(2)}) collective-permute-start(bf16[768,1024]{1,0:T(8,128)(2,1)} %copy.22), channel_id=1, source_target_pairs={{3,0},{0,1},{1,2},{2,3},{7,4},{4,5},{5,6},{6,7},{11,8},{8,9},{9,10... | collective-permute-start | bytes 4718600 | tf_op jit(solution)/shard_map/while/body/eval_jaxpr/ppermute | solution.py:13
  551.4 69.4 %copy-start.11 = (bf16[1,768,768]{2,1,0:T(8,128)(2,1)S(1)}, bf16[1,768,768]{2,1,0:T(8,128)(2,1)}, u32[]{:S(2)}) copy-start(bf16[1,768,768]{2,1,0:T(8,128)(2,1)} %param.9) | copy-start | bytes 3538948
  627.9 3.6 copy-start.12
  627.9 75.1 %reduce-scatter.9.cloned.1.call-start = ((), (), s32[]{:S(2)}) async-start(), calls=%async_computation.5 | async-start | bytes 3932160 | tf_op jit(solution)/shard_map/reduce_scatter | solution.py:90
  628.0 4.0 copy-start.4
  628.0 5.1 copy-start.5
  637.4 146.4 %reduce-scatter.15.cloned.1.call-start = ((), (), s32[]{:S(2)}) async-start(), calls=%async_computation.8 | async-start | bytes 811008
  664.8 199.6 %reduce-scatter.13.cloned.1.call-start = ((), (), s32[]{:S(2)}) async-start(), calls=%async_computation.7 | async-start | bytes 811008
  (1 other events, 1.4 us)
Sparse Core Ops, SparseCore 0:
  14.8 68.3 all-gather.1
  628.1 34.4 reduce-scatter.10
  664.9 38.0 reduce-scatter.8
  706.9 76.8 reduce-scatter.14
  787.7 76.6 reduce-scatter.12
where the time goes:
time: 873 us; the launch traced here: 872 us
  waiting for transfers between devices  673 us (77%)
  matrix products  85.6 us (10%)
  blocking collectives  65.3 us (7%)
  local copies, waits for them, and re-layouts  17.7 us (2%)
  between operations  16.4 us (2%)
  other arithmetic  10.5 us (1%)
    ppermute x8, waiting for transfers between devices, passed_along(): return lax.ppermute(block, axis, route)  389 us
    unnamed x7, waiting for transfers between devices  158 us
    psum x1, blocking collectives, per_device(): loss_sum, weight_total = lax.psum((loss_local, weight_local), ('dp', 'blk'))  65.3 us
    all_gather x1, waiting for transfers between devices, per_device(): shard_rows = lax.all_gather(unit16_prec, 'blk', axis=0, tiled=True)  63 us
    reduce_scatter x1, waiting for transfers between devices, per_device(): lax.psum_scatter(head_prod, 'blk', scatter_dimension=1, tiled=True)  38.1 us
    reduce_scatter x1, waiting for transfers between devices, per_device(): lax.psum_scatter(head_prec, 'blk', scatter_dimension=1, tiled=True)  25.1 us
    dot_general x5, matrix products, similarity(): lax.dot_general(queries, key_rows, (((1,), (1,)), ((), ())), preferred_el...  24.9 us
    dot_general x4, matrix products, cycle_turn(): jnp.dot(coeffs, tile_now, preferred_element_type=jnp.float32)  22.2 us
  transfers between devices with their start and end apart: 13, of which 9 were waited for; matrix products, arithmetic and copies ran while one was open for 4% of the time, Pallas kernels for 0%

commit v1 on v0

v1 whole, which is shorter than its diff:
```python
import jax
import jax.numpy as jnp
from jax import lax
from jax.sharding import PartitionSpec as P

EPS = 1e-06
LOGIT_SCALE = 50.0


def embed_rows(features, weight):
    projected_raw = jnp.dot(features, weight, preferred_element_type=jnp.float32)
    radius = jnp.sqrt(jnp.sum(projected_raw * projected_raw, axis=1, keepdims=True) + EPS)
    unit_vec = projected_raw / radius
    return (unit_vec, unit_vec.astype(jnp.bfloat16), radius)


def similarity(queries, key_rows):
    return LOGIT_SCALE * lax.dot_general(
        queries, key_rows, (((1,), (1,)), ((), ())), preferred_element_type=jnp.float32
    )


def coefficient(scores, matches, weights, totals):
    probability = jnp.exp(scores - LOGIT_SCALE) / totals[:, None]
    return (weights[:, None] * (probability - matches.astype(jnp.float32))).astype(jnp.bfloat16)


def back_norm(unit_vec, radius, gradient):
    projected = jnp.sum(unit_vec * gradient, axis=1, keepdims=True)
    return ((gradient - unit_vec * projected) / radius).astype(jnp.bfloat16)


def spread_blocks(head, dp_size, blk_size):
    feat, embed = head.shape
    tiles = head.reshape(dp_size, feat // dp_size, blk_size, embed // blk_size)
    tiles = tiles.transpose(0, 2, 1, 3)
    return tiles.reshape(dp_size * blk_size * (feat // dp_size), embed // blk_size)


def per_device(prod_feat, prec_feat, matched, row_weight, proj_prod, proj_prec):
    feat_prod = prod_feat[0]
    feat_prec = prec_feat[0]
    targets = matched[0]
    weights = row_weight[0]
    dp_size = lax.axis_size("dp")
    blk_size = lax.axis_size("blk")
    unit_prod, unit16_prod, radius_prod = embed_rows(feat_prod, proj_prod)
    feat_prec_all = lax.all_gather(feat_prec, "blk", axis=0, tiled=True)
    unit_prec, unit16_prec, radius_prec = embed_rows(feat_prec_all, proj_prec)
    scores = similarity(unit16_prod, unit16_prec)
    columns = lax.iota(jnp.int32, unit16_prec.shape[0])
    matches = targets[:, None] == columns[None, :]
    totals = jnp.sum(jnp.exp(scores - LOGIT_SCALE), axis=1)
    positive = jnp.sum(jnp.where(matches, scores, 0.0), axis=1)
    losses = LOGIT_SCALE + jnp.log(totals) - positive
    loss_local = jnp.sum(weights * losses)
    weight_local = jnp.sum(weights)
    loss_sum, weight_total = lax.psum((loss_local, weight_local), ("dp", "blk"))
    coeffs = coefficient(scores, matches, weights, totals)
    grad_unit_prod = LOGIT_SCALE * jnp.dot(coeffs, unit16_prec, preferred_element_type=jnp.float32)
    grad_prec_part = LOGIT_SCALE * lax.dot_general(
        coeffs, unit16_prod, (((0,), (0,)), ((), ())), preferred_element_type=jnp.float32
    )
    dir_prod = back_norm(unit_prod, radius_prod, grad_unit_prod)
    dir_prec = back_norm(unit_prec, radius_prec, grad_prec_part)
    head_prod = lax.dot_general(
        feat_prod, dir_prod, (((0,), (0,)), ((), ())), preferred_element_type=jnp.float32
    )
    head_prec = lax.dot_general(
        feat_prec_all, dir_prec, (((0,), (0,)), ((), ())), preferred_element_type=jnp.float32
    )
    summed_prod = lax.psum_scatter(
        spread_blocks(head_prod, dp_size, blk_size), ("dp", "blk"), scatter_dimension=0, tiled=True
    )
    summed_prec = lax.psum_scatter(
        spread_blocks(head_prec, dp_size, blk_size), ("dp", "blk"), scatter_dimension=0, tiled=True
    )
    return (loss_sum / weight_total, summed_prod / weight_total, summed_prec / weight_total)


def solution(mesh):
    placed = (P("dp", "blk", None), P("dp", "blk", None), P("dp", "blk"), P("dp", "blk"), P(), P())
    return jax.shard_map(
        per_device,
        mesh=mesh,
        in_specs=placed,
        out_specs=(P(), P("dp", "blk"), P("dp", "blk")),
        check_vma=False,
    )
```

time: 873 us -> 557 us (0.64)
  waiting for transfers between devices: 673 us -> 380 us
  matrix products: 85.6 us -> 67 us
    ppermute x8 -> x0, waiting for transfers between devices: 389 us -> none  [passed_along(): return lax.ppermute(block, axis, route)]
    reduce_scatter x2, waiting for transfers between devices: 63.2 us -> 329 us  [the longest x1 210 us: per_device(): lax.psum_scatter(spread_blocks(head_prec, dp_size, blk_size), ('dp', 'blk...]
    unnamed x7 -> x3, waiting for transfers between devices: 158 us -> 0.71 us
    dot_general x5 -> x1, matrix products: 24.9 us -> 9.72 us  [similarity(): lax.dot_general(queries, key_rows, (((1,), (1,)), ((), ())), preferred_el...]
    all_gather x1, waiting for transfers between devices: 63 us -> 50.2 us  [per_device(): feat_prec_all = lax.all_gather(feat_prec, 'blk', axis=0, tiled=True)]
    unnamed x26 -> x10, local copies, waits for them, and re-layouts: 10.8 us -> 0.03 us
    dot_general x9 -> x3, matrix products: 51 us -> 41.2 us  [the longest x1 15.1 us: per_device(): lax.dot_general(coeffs, unit16_prod, (((0,), (0,)), ((), ())), preferred_...]
  transfers between devices with their start and end apart: 13 -> 3, of which waited for: 9 -> 3; matrix products, arithmetic and copies ran while one was open for 4% -> 6% of each run, Pallas kernels for 0% -> 0%
where the time goes in v1:
time: 557 us; the launch traced here: 556 us
  waiting for transfers between devices  380 us (68%)
  matrix products  67 us (12%)
  blocking collectives  64.6 us (12%)
  local copies, waits for them, and re-layouts  21.4 us (4%)
  between operations  16.3 us (3%)
  other arithmetic  6.71 us (1%)
    reduce_scatter x1, waiting for transfers between devices, per_device(): lax.psum_scatter(spread_blocks(head_prec, dp_size, blk_size), ('dp', 'blk...  210 us
    reduce_scatter x1, waiting for transfers between devices, per_device(): lax.psum_scatter(spread_blocks(head_prod, dp_size, blk_size), ('dp', 'blk...  119 us
    psum x1, blocking collectives, per_device(): loss_sum, weight_total = lax.psum((loss_local, weight_local), ('dp', 'blk'))  64.6 us
    all_gather x1, waiting for transfers between devices, per_device(): feat_prec_all = lax.all_gather(feat_prec, 'blk', axis=0, tiled=True)  50.2 us
    dot_general x1, matrix products, per_device(): lax.dot_general(coeffs, unit16_prod, (((0,), (0,)), ((), ())), preferred_...  15.1 us
    dot_general x1, matrix products, per_device(): jnp.dot(coeffs, unit16_prec, preferred_element_type=jnp.float32)  13.6 us
    dot_general x1, matrix products, per_device(): lax.dot_general(feat_prec_all, dir_prec, (((0,), (0,)), ((), ())), prefer...  12.6 us
    dot_general x2, matrix products, embed_rows(): jnp.dot(features, weight, preferred_element_type=jnp.float32)  12.2 us
  transfers between devices with their start and end apart: 3, of which 3 were waited for; matrix products, arithmetic and copies ran while one was open for 6% of the time, Pallas kernels for 0%

profile of v1, /device:TPU:0, one launch (start us, length us, event | category | flops | bytes accessed | tf_op | source)
XLA Modules:
  0.0 556.1 jit_solution(3797390125440202433)
XLA Ops:
  7.2 0.0 copy-start
  7.2 0.0 all-gather.3.cloned.1.call-start
  7.2 0.7 all-gather.3.cloned.1.call-update
  7.9 0.0 reduce-scatter.3.cloned.1.call-start
  8.0 0.7 reduce.2
  8.7 1.3 fusion.20
  10.0 4.8 multiply_reduce_fusion.3
  14.8 50.2 %all-gather.3.cloned.1.call-done = bf16[1,3072,768]{2,1,0:T(8,128)(2,1)} async-done(((bf16[1,768,768]{2,1,0:T(8,128)(2,1)}), bf16[1,3072,768]{2,1,0:T(8,128)(2,1)}) %all-gather.3.cloned.1.call-update) | async-done | bytes 4718608 | tf_op jit(solution)/shard_map/all_gather | solution.py:48
  65.0 0.0 copy-done
  65.0 7.4 %multiply_reduce_fusion.1 = (f32[3072]{0:T(1024)S(1)}, f32[3072,1024]{0,1:T(8,128)S(1)}) fusion(bf16[768,1024]{1,0:T(8,128)(2,1)S(1)} %copy-done, bf16[1,3072,768]{2,1,0:T(8,128)(2,1)} %all-gather.3.cloned.1.call-done), kind=kOutput, calls=%fused_computation.2 | convolution fusion | flops 4838126592 | bytes 18886656 | tf_op jit(solution)/shard_map/dot_general | solution.py:11
  72.4 0.0 copy-start.4
  72.4 9.7 %fusion = (f32[768]{0:T(1024)S(1)}, f32[768]{0:T(1024)S(1)}, f32[768,3072]{1,0:T(8,128)}) fusion(s32[768]{0:T(1024)S(1)} %reduce.2, f32[3072,1024]{0,1:T(8,128)S(1)} %get-tuple-element.12, f32[3072]{0:T(1024)S(1)} %add_sqrt_fusion, f32[768,1024]{1,0:T(8,128)S(1)} %copy-done.3, f32[768]{0:T(1024)S(1)} %add_sqrt_fusion.1), kind=kOutput, calls=%fused_computation.7 | convolution fusion | flops 4853856256 | bytes 25190400 | tf_op jit(solution)/shard_map/dot_general | solution.py:18
  82.2 13.6 %multiply_reduce_fusion.2 = (f32[768]{0:T(1024)S(1)}, f32[768,1024]{1,0:T(8,128)S(1)}) fusion(f32[768,1024]{1,0:T(8,128)S(1)} %copy-done.3, f32[768]{0:T(1024)S(1)} %add_sqrt_fusion.1, f32[3072,1024]{0,1:T(8,128)} %copy-done.4, f32[3072]{0:T(1024)S(1)} %add_sqrt_fusion, f32[768,3072]{1,0:T(8,128)} %get-tuple-element.13, f32[768]{0:T(1024)S(1)} %get-tuple-element.3, ...), kind=kOutput, calls=%fused_computation.14 | convolution fusion | flops 4860148736 | bytes 28339200 | tf_op jit(solution)/shard_map/dot_general | solution.py:60
  95.7 0.0 copy-start.2
  95.7 15.1 %multiply_reduce_fusion = (f32[3072]{0:T(1024)S(1)}, f32[3072,1024]{0,1:T(8,128)}) fusion(f32[3072,1024]{0,1:T(8,128)} %copy-done.4, f32[3072]{0:T(1024)S(1)} %add_sqrt_fusion, f32[768,1024]{1,0:T(8,128)S(1)} %copy-done.3, f32[768]{0:T(1024)S(1)} %add_sqrt_fusion.1, f32[768,3072]{1,0:T(8,128)} %get-tuple-element.13, f32[768]{0:T(1024)S(1)} %get-tuple-element.3, ...), kind=kOutput, calls=%fused_computation.1 | convolution fusion | flops 4864865280 | bytes 37785600 | tf_op jit(solution)/shard_map/dot_general | solution.py:61
  110.8 3.9 convolution_bitcast_fusion
  114.7 2.4 copy.13
  117.1 2.9 reshape.35
  120.0 4.2 copy.14
  124.3 0.0 reduce-scatter.3.cloned.1.call-update
  124.3 0.0 reduce-scatter.5.cloned.1.call-start
  124.3 12.6 %fusion.9 = f32[768,1024]{0,1:T(8,128)S(1)} fusion(bf16[1,3072,768]{2,1,0:T(8,128)(2,1)} %all-gather.3.cloned.1.call-done, f32[3072,1024]{0,1:T(8,128)} %get-tuple-element.17, f32[3072]{0:T(1024)S(1)} %get-tuple-element.16, f32[3072]{0:T(1024)S(1)} %add_sqrt_fusion, f32[3072,1024]{0,1:T(8,128)} %copy-done.4), kind=kOutput, calls=%fused_computation.20 | convolution fusion | flops 4850712576 | bytes 33054720 | tf_op jit(solution)/shard_map/dot_general | solution.py:69
  136.9 2.4 copy.15
  139.3 5.3 reshape.37
  144.6 4.2 copy.16
  148.7 0.0 reduce-scatter.5.cloned.1.call-update
  148.8 0.6 multiply_reduce_fusion.4
  149.4 64.6 %all-reduce = (f32[]{:T(128)}, f32[]{:T(128)}) all-reduce(f32[]{:T(128)} %multiply_reduce_fusion.4, f32[]{:T(128)} %get-tuple-element.5), channel_id=1, replica_groups=mesh['dp'=32,'blk'=4] {'dp','blk'}, use_global_device_ids=true, to_apply=%region_5.6 | all-reduce | flops 2 | bytes 16 | tf_op jit(solution)/shard_map/psum | solution.py:58
  215.4 119.1 %reduce-scatter.3.cloned.1.call-done = f32[24,256]{1,0:T(8,128)} async-done(((f32[3072,256]{1,0:T(8,128)}), f32[24,256]{1,0:T(8,128)}) %reduce-scatter.3.cloned.1.call-update) | async-done | bytes 24592 | tf_op jit(solution)/shard_map/reduce_scatter | solution.py:72
  334.5 2.0 broadcast_divide_fusion.3
  336.5 209.9 %reduce-scatter.5.cloned.1.call-done = f32[24,256]{1,0:T(8,128)} async-done(((f32[3072,256]{1,0:T(8,128)}), f32[24,256]{1,0:T(8,128)}) %reduce-scatter.5.cloned.1.call-update) | async-done | bytes 24592 | tf_op jit(solution)/shard_map/reduce_scatter | solution.py:75
  546.4 2.0 broadcast_divide_fusion.2
  (8 shorter events, 0.0 us)
Async XLA Ops:
  7.2 57.9 %copy-start = (bf16[768,1024]{1,0:T(8,128)(2,1)S(1)}, bf16[768,1024]{1,0:T(8,128)(2,1)}, u32[]{:S(2)}) copy-start(bf16[768,1024]{1,0:T(8,128)(2,1)} %param.11) | copy-start | bytes 4718596
  7.2 57.8 %all-gather.3.cloned.1.call-start = ((), (), s32[]{:S(2)}) async-start(), calls=%async_computation.4 | async-start | bytes 5898240 | tf_op jit(solution)/shard_map/all_gather | solution.py:48
  7.9 326.6 %reduce-scatter.3.cloned.1.call-start = ((), (), s32[]{:S(2)}) async-start(), calls=%async_computation.2 | async-start | bytes 3170304 | tf_op jit(solution)/shard_map/reduce_scatter | solution.py:72
  65.0 7.4 %copy-start.3 = (f32[768,1024]{1,0:T(8,128)S(1)}, f32[768,1024]{1,0:T(8,128)}, u32[]{:S(2)}) copy-start(f32[768,1024]{1,0:T(8,128)} %get-tuple-element.10) | copy-start | bytes 9437188
  72.4 9.8 %copy-start.4 = (f32[3072,1024]{0,1:T(8,128)}, f32[3072,1024]{0,1:T(8,128)S(1)}, u32[]{:S(2)}) copy-start(f32[3072,1024]{0,1:T(8,128)S(1)} %get-tuple-element.12) | copy-start | bytes 37748740
  95.7 15.1 %copy-start.2 = (bf16[1,768,768]{2,1,0:T(8,128)(2,1)S(1)}, bf16[1,768,768]{2,1,0:T(8,128)(2,1)}, u32[]{:S(2)}) copy-start(bf16[1,768,768]{2,1,0:T(8,128)(2,1)} %param.6) | copy-start | bytes 3538948
  124.3 422.1 %reduce-scatter.5.cloned.1.call-start = ((), (), s32[]{:S(2)}) async-start(), calls=%async_computation.3 | async-start | bytes 3170304 | tf_op jit(solution)/shard_map/reduce_scatter | solution.py:75
  139.3 409.2 %copy-start.1 = (bf16[768,1024]{1,0:T(8,128)(2,1)S(1)}, bf16[768,1024]{1,0:T(8,128)(2,1)}, u32[]{:S(2)}) copy-start(bf16[768,1024]{1,0:T(8,128)(2,1)} %param.11) | copy-start | bytes 4718596
Sparse Core Ops, SparseCore 0:
  9.7 55.3 all-gather.2
  124.4 210.0 reduce-scatter.2
  339.3 207.0 reduce-scatter.4

commit v2 on v1

--- a/solution.py
+++ b/solution.py
@@ -1,7 +1,7 @@
 import jax
 import jax.numpy as jnp
 from jax import lax
-from jax.sharding import PartitionSpec as P
+from jax.sharding import Mesh, PartitionSpec as P
 
 EPS = 1e-06
 LOGIT_SCALE = 50.0
@@ -30,20 +30,11 @@
     return ((gradient - unit_vec * projected) / radius).astype(jnp.bfloat16)
 
 
-def spread_blocks(head, dp_size, blk_size):
-    feat, embed = head.shape
-    tiles = head.reshape(dp_size, feat // dp_size, blk_size, embed // blk_size)
-    tiles = tiles.transpose(0, 2, 1, 3)
-    return tiles.reshape(dp_size * blk_size * (feat // dp_size), embed // blk_size)
-
-
 def per_device(prod_feat, prec_feat, matched, row_weight, proj_prod, proj_prec):
     feat_prod = prod_feat[0]
     feat_prec = prec_feat[0]
     targets = matched[0]
     weights = row_weight[0]
-    dp_size = lax.axis_size("dp")
-    blk_size = lax.axis_size("blk")
     unit_prod, unit16_prod, radius_prod = embed_rows(feat_prod, proj_prod)
     feat_prec_all = lax.all_gather(feat_prec, "blk", axis=0, tiled=True)
     unit_prec, unit16_prec, radius_prec = embed_rows(feat_prec_all, proj_prec)
@@ -55,7 +46,9 @@
     losses = LOGIT_SCALE + jnp.log(totals) - positive
     loss_local = jnp.sum(weights * losses)
     weight_local = jnp.sum(weights)
-    loss_sum, weight_total = lax.psum((loss_local, weight_local), ("dp", "blk"))
+    scalars = lax.psum(jnp.stack([loss_local, weight_local]), ("y", "x", "core", "blk"))
+    loss_sum = scalars[0]
+    weight_total = scalars[1]
     coeffs = coefficient(scores, matches, weights, totals)
     grad_unit_prod = LOGIT_SCALE * jnp.dot(coeffs, unit16_prec, preferred_element_type=jnp.float32)
     grad_prec_part = LOGIT_SCALE * lax.dot_general(
@@ -69,21 +62,31 @@
     head_prec = lax.dot_general(
         feat_prec_all, dir_prec, (((0,), (0,)), ((), ())), preferred_element_type=jnp.float32
     )
-    summed_prod = lax.psum_scatter(
-        spread_blocks(head_prod, dp_size, blk_size), ("dp", "blk"), scatter_dimension=0, tiled=True
-    )
-    summed_prec = lax.psum_scatter(
-        spread_blocks(head_prec, dp_size, blk_size), ("dp", "blk"), scatter_dimension=0, tiled=True
-    )
-    return (loss_sum / weight_total, summed_prod / weight_total, summed_prec / weight_total)
+    heads = jnp.stack([head_prod, head_prec])
+    feat, embed = head_prod.shape
+    y_size = lax.axis_size("y")
+    x_size = lax.axis_size("x")
+    core_size = lax.axis_size("core")
+    heads = heads.reshape(2, y_size, x_size, core_size, feat // (y_size * x_size * core_size), embed)
+    heads = lax.psum_scatter(heads, "core", scatter_dimension=3, tiled=False)
+    heads = lax.psum_scatter(heads, "x", scatter_dimension=2, tiled=False)
+    heads = lax.psum_scatter(heads, "y", scatter_dimension=1, tiled=False)
+    heads = lax.psum_scatter(heads, "blk", scatter_dimension=2, tiled=True)
+    heads = heads / weight_total
+    return (loss_sum / weight_total, heads[0], heads[1])
 
 
 def solution(mesh):
-    placed = (P("dp", "blk", None), P("dp", "blk", None), P("dp", "blk"), P("dp", "blk"), P(), P())
+    dp_size = mesh.shape["dp"]
+    blk_size = mesh.shape["blk"]
+    lanes = mesh.devices.reshape(dp_size // 8, 4, 2, blk_size)
+    fine = Mesh(lanes, ("y", "x", "core", "blk"))
+    rows = ("y", "x", "core")
+    placed = (P(rows, "blk", None), P(rows, "blk", None), P(rows, "blk"), P(rows, "blk"), P(), P())
     return jax.shard_map(
         per_device,
-        mesh=mesh,
+        mesh=fine,
         in_specs=placed,
-        out_specs=(P(), P("dp", "blk"), P("dp", "blk")),
+        out_specs=(P(), P(rows, "blk"), P(rows, "blk")),
         check_vma=False,
     )

time: 557 us -> 297 us (0.53)
  waiting for transfers between devices: 380 us -> 135 us
  local copies, waits for them, and re-layouts: 21.4 us -> 4.49 us
    reduce_scatter x2 -> x4, waiting for transfers between devices: 329 us -> 84.3 us  [the longest x1 42.1 us: per_device(): heads = lax.psum_scatter(heads, 'x', scatter_dimension=2, tiled=False)]
    transpose x2 -> x0, local copies, waits for them, and re-layouts: 8.37 us -> none  [spread_blocks(): tiles = tiles.transpose(0, 2, 1, 3)]
    reshape x2 -> x0, local copies, waits for them, and re-layouts: 8.26 us -> none  [spread_blocks(): tiles = head.reshape(dp_size, feat // dp_size, blk_size, embed // blk_size)]
  transfers between devices with their start and end apart: 3 -> 5, of which waited for: 3 -> 4; matrix products, arithmetic and copies ran while one was open for 6% -> 3% of each run, Pallas kernels for 0% -> 0%
where the time goes in v2:
time: 297 us; the launch traced here: 296 us
  waiting for transfers between devices  135 us (45%)
  matrix products  69 us (23%)
  blocking collectives  65 us (22%)
  between operations  16.3 us (5%)
  other arithmetic  6.02 us (2%)
  local copies, waits for them, and re-layouts  4.49 us (2%)
    psum x1, blocking collectives, per_device(): lax.psum(jnp.stack([loss_local, weight_local]), ('y', 'x', 'core', 'blk'))  65 us
    all_gather x1, waiting for transfers between devices, per_device(): feat_prec_all = lax.all_gather(feat_prec, 'blk', axis=0, tiled=True)  50.2 us
    reduce_scatter x1, waiting for transfers between devices, per_device(): heads = lax.psum_scatter(heads, 'x', scatter_dimension=2, tiled=False)  42.1 us
    reduce_scatter x1, waiting for transfers between devices, per_device(): heads = lax.psum_scatter(heads, 'y', scatter_dimension=1, tiled=False)  24.6 us
    reduce_scatter x1, waiting for transfers between devices, per_device(): heads = lax.psum_scatter(heads, 'core', scatter_dimension=3, tiled=False)  17.5 us
    dot_general x1, matrix products, per_device(): jnp.dot(coeffs, unit16_prec, preferred_element_type=jnp.float32)  15.3 us
    dot_general x1, matrix products, per_device(): lax.dot_general(coeffs, unit16_prod, (((0,), (0,)), ((), ())), preferred_...  14.8 us
    dot_general x1, matrix products, per_device(): lax.dot_general(feat_prec_all, dir_prec, (((0,), (0,)), ((), ())), prefer...  12.5 us
  transfers between devices with their start and end apart: 5, of which 4 were waited for; matrix products, arithmetic and copies ran while one was open for 3% of the time, Pallas kernels for 0%

profile of v2, /device:TPU:0, one launch (start us, length us, event | category | flops | bytes accessed | tf_op | source)
XLA Modules:
  0.0 296.3 jit_solution(9143300749455362254)
XLA Ops:
  7.2 0.0 all-gather.3.cloned.1.call-start
  7.2 0.7 all-gather.3.cloned.1.call-update
  7.9 0.0 reduce-scatter.5.cloned.1.call-start
  8.0 0.7 reduce.2
  8.7 1.3 fusion.18
  10.0 4.8 %multiply_reduce_fusion.3 = (f32[768]{0:T(1024)S(1)}, f32[768,1024]{1,0:T(8,128)}) fusion(bf16[768,1024]{1,0:T(8,128)(2,1)} %param.10, bf16[1,768,768]{2,1,0:T(8,128)(2,1)} %param.6), kind=kOutput, calls=%fused_computation.20 | convolution fusion | flops 1209531648 | bytes 5901312 | tf_op jit(solution)/shard_map/dot_general | solution.py:11
  14.8 50.2 %all-gather.3.cloned.1.call-done = bf16[1,3072,768]{2,1,0:T(8,128)(2,1)} async-done(((bf16[1,768,768]{2,1,0:T(8,128)(2,1)}), bf16[1,3072,768]{2,1,0:T(8,128)(2,1)}) %all-gather.3.cloned.1.call-update) | async-done | bytes 4718608 | tf_op jit(solution)/shard_map/all_gather | solution.py:39
  65.0 7.5 %multiply_reduce_fusion.1 = (f32[3072]{0:T(1024)S(1)}, f32[3072,1024]{0,1:T(8,128)S(1)}) fusion(bf16[768,1024]{1,0:T(8,128)(2,1)S(1)} %copy-done, bf16[1,3072,768]{2,1,0:T(8,128)(2,1)} %all-gather.3.cloned.1.call-done), kind=kOutput, calls=%fused_computation.2 | convolution fusion | flops 4838126592 | bytes 18886656 | tf_op jit(solution)/shard_map/dot_general | solution.py:11
  72.6 10.4 %fusion = (f32[768]{0:T(1024)S(1)}, f32[768]{0:T(1024)}, f32[768,3072]{1,0:T(8,128)}) fusion(s32[768]{0:T(1024)S(1)} %reduce.2, f32[3072,1024]{0,1:T(8,128)S(1)} %get-tuple-element.14, f32[3072]{0:T(1024)S(1)} %add_sqrt_fusion, f32[768,1024]{1,0:T(8,128)S(1)} %copy-done.4, f32[768]{0:T(1024)S(1)} %add_sqrt_fusion.1), kind=kOutput, calls=%fused_computation.7 | convolution fusion | flops 4853856256 | bytes 25190400 | tf_op jit(solution)/shard_map/dot_general | solution.py:18
  83.0 14.8 %multiply_reduce_fusion = (f32[3072]{0:T(1024)S(1)}, f32[3072,1024]{0,1:T(8,128)}) fusion(f32[3072,1024]{0,1:T(8,128)} %copy-done.5, f32[3072]{0:T(1024)S(1)} %add_sqrt_fusion, f32[768,1024]{1,0:T(8,128)S(1)} %copy-done.4, f32[768]{0:T(1024)S(1)} %add_sqrt_fusion.1, f32[768,3072]{1,0:T(8,128)} %get-tuple-element.15, f32[768]{0:T(1024)S(1)} %get-tuple-element.3, ...), kind=kOutput, calls=%fused_computation.1 | convolution fusion | flops 4864865280 | bytes 37785600 | tf_op jit(solution)/shard_map/dot_general | solution.py:54
  97.8 15.3 %multiply_reduce_fusion.2 = (f32[768]{0:T(1024)S(1)}, f32[768,1024]{1,0:T(8,128)}) fusion(f32[768,1024]{1,0:T(8,128)S(1)} %copy-done.4, f32[768]{0:T(1024)S(1)} %add_sqrt_fusion.1, f32[3072,1024]{0,1:T(8,128)} %copy-done.5, f32[3072]{0:T(1024)S(1)} %add_sqrt_fusion, f32[768,3072]{1,0:T(8,128)} %get-tuple-element.15, f32[768]{0:T(1024)S(1)} %get-tuple-element.3, ...), kind=kOutput, calls=%fused_computation.15 | convolution fusion | flops 4860148736 | bytes 28339200 | tf_op jit(solution)/shard_map/dot_general | solution.py:53
  113.1 3.7 %fusion.9 = f32[1024,768]{0,1:T(8,128)S(1)} fusion(f32[768,1024]{1,0:T(8,128)} %get-tuple-element.19, f32[768]{0:T(1024)S(1)} %get-tuple-element.18, f32[768]{0:T(1024)S(1)} %add_sqrt_fusion.1, bf16[1,768,768]{2,1,0:T(8,128)(2,1)S(1)} %copy-done.3, f32[768,1024]{1,0:T(8,128)S(1)} %copy-done.4), kind=kOutput, calls=%fused_computation.22 | convolution fusion | flops 1212678144 | bytes 10622976 | tf_op jit(solution)/shard_map/dot_general | solution.py:59
  116.8 12.5 %fusion.1 = f32[1024,768]{0,1:T(8,128)S(1)} fusion(f32[3072,1024]{0,1:T(8,128)} %get-tuple-element.17, f32[3072]{0:T(1024)S(1)} %get-tuple-element.16, f32[3072]{0:T(1024)S(1)} %add_sqrt_fusion, bf16[1,3072,768]{2,1,0:T(8,128)(2,1)} %all-gather.3.cloned.1.call-done, f32[3072,1024]{0,1:T(8,128)} %copy-done.5), kind=kOutput, calls=%fused_computation.10 | convolution fusion | flops 4850712576 | bytes 33054720 | tf_op jit(solution)/shard_map/dot_general | solution.py:62
  129.3 0.6 pad_maximum_fusion
  129.9 3.2 %copy.11 = f32[2,4,4,2,24,1024]{5,4,0,1,2,3:T(8,128)} copy(f32[2,4,4,2,24,1024]{5,4,3,2,1,0:T(8,128)S(1)} %pad_maximum_fusion) | data formatting | bytes 12582912 | tf_op jit(solution)/shard_map/stack | solution.py:65
  133.1 0.0 reduce-scatter.5.cloned.1.call-update
  133.1 0.0 reduce-scatter.7.cloned.1.call-start
  133.2 17.5 %reduce-scatter.5.cloned.1.call-done = f32[2,4,4,1,24,1024]{5,4,0,1,2,3:T(8,128)} async-done(((f32[2,4,4,2,24,1024]{5,4,0,1,2,3:T(8,128)}), f32[2,4,4,1,24,1024]{5,4,0,1,2,3:T(8,128)}) %reduce-scatter.5.cloned.1.call-update) | async-done | bytes 3145744 | tf_op jit(solution)/shard_map/reduce_scatter | solution.py:71
  150.7 0.0 reduce-scatter.7.cloned.1.call-update
  150.7 0.0 reduce-scatter.9.cloned.1.call-start
  150.8 42.1 %reduce-scatter.7.cloned.1.call-done = f32[2,4,1,24,1024]{4,3,0,1,2:T(8,128)} async-done(((f32[2,4,4,24,1024]{4,3,0,1,2:T(8,128)}), f32[2,4,1,24,1024]{4,3,0,1,2:T(8,128)}) %reduce-scatter.7.cloned.1.call-update) | async-done | bytes 786448 | tf_op jit(solution)/shard_map/reduce_scatter | solution.py:72
  192.9 0.0 reduce-scatter.9.cloned.1.call-update
  192.9 0.0 reduce-scatter.11.cloned.1.call-start
  192.9 24.6 %reduce-scatter.9.cloned.1.call-done = f32[2,1,24,1024]{3,2,0,1:T(8,128)} async-done(((f32[2,4,24,1024]{3,2,0,1:T(8,128)}), f32[2,1,24,1024]{3,2,0,1:T(8,128)}) %reduce-scatter.9.cloned.1.call-update) | async-done | bytes 196624 | tf_op jit(solution)/shard_map/reduce_scatter | solution.py:73
  217.6 0.0 reduce-scatter.11.cloned.1.call-update
  217.6 0.6 multiply_reduce_fusion.4
  218.2 1.4 pad_maximum_fusion.1
  219.6 65.0 %psum.7 = f32[2]{0:T(128)S(1)} all-reduce(f32[2]{0:T(128)S(1)} %pad_maximum_fusion.1), channel_id=1, replica_groups=mesh['y'=4,'x'=4,'core'=2,'blk'=4] {'y','x','core','blk'}, use_global_device_ids=true, to_apply=%region_6.7 | all-reduce | flops 2 | bytes 16 | tf_op jit(solution)/shard_map/psum | solution.py:49
  284.6 0.6 fusion.19
  286.5 0.0 reduce-scatter.11.cloned.1.call-done
  286.5 1.5 broadcast_divide_fusion.2
  288.0 0.6 slice_bitcast_fusion
  (14 shorter events, 0.0 us)
Async XLA Ops:
  7.2 57.9 %copy-start = (bf16[768,1024]{1,0:T(8,128)(2,1)S(1)}, bf16[768,1024]{1,0:T(8,128)(2,1)}, u32[]{:S(2)}) copy-start(bf16[768,1024]{1,0:T(8,128)(2,1)} %param.11) | copy-start | bytes 4718596
  7.2 57.8 %all-gather.3.cloned.1.call-start = ((), (), s32[]{:S(2)}) async-start(), calls=%async_computation.8 | async-start | bytes 5898240 | tf_op jit(solution)/shard_map/all_gather | solution.py:39
  7.9 142.8 %reduce-scatter.5.cloned.1.call-start = ((), (), s32[]{:S(2)}) async-start(), calls=%async_computation.4 | async-start | bytes 9437184 | tf_op jit(solution)/shard_map/reduce_scatter | solution.py:71
  65.0 7.5 %copy-start.4 = (f32[768,1024]{1,0:T(8,128)S(1)}, f32[768,1024]{1,0:T(8,128)}, u32[]{:S(2)}) copy-start(f32[768,1024]{1,0:T(8,128)} %get-tuple-element.12) | copy-start | bytes 9437188
  72.5 10.5 %copy-start.5 = (f32[3072,1024]{0,1:T(8,128)}, f32[3072,1024]{0,1:T(8,128)S(1)}, u32[]{:S(2)}) copy-start(f32[3072,1024]{0,1:T(8,128)S(1)} %get-tuple-element.14) | copy-start | bytes 37748740
  97.8 15.3 %copy-start.3 = (bf16[1,768,768]{2,1,0:T(8,128)(2,1)S(1)}, bf16[1,768,768]{2,1,0:T(8,128)(2,1)}, u32[]{:S(2)}) copy-start(bf16[1,768,768]{2,1,0:T(8,128)(2,1)} %param.6) | copy-start | bytes 3538948
  129.9 158.7 %copy-start.1 = (bf16[768,1024]{1,0:T(8,128)(2,1)S(1)}, bf16[768,1024]{1,0:T(8,128)(2,1)}, u32[]{:S(2)}) copy-start(bf16[768,1024]{1,0:T(8,128)(2,1)} %param.11) | copy-start | bytes 4718596
  133.1 84.5 %copy-start.2 = (f32[768]{0:T(1024)S(1)}, f32[768]{0:T(1024)}, u32[]{:S(2)}) copy-start(f32[768]{0:T(1024)} %get-tuple-element.4) | copy-start | bytes 9220
  133.1 59.7 %reduce-scatter.7.cloned.1.call-start = ((), (), s32[]{:S(2)}) async-start(), calls=%async_computation.5 | async-start | bytes 3932160 | tf_op jit(solution)/shard_map/reduce_scatter | solution.py:72
  150.7 66.9 %reduce-scatter.9.cloned.1.call-start = ((), (), s32[]{:S(2)}) async-start(), calls=%async_computation.6 | async-start | bytes 983040 | tf_op jit(solution)/shard_map/reduce_scatter | solution.py:73
  192.9 93.6 %reduce-scatter.11.cloned.1.call-start = ((), (), s32[]{:S(2)}) async-start(), calls=%async_computation.7 | async-start | bytes 245760 | tf_op jit(solution)/shard_map/reduce_scatter | solution.py:74
Sparse Core Ops, SparseCore 0:
  9.7 55.3 all-gather.2
  133.3 17.3 reduce-scatter.4
  153.2 39.5 reduce-scatter.6
  195.3 22.2 reduce-scatter.8
  219.9 20.4 reduce-scatter.10

commit v3 on v2

--- a/solution.py
+++ b/solution.py
@@ -30,6 +30,17 @@
     return ((gradient - unit_vec * projected) / radius).astype(jnp.bfloat16)
 
 
+def gather_along(values, axis):
+    size = lax.axis_size(axis)
+    pieces = [values]
+    for shift in range(1, size):
+        route = [(i, (i + shift) % size) for i in range(size)]
+        pieces.append(lax.ppermute(values, axis, route))
+    stacked = jnp.stack(pieces)
+    order = (lax.axis_index(axis) - jnp.arange(size)) % size
+    return stacked[order]
+
+
 def per_device(prod_feat, prec_feat, matched, row_weight, proj_prod, proj_prec):
     feat_prod = prod_feat[0]
     feat_prec = prec_feat[0]
@@ -46,9 +57,12 @@
     losses = LOGIT_SCALE + jnp.log(totals) - positive
     loss_local = jnp.sum(weights * losses)
     weight_local = jnp.sum(weights)
-    scalars = lax.psum(jnp.stack([loss_local, weight_local]), ("y", "x", "core", "blk"))
-    loss_sum = scalars[0]
-    weight_total = scalars[1]
+    scalars = jnp.stack([loss_local, weight_local])
+    for axis in ("core", "x", "y", "blk"):
+        scalars = gather_along(scalars, axis)
+    scalars = scalars.reshape(-1, 2)
+    loss_sum = jnp.sum(scalars[:, 0])
+    weight_total = jnp.sum(scalars[:, 1])
     coeffs = coefficient(scores, matches, weights, totals)
     grad_unit_prod = LOGIT_SCALE * jnp.dot(coeffs, unit16_prec, preferred_element_type=jnp.float32)
     grad_prec_part = LOGIT_SCALE * lax.dot_general(

time: 297 us -> 250 us (0.84)
  blocking collectives: 65 us -> 0 us
  starting transfers between devices: 0.19 us -> 12.4 us
    psum x1 -> x0, blocking collectives: 65 us -> none  [per_device(): lax.psum(jnp.stack([loss_local, weight_local]), ('y', 'x', 'core', 'blk'))]
    reduce_scatter x1, waiting for transfers between devices: 24.6 us -> 4.21 us  [per_device(): heads = lax.psum_scatter(heads, 'y', scatter_dimension=1, tiled=False)]
    ppermute x0 -> x10, starting transfers between devices: none -> 12.2 us  [gather_along(): pieces.append(lax.ppermute(values, axis, route))]
    ppermute x0 -> x10, waiting for transfers between devices: none -> 11.7 us  [gather_along(): pieces.append(lax.ppermute(values, axis, route))]
    reduce_scatter x1, waiting for transfers between devices: 0.02 us -> 10.7 us  [per_device(): heads = lax.psum_scatter(heads, 'blk', scatter_dimension=2, tiled=True)]
  transfers between devices with their start and end apart: 5 -> 15, of which waited for: 4 -> 12; matrix products, arithmetic and copies ran while one was open for 3% -> 6% of each run, Pallas kernels for 0% -> 0%
where the time goes in v3:
time: 250 us
  waiting for transfers between devices  137 us (55%)
  matrix products  68.5 us (27%)
  between operations  16.4 us (7%)
  starting transfers between devices  12.4 us (5%)
  other arithmetic  8.11 us (3%)
  local copies, waits for them, and re-layouts  7.04 us (3%)
    all_gather x1, waiting for transfers between devices, per_device(): feat_prec_all = lax.all_gather(feat_prec, 'blk', axis=0, tiled=True)  50.2 us
    reduce_scatter x1, waiting for transfers between devices, per_device(): heads = lax.psum_scatter(heads, 'x', scatter_dimension=2, tiled=False)  42.1 us
    reduce_scatter x1, waiting for transfers between devices, per_device(): heads = lax.psum_scatter(heads, 'core', scatter_dimension=3, tiled=False)  17.5 us
    dot_general x1, matrix products, per_device(): jnp.dot(coeffs, unit16_prec, preferred_element_type=jnp.float32)  15.3 us
    dot_general x1, matrix products, per_device(): lax.dot_general(coeffs, unit16_prod, (((0,), (0,)), ((), ())), preferred_...  14.8 us
    dot_general x1, matrix products, per_device(): lax.dot_general(feat_prec_all, dir_prec, (((0,), (0,)), ((), ())), prefer...  12.5 us
    ppermute x10, starting transfers between devices, gather_along(): pieces.append(lax.ppermute(values, axis, route))  12.2 us
    dot_general x2, matrix products, embed_rows(): jnp.dot(features, weight, preferred_element_type=jnp.float32)  12 us
  transfers between devices with their start and end apart: 15, of which 12 were waited for; matrix products, arithmetic and copies ran while one was open for 6% of the time, Pallas kernels for 0%

profile of v3, /device:TPU:0, one launch (start us, length us, event | category | flops | bytes accessed | tf_op | source)
XLA Modules:
  0.0 249.7 jit_solution(3326319025036800721)
XLA Ops:
  7.2 0.7 all-gather.3.cloned.1.call-update
  8.0 0.7 reduce.4
  8.7 1.3 fusion.26
  10.0 4.8 %multiply_reduce_fusion.3 = (f32[768]{0:T(1024)S(1)}, f32[768,1024]{1,0:T(8,128)}) fusion(bf16[768,1024]{1,0:T(8,128)(2,1)} %param.10, bf16[1,768,768]{2,1,0:T(8,128)(2,1)} %param.6), kind=kOutput, calls=%fused_computation.24 | convolution fusion | flops 1209531648 | bytes 5901312 | tf_op jit(solution)/shard_map/dot_general | solution.py:11
  14.8 50.2 %all-gather.3.cloned.1.call-done = bf16[1,3072,768]{2,1,0:T(8,128)(2,1)} async-done(((bf16[1,768,768]{2,1,0:T(8,128)(2,1)}), bf16[1,3072,768]{2,1,0:T(8,128)(2,1)}) %all-gather.3.cloned.1.call-update) | async-done | bytes 4718608 | tf_op jit(solution)/shard_map/all_gather | solution.py:50
  65.0 7.2 %multiply_reduce_fusion.1 = (f32[3072]{0:T(1024)S(1)}, f32[3072,1024]{0,1:T(8,128)S(1)}) fusion(bf16[768,1024]{1,0:T(8,128)(2,1)S(1)} %copy-done, bf16[1,3072,768]{2,1,0:T(8,128)(2,1)} %all-gather.3.cloned.1.call-done), kind=kOutput, calls=%fused_computation.6 | convolution fusion | flops 4838126592 | bytes 18886656 | tf_op jit(solution)/shard_map/dot_general | solution.py:11
  72.3 10.3 %fusion = (f32[768]{0:T(1024)S(1)}, f32[768]{0:T(1024)}, f32[768,3072]{1,0:T(8,128)}) fusion(s32[768]{0:T(1024)S(1)} %reduce.4, f32[3072,1024]{0,1:T(8,128)S(1)} %get-tuple-element.14, f32[3072]{0:T(1024)S(1)} %add_sqrt_fusion, f32[768,1024]{1,0:T(8,128)S(1)} %copy-done.4, f32[768]{0:T(1024)S(1)} %add_sqrt_fusion.1), kind=kOutput, calls=%fused_computation.11 | convolution fusion | flops 4853856256 | bytes 25190400 | tf_op jit(solution)/shard_map/dot_general | solution.py:18
  82.6 14.8 %multiply_reduce_fusion = (f32[3072]{0:T(1024)S(1)}, f32[3072,1024]{0,1:T(8,128)}) fusion(f32[3072,1024]{0,1:T(8,128)} %copy-done.5, f32[3072]{0:T(1024)S(1)} %add_sqrt_fusion, f32[768,1024]{1,0:T(8,128)S(1)} %copy-done.4, f32[768]{0:T(1024)S(1)} %add_sqrt_fusion.1, f32[768,3072]{1,0:T(8,128)} %get-tuple-element.15, f32[768]{0:T(1024)S(1)} %get-tuple-element.3, ...), kind=kOutput, calls=%fused_computation.5 | convolution fusion | flops 4864865280 | bytes 37785600 | tf_op jit(solution)/shard_map/dot_general | solution.py:68
  97.3 15.3 %multiply_reduce_fusion.2 = (f32[768]{0:T(1024)S(1)}, f32[768,1024]{1,0:T(8,128)}) fusion(f32[768,1024]{1,0:T(8,128)S(1)} %copy-done.4, f32[768]{0:T(1024)S(1)} %add_sqrt_fusion.1, f32[3072,1024]{0,1:T(8,128)} %copy-done.5, f32[3072]{0:T(1024)S(1)} %add_sqrt_fusion, f32[768,3072]{1,0:T(8,128)} %get-tuple-element.15, f32[768]{0:T(1024)S(1)} %get-tuple-element.3, ...), kind=kOutput, calls=%fused_computation.19 | convolution fusion | flops 4860148736 | bytes 28339200 | tf_op jit(solution)/shard_map/dot_general | solution.py:67
  112.6 3.7 %fusion.9 = f32[1024,768]{0,1:T(8,128)S(1)} fusion(f32[768,1024]{1,0:T(8,128)} %get-tuple-element.19, f32[768]{0:T(1024)S(1)} %get-tuple-element.18, f32[768]{0:T(1024)S(1)} %add_sqrt_fusion.1, bf16[1,768,768]{2,1,0:T(8,128)(2,1)S(1)} %copy-done.3, f32[768,1024]{1,0:T(8,128)S(1)} %copy-done.4), kind=kOutput, calls=%fused_computation.26 | convolution fusion | flops 1212678144 | bytes 10622976 | tf_op jit(solution)/shard_map/dot_general | solution.py:73
  116.3 12.5 %fusion.1 = f32[1024,768]{0,1:T(8,128)S(1)} fusion(f32[3072,1024]{0,1:T(8,128)} %get-tuple-element.17, f32[3072]{0:T(1024)S(1)} %get-tuple-element.16, f32[3072]{0:T(1024)S(1)} %add_sqrt_fusion, bf16[1,3072,768]{2,1,0:T(8,128)(2,1)} %all-gather.3.cloned.1.call-done, f32[3072,1024]{0,1:T(8,128)} %copy-done.5), kind=kOutput, calls=%fused_computation.14 | convolution fusion | flops 4850712576 | bytes 33054720 | tf_op jit(solution)/shard_map/dot_general | solution.py:76
  129.4 3.2 %copy.30 = f32[2,4,4,2,24,1024]{5,4,0,1,2,3:T(8,128)} copy(f32[2,4,4,2,24,1024]{5,4,3,2,1,0:T(8,128)S(1)} %pad_maximum_fusion) | data formatting | bytes 12582912 | tf_op jit(solution)/shard_map/stack | solution.py:79
  132.7 17.5 %reduce-scatter.5.cloned.1.call-done = f32[2,4,4,1,24,1024]{5,4,0,1,2,3:T(8,128)} async-done(((f32[2,4,4,2,24,1024]{5,4,0,1,2,3:T(8,128)}), f32[2,4,4,1,24,1024]{5,4,0,1,2,3:T(8,128)}) %reduce-scatter.5.cloned.1.call-update) | async-done | bytes 3145744 | tf_op jit(solution)/shard_map/reduce_scatter | solution.py:85
  150.3 42.1 %reduce-scatter.7.cloned.1.call-done = f32[2,4,1,24,1024]{4,3,0,1,2:T(8,128)} async-done(((f32[2,4,4,24,1024]{4,3,0,1,2:T(8,128)}), f32[2,4,1,24,1024]{4,3,0,1,2:T(8,128)}) %reduce-scatter.7.cloned.1.call-update) | async-done | bytes 786448 | tf_op jit(solution)/shard_map/reduce_scatter | solution.py:86
  193.2 1.4 pad_maximum_fusion.5
  194.6 1.4 fusion.29
  196.6 0.9 collective-permute-start.3
  197.5 1.5 collective-permute-start.2
  199.5 0.7 collective-permute-done.3
  200.2 2.4 collective-permute-done.2
  202.6 1.2 collective-permute-done.1
  204.3 2.8 %collective-permute-start.6 = (f32[4,2,2]{2,1,0:T(2,128)S(1)}, f32[4,2,2]{2,1,0:T(2,128)S(1)}, u32[]{:S(2)}, u32[]{:S(2)}) collective-permute-start(f32[4,2,2]{2,1,0:T(2,128)S(1)} %gather_fusion.1), channel_id=1, source_target_pairs={{0,96},{32,0},{64,32},{96,64},{1,97},{33,1},{65,33},{97,65},{2,98}... | collective-permute-start | bytes 200 | tf_op jit(solution)/shard_map/ppermute | solution.py:38
  207.1 0.8 collective-permute-start.5
  207.9 0.9 collective-permute-start.4
  209.0 3.2 %collective-permute-done.5 = f32[4,2,2]{2,1,0:T(2,128)S(1)} collective-permute-done((f32[4,2,2]{2,1,0:T(2,128)S(1)}, f32[4,2,2]{2,1,0:T(2,128)S(1)}, u32[]{:S(2)}, u32[]{:S(2)}) %collective-permute-start.5) | collective-permute-done | bytes 96 | tf_op jit(solution)/shard_map/ppermute | solution.py:38
  212.8 4.2 %reduce-scatter.9.cloned.1.call-done = f32[2,1,24,1024]{3,2,0,1:T(8,128)} async-done(((f32[2,4,24,1024]{3,2,0,1:T(8,128)}), f32[2,1,24,1024]{3,2,0,1:T(8,128)}) %reduce-scatter.9.cloned.1.call-update) | async-done | bytes 196624 | tf_op jit(solution)/shard_map/reduce_scatter | solution.py:87
  217.7 3.0 %collective-permute-start.9 = (f32[4,4,2,2]{1,3,2,0:T(2,128)S(1)}, f32[4,4,2,2]{1,3,2,0:T(2,128)S(1)}, u32[]{:S(2)}, u32[]{:S(2)}) collective-permute-start(f32[4,4,2,2]{1,3,2,0:T(2,128)S(1)} %gather_fusion.2), channel_id=1, source_target_pairs={{0,3},{1,0},{2,1},{3,2},{4,7},{5,4},{6,5},{7,6},{8,11},{9,8},{10,9... | collective-permute-start | bytes 776 | tf_op jit(solution)/shard_map/ppermute | solution.py:38
  220.7 0.7 collective-permute-start.8
  221.4 1.0 collective-permute-start.7
  222.4 3.4 %collective-permute-done.8 = f32[4,4,2,2]{1,3,2,0:T(2,128)S(1)} collective-permute-done((f32[4,4,2,2]{1,3,2,0:T(2,128)S(1)}, f32[4,4,2,2]{1,3,2,0:T(2,128)S(1)}, u32[]{:S(2)}, u32[]{:S(2)}) %collective-permute-start.8) | collective-permute-done | bytes 288 | tf_op jit(solution)/shard_map/ppermute | solution.py:38
  229.3 10.7 %reduce-scatter.11.cloned.1.call-done = f32[2,24,256]{2,1,0:T(8,128)} async-done(((f32[2,24,1024]{2,1,0:T(8,128)}), f32[2,24,256]{2,1,0:T(8,128)}) %reduce-scatter.11.cloned.1.call-update) | async-done | bytes 49168 | tf_op jit(solution)/shard_map/reduce_scatter | solution.py:88
  240.0 1.5 broadcast_divide_fusion.2
  (60 shorter events, 7.5 us)
Async XLA Ops:
  7.2 57.9 %copy-start = (bf16[768,1024]{1,0:T(8,128)(2,1)S(1)}, bf16[768,1024]{1,0:T(8,128)(2,1)}, u32[]{:S(2)}) copy-start(bf16[768,1024]{1,0:T(8,128)(2,1)} %param.11) | copy-start | bytes 4718596
  7.2 57.8 %all-gather.3.cloned.1.call-start = ((), (), s32[]{:S(2)}) async-start(), calls=%async_computation.8 | async-start | bytes 5898240 | tf_op jit(solution)/shard_map/all_gather | solution.py:50
  7.9 142.3 %reduce-scatter.5.cloned.1.call-start = ((), (), s32[]{:S(2)}) async-start(), calls=%async_computation.4 | async-start | bytes 9437184 | tf_op jit(solution)/shard_map/reduce_scatter | solution.py:85
  65.0 7.2 %copy-start.4 = (f32[768,1024]{1,0:T(8,128)S(1)}, f32[768,1024]{1,0:T(8,128)}, u32[]{:S(2)}) copy-start(f32[768,1024]{1,0:T(8,128)} %get-tuple-element.12) | copy-start | bytes 9437188
  72.2 10.3 %copy-start.5 = (f32[3072,1024]{0,1:T(8,128)}, f32[3072,1024]{0,1:T(8,128)S(1)}, u32[]{:S(2)}) copy-start(f32[3072,1024]{0,1:T(8,128)S(1)} %get-tuple-element.14) | copy-start | bytes 37748740
  97.3 15.3 %copy-start.3 = (bf16[1,768,768]{2,1,0:T(8,128)(2,1)S(1)}, bf16[1,768,768]{2,1,0:T(8,128)(2,1)}, u32[]{:S(2)}) copy-start(bf16[1,768,768]{2,1,0:T(8,128)(2,1)} %param.6) | copy-start | bytes 3538948
  129.4 112.7 %copy-start.1 = (bf16[768,1024]{1,0:T(8,128)(2,1)S(1)}, bf16[768,1024]{1,0:T(8,128)(2,1)}, u32[]{:S(2)}) copy-start(bf16[768,1024]{1,0:T(8,128)(2,1)} %param.11) | copy-start | bytes 4718596
  132.7 60.0 %copy-start.2 = (f32[768]{0:T(1024)S(1)}, f32[768]{0:T(1024)}, u32[]{:S(2)}) copy-start(f32[768]{0:T(1024)} %get-tuple-element.4) | copy-start | bytes 9220
  132.7 59.7 %reduce-scatter.7.cloned.1.call-start = ((), (), s32[]{:S(2)}) async-start(), calls=%async_computation.5 | async-start | bytes 3932160 | tf_op jit(solution)/shard_map/reduce_scatter | solution.py:86
  150.3 66.8 %reduce-scatter.9.cloned.1.call-start = ((), (), s32[]{:S(2)}) async-start(), calls=%async_computation.6 | async-start | bytes 983040 | tf_op jit(solution)/shard_map/reduce_scatter | solution.py:87
  192.4 47.5 %reduce-scatter.11.cloned.1.call-start = ((), (), s32[]{:S(2)}) async-start(), calls=%async_computation.7 | async-start | bytes 245760 | tf_op jit(solution)/shard_map/reduce_scatter | solution.py:88
  194.6 1.4 collective-permute-start
  196.6 3.6 %collective-permute-start.3 = (f32[2,2]{1,0:T(2,128)S(1)}, f32[2,2]{1,0:T(2,128)S(1)}, u32[]{:S(2)}, u32[]{:S(2)}) collective-permute-start(f32[2,2]{1,0:T(2,128)S(1)} %gather_fusion), channel_id=1, source_target_pairs={{0,24},{8,0},{16,8},{24,16},{1,25},{9,1},{17,9},{25,17},{2,26},{10... | collective-permute-start | bytes 56 | tf_op jit(solution)/shard_map/ppermute | solution.py:38
  197.5 5.1 %collective-permute-start.2 = (f32[2,2]{1,0:T(2,128)S(1)}, f32[2,2]{1,0:T(2,128)S(1)}, u32[]{:S(2)}, u32[]{:S(2)}) collective-permute-start(f32[2,2]{1,0:T(2,128)S(1)} %gather_fusion), channel_id=1, source_target_pairs={{0,16},{8,24},{16,0},{24,8},{1,17},{9,25},{17,1},{25,9},{2,18},{10... | collective-permute-start | bytes 56 | tf_op jit(solution)/shard_map/ppermute | solution.py:38
  199.0 4.8 %collective-permute-start.1 = (f32[2,2]{1,0:T(2,128)S(1)}, f32[2,2]{1,0:T(2,128)S(1)}, u32[]{:S(2)}, u32[]{:S(2)}) collective-permute-start(f32[2,2]{1,0:T(2,128)S(1)} %gather_fusion), channel_id=1, source_target_pairs={{0,8},{8,16},{16,24},{24,0},{1,9},{9,17},{17,25},{25,1},{2,10},{10... | collective-permute-start | bytes 56 | tf_op jit(solution)/shard_map/ppermute | solution.py:38
  204.3 4.6 %collective-permute-start.6 = (f32[4,2,2]{2,1,0:T(2,128)S(1)}, f32[4,2,2]{2,1,0:T(2,128)S(1)}, u32[]{:S(2)}, u32[]{:S(2)}) collective-permute-start(f32[4,2,2]{2,1,0:T(2,128)S(1)} %gather_fusion.1), channel_id=1, source_target_pairs={{0,96},{32,0},{64,32},{96,64},{1,97},{33,1},{65,33},{97,65},{2,98}... | collective-permute-start | bytes 200 | tf_op jit(solution)/shard_map/ppermute | solution.py:38
  207.1 5.1 %collective-permute-start.5 = (f32[4,2,2]{2,1,0:T(2,128)S(1)}, f32[4,2,2]{2,1,0:T(2,128)S(1)}, u32[]{:S(2)}, u32[]{:S(2)}) collective-permute-start(f32[4,2,2]{2,1,0:T(2,128)S(1)} %gather_fusion.1), channel_id=1, source_target_pairs={{0,64},{32,96},{64,0},{96,32},{1,65},{33,97},{65,1},{97,33},{2,66}... | collective-permute-start | bytes 200 | tf_op jit(solution)/shard_map/ppermute | solution.py:38
  207.9 4.8 %collective-permute-start.4 = (f32[4,2,2]{2,1,0:T(2,128)S(1)}, f32[4,2,2]{2,1,0:T(2,128)S(1)}, u32[]{:S(2)}, u32[]{:S(2)}) collective-permute-start(f32[4,2,2]{2,1,0:T(2,128)S(1)} %gather_fusion.1), channel_id=1, source_target_pairs={{0,32},{32,64},{64,96},{96,0},{1,33},{33,65},{65,97},{97,1},{2,34}... | collective-permute-start | bytes 200 | tf_op jit(solution)/shard_map/ppermute | solution.py:38
  217.7 4.7 %collective-permute-start.9 = (f32[4,4,2,2]{1,3,2,0:T(2,128)S(1)}, f32[4,4,2,2]{1,3,2,0:T(2,128)S(1)}, u32[]{:S(2)}, u32[]{:S(2)}) collective-permute-start(f32[4,4,2,2]{1,3,2,0:T(2,128)S(1)} %gather_fusion.2), channel_id=1, source_target_pairs={{0,3},{1,0},{2,1},{3,2},{4,7},{5,4},{6,5},{7,6},{8,11},{9,8},{10,9... | collective-permute-start | bytes 776 | tf_op jit(solution)/shard_map/ppermute | solution.py:38
  220.7 5.2 %collective-permute-start.8 = (f32[4,4,2,2]{1,3,2,0:T(2,128)S(1)}, f32[4,4,2,2]{1,3,2,0:T(2,128)S(1)}, u32[]{:S(2)}, u32[]{:S(2)}) collective-permute-start(f32[4,4,2,2]{1,3,2,0:T(2,128)S(1)} %gather_fusion.2), channel_id=1, source_target_pairs={{0,2},{1,3},{2,0},{3,1},{4,6},{5,7},{6,4},{7,5},{8,10},{9,11},{10,... | collective-permute-start | bytes 776 | tf_op jit(solution)/shard_map/ppermute | solution.py:38
  221.4 4.9 %collective-permute-start.7 = (f32[4,4,2,2]{1,3,2,0:T(2,128)S(1)}, f32[4,4,2,2]{1,3,2,0:T(2,128)S(1)}, u32[]{:S(2)}, u32[]{:S(2)}) collective-permute-start(f32[4,4,2,2]{1,3,2,0:T(2,128)S(1)} %gather_fusion.2), channel_id=1, source_target_pairs={{0,1},{1,2},{2,3},{3,0},{4,5},{5,6},{6,7},{7,4},{8,9},{9,10},{10,1... | collective-permute-start | bytes 776 | tf_op jit(solution)/shard_map/ppermute | solution.py:38
Sparse Core Ops, SparseCore 0:
  9.7 55.3 all-gather.2
  132.8 17.3 reduce-scatter.4
  152.8 39.5 reduce-scatter.6
  194.8 22.1 reduce-scatter.8
  219.4 20.5 reduce-scatter.10

commit v4 on v3

--- a/solution.py
+++ b/solution.py
@@ -84,8 +84,11 @@
     heads = heads.reshape(2, y_size, x_size, core_size, feat // (y_size * x_size * core_size), embed)
     heads = lax.psum_scatter(heads, "core", scatter_dimension=3, tiled=False)
     heads = lax.psum_scatter(heads, "x", scatter_dimension=2, tiled=False)
-    heads = lax.psum_scatter(heads, "y", scatter_dimension=1, tiled=False)
-    heads = lax.psum_scatter(heads, "blk", scatter_dimension=2, tiled=True)
+    blk_size = lax.axis_size("blk")
+    heads = heads.reshape(2, y_size, feat // (y_size * x_size * core_size), blk_size, embed // blk_size)
+    heads = heads.transpose(1, 3, 0, 2, 4).reshape((y_size * blk_size, 2) + heads.shape[2:3] + heads.shape[4:])
+    heads = lax.all_to_all(heads, ("y", "blk"), 0, 0, tiled=True)
+    heads = jnp.sum(heads, axis=0)
     heads = heads / weight_total
     return (loss_sum / weight_total, heads[0], heads[1])
 

time: 250 us -> 242 us (0.968)
  waiting for transfers between devices: 137 us -> 120 us
  starting transfers between devices: 12.4 us -> 19.7 us
    reduce_scatter x2 -> x0, waiting for transfers between devices: 14.9 us -> none  [the longest x1 10.7 us: per_device(): heads = lax.psum_scatter(heads, 'blk', scatter_dimension=2, tiled=True)]
    all_to_all x0 -> x1, starting transfers between devices: none -> 6.99 us  [per_device(): heads = lax.all_to_all(heads, ('y', 'blk'), 0, 0, tiled=True)]
  transfers between devices with their start and end apart: 15 -> 14, of which waited for: 12 -> 10; matrix products, arithmetic and copies ran while one was open for 6% -> 7% of each run, Pallas kernels for 0% -> 0%
where the time goes in v4:
time: 242 us
  waiting for transfers between devices  120 us (50%)
  matrix products  68.5 us (28%)
  starting transfers between devices  19.7 us (8%)
  between operations  16.4 us (7%)
  local copies, waits for them, and re-layouts  9.53 us (4%)
  other arithmetic  7.37 us (3%)
    all_gather x1, waiting for transfers between devices, per_device(): feat_prec_all = lax.all_gather(feat_prec, 'blk', axis=0, tiled=True)  50.2 us
    reduce_scatter x1, waiting for transfers between devices, per_device(): heads = lax.psum_scatter(heads, 'x', scatter_dimension=2, tiled=False)  39.8 us
    reduce_scatter x1, waiting for transfers between devices, per_device(): heads = lax.psum_scatter(heads, 'core', scatter_dimension=3, tiled=False)  17.5 us
    dot_general x1, matrix products, per_device(): jnp.dot(coeffs, unit16_prec, preferred_element_type=jnp.float32)  15.3 us
    dot_general x1, matrix products, per_device(): lax.dot_general(coeffs, unit16_prod, (((0,), (0,)), ((), ())), preferred_...  14.8 us
    ppermute x10, starting transfers between devices, gather_along(): pieces.append(lax.ppermute(values, axis, route))  12.6 us
    dot_general x1, matrix products, per_device(): lax.dot_general(feat_prec_all, dir_prec, (((0,), (0,)), ((), ())), prefer...  12.5 us
    dot_general x2, matrix products, embed_rows(): jnp.dot(features, weight, preferred_element_type=jnp.float32)  12 us
  transfers between devices with their start and end apart: 14, of which 10 were waited for; matrix products, arithmetic and copies ran while one was open for 7% of the time, Pallas kernels for 0%

profile of v4, /device:TPU:0, one launch (start us, length us, event | category | flops | bytes accessed | tf_op | source)
XLA Modules:
  0.0 241.6 jit_solution(16906249411543061909)
XLA Ops:
  7.2 0.7 all-gather.3.cloned.1.call-update
  8.0 0.7 reduce.4
  8.7 1.3 fusion.26
  10.0 4.8 %multiply_reduce_fusion.3 = (f32[768]{0:T(1024)S(1)}, f32[768,1024]{1,0:T(8,128)}) fusion(bf16[768,1024]{1,0:T(8,128)(2,1)} %param.10, bf16[1,768,768]{2,1,0:T(8,128)(2,1)} %param.6), kind=kOutput, calls=%fused_computation.24 | convolution fusion | flops 1209531648 | bytes 5901312 | tf_op jit(solution)/shard_map/dot_general | solution.py:11
  14.8 50.2 %all-gather.3.cloned.1.call-done = bf16[1,3072,768]{2,1,0:T(8,128)(2,1)} async-done(((bf16[1,768,768]{2,1,0:T(8,128)(2,1)}), bf16[1,3072,768]{2,1,0:T(8,128)(2,1)}) %all-gather.3.cloned.1.call-update) | async-done | bytes 4718608 | tf_op jit(solution)/shard_map/all_gather | solution.py:50
  65.0 7.2 %multiply_reduce_fusion.1 = (f32[3072]{0:T(1024)S(1)}, f32[3072,1024]{0,1:T(8,128)S(1)}) fusion(bf16[768,1024]{1,0:T(8,128)(2,1)S(1)} %copy-done, bf16[1,3072,768]{2,1,0:T(8,128)(2,1)} %all-gather.3.cloned.1.call-done), kind=kOutput, calls=%fused_computation.6 | convolution fusion | flops 4838126592 | bytes 18886656 | tf_op jit(solution)/shard_map/dot_general | solution.py:11
  72.3 10.3 %fusion = (f32[768]{0:T(1024)S(1)}, f32[768]{0:T(1024)}, f32[768,3072]{1,0:T(8,128)}) fusion(s32[768]{0:T(1024)S(1)} %reduce.4, f32[3072,1024]{0,1:T(8,128)S(1)} %get-tuple-element.14, f32[3072]{0:T(1024)S(1)} %add_sqrt_fusion, f32[768,1024]{1,0:T(8,128)S(1)} %copy-done.4, f32[768]{0:T(1024)S(1)} %add_sqrt_fusion.1), kind=kOutput, calls=%fused_computation.11 | convolution fusion | flops 4853856256 | bytes 25190400 | tf_op jit(solution)/shard_map/dot_general | solution.py:18
  82.6 14.8 %multiply_reduce_fusion = (f32[3072]{0:T(1024)S(1)}, f32[3072,1024]{0,1:T(8,128)}) fusion(f32[3072,1024]{0,1:T(8,128)} %copy-done.5, f32[3072]{0:T(1024)S(1)} %add_sqrt_fusion, f32[768,1024]{1,0:T(8,128)S(1)} %copy-done.4, f32[768]{0:T(1024)S(1)} %add_sqrt_fusion.1, f32[768,3072]{1,0:T(8,128)} %get-tuple-element.15, f32[768]{0:T(1024)S(1)} %get-tuple-element.3, ...), kind=kOutput, calls=%fused_computation.5 | convolution fusion | flops 4864865280 | bytes 37785600 | tf_op jit(solution)/shard_map/dot_general | solution.py:68
  97.3 15.3 %multiply_reduce_fusion.2 = (f32[768]{0:T(1024)S(1)}, f32[768,1024]{1,0:T(8,128)}) fusion(f32[768,1024]{1,0:T(8,128)S(1)} %copy-done.4, f32[768]{0:T(1024)S(1)} %add_sqrt_fusion.1, f32[3072,1024]{0,1:T(8,128)} %copy-done.5, f32[3072]{0:T(1024)S(1)} %add_sqrt_fusion, f32[768,3072]{1,0:T(8,128)} %get-tuple-element.15, f32[768]{0:T(1024)S(1)} %get-tuple-element.3, ...), kind=kOutput, calls=%fused_computation.19 | convolution fusion | flops 4860148736 | bytes 28339200 | tf_op jit(solution)/shard_map/dot_general | solution.py:67
  112.6 3.7 %fusion.9 = f32[1024,768]{0,1:T(8,128)S(1)} fusion(f32[768,1024]{1,0:T(8,128)} %get-tuple-element.19, f32[768]{0:T(1024)S(1)} %get-tuple-element.18, f32[768]{0:T(1024)S(1)} %add_sqrt_fusion.1, bf16[1,768,768]{2,1,0:T(8,128)(2,1)S(1)} %copy-done.3, f32[768,1024]{1,0:T(8,128)S(1)} %copy-done.4), kind=kOutput, calls=%fused_computation.26 | convolution fusion | flops 1212678144 | bytes 10622976 | tf_op jit(solution)/shard_map/dot_general | solution.py:73
  116.3 12.5 %fusion.1 = f32[1024,768]{0,1:T(8,128)S(1)} fusion(f32[3072,1024]{0,1:T(8,128)} %get-tuple-element.17, f32[3072]{0:T(1024)S(1)} %get-tuple-element.16, f32[3072]{0:T(1024)S(1)} %add_sqrt_fusion, bf16[1,3072,768]{2,1,0:T(8,128)(2,1)} %all-gather.3.cloned.1.call-done, f32[3072,1024]{0,1:T(8,128)} %copy-done.5), kind=kOutput, calls=%fused_computation.14 | convolution fusion | flops 4850712576 | bytes 33054720 | tf_op jit(solution)/shard_map/dot_general | solution.py:76
  129.4 3.2 %copy.38 = f32[2,4,4,2,24,1024]{5,4,1,0,2,3:T(8,128)} copy(f32[2,4,4,2,24,1024]{5,4,3,2,1,0:T(8,128)S(1)} %pad_maximum_fusion) | data formatting | bytes 12582912 | tf_op jit(solution)/shard_map/stack | solution.py:79
  132.7 17.5 %reduce-scatter.3.cloned.1.call-done = f32[2,4,4,1,24,1024]{5,4,1,0,2,3:T(8,128)} async-done(((f32[2,4,4,2,24,1024]{5,4,1,0,2,3:T(8,128)}), f32[2,4,4,1,24,1024]{5,4,1,0,2,3:T(8,128)}) %reduce-scatter.3.cloned.1.call-update) | async-done | bytes 3145744 | tf_op jit(solution)/shard_map/reduce_scatter | solution.py:85
  151.0 1.4 pad_maximum_fusion.5
  152.6 39.8 %reduce-scatter.5.cloned.1.call-done = f32[2,4,1,24,1024]{4,3,1,0,2:T(8,128)} async-done(((f32[2,4,4,24,1024]{4,3,1,0,2:T(8,128)}), f32[2,4,1,24,1024]{4,3,1,0,2:T(8,128)}) %reduce-scatter.5.cloned.1.call-update) | async-done | bytes 786448 | tf_op jit(solution)/shard_map/reduce_scatter | solution.py:86
  192.4 1.5 reshape_reduce_scatter.3
  193.9 1.0 copy.37
  194.9 7.0 %all-to-all-start = ((f32[16,2,24,256]{3,2,1,0:T(8,128)}), f32[16,2,24,256]{3,2,1,0:T(8,128)S(1)}, u32[]{:S(2)}, u32[]{:S(2)}) async-start(f32[16,2,24,256]{3,2,1,0:T(8,128)} %bitcast.28), calls=%async_computation.2 | async-start | bytes 1572864 | tf_op jit(solution)/shard_map/all_to_all | solution.py:90
  201.9 1.4 fusion.29
  203.8 0.9 collective-permute-start.3
  204.8 1.5 collective-permute-start.2
  206.8 0.7 collective-permute-done.3
  207.5 2.3 collective-permute-done.2
  209.8 1.2 collective-permute-done.1
  211.6 3.2 %collective-permute-start.6 = (f32[4,2,2]{2,1,0:T(2,128)S(1)}, f32[4,2,2]{2,1,0:T(2,128)S(1)}, u32[]{:S(2)}, u32[]{:S(2)}) collective-permute-start(f32[4,2,2]{2,1,0:T(2,128)S(1)} %gather_fusion.1), channel_id=1, source_target_pairs={{0,96},{32,0},{64,32},{96,64},{1,97},{33,1},{65,33},{97,65},{2,98}... | collective-permute-start | bytes 200 | tf_op jit(solution)/shard_map/ppermute | solution.py:38
  214.8 0.9 collective-permute-start.5
  215.6 0.9 collective-permute-start.4
  216.7 3.2 %collective-permute-done.5 = f32[4,2,2]{2,1,0:T(2,128)S(1)} collective-permute-done((f32[4,2,2]{2,1,0:T(2,128)S(1)}, f32[4,2,2]{2,1,0:T(2,128)S(1)}, u32[]{:S(2)}, u32[]{:S(2)}) %collective-permute-start.5) | collective-permute-done | bytes 96 | tf_op jit(solution)/shard_map/ppermute | solution.py:38
  221.1 2.7 %collective-permute-start.9 = (f32[4,4,2,2]{1,3,2,0:T(2,128)S(1)}, f32[4,4,2,2]{1,3,2,0:T(2,128)S(1)}, u32[]{:S(2)}, u32[]{:S(2)}) collective-permute-start(f32[4,4,2,2]{1,3,2,0:T(2,128)S(1)} %gather_fusion.2), channel_id=1, source_target_pairs={{0,3},{1,0},{2,1},{3,2},{4,7},{5,4},{6,5},{7,6},{8,11},{9,8},{10,9... | collective-permute-start | bytes 776 | tf_op jit(solution)/shard_map/ppermute | solution.py:38
  223.9 0.9 collective-permute-start.8
  224.7 0.9 collective-permute-start.7
  225.6 3.4 %collective-permute-done.8 = f32[4,4,2,2]{1,3,2,0:T(2,128)S(1)} collective-permute-done((f32[4,4,2,2]{1,3,2,0:T(2,128)S(1)}, f32[4,4,2,2]{1,3,2,0:T(2,128)S(1)}, u32[]{:S(2)}, u32[]{:S(2)}) %collective-permute-start.8) | collective-permute-done | bytes 288 | tf_op jit(solution)/shard_map/ppermute | solution.py:38
  (59 shorter events, 8.4 us)
Async XLA Ops:
  7.2 57.9 %copy-start = (bf16[768,1024]{1,0:T(8,128)(2,1)S(1)}, bf16[768,1024]{1,0:T(8,128)(2,1)}, u32[]{:S(2)}) copy-start(bf16[768,1024]{1,0:T(8,128)(2,1)} %param.11) | copy-start | bytes 4718596
  7.2 57.8 %all-gather.3.cloned.1.call-start = ((), (), s32[]{:S(2)}) async-start(), calls=%async_computation.5 | async-start | bytes 5898240 | tf_op jit(solution)/shard_map/all_gather | solution.py:50
  7.9 142.3 %reduce-scatter.3.cloned.1.call-start = ((), (), s32[]{:S(2)}) async-start(), calls=%async_computation.3 | async-start | bytes 9437184 | tf_op jit(solution)/shard_map/reduce_scatter | solution.py:85
  65.0 7.2 %copy-start.4 = (f32[768,1024]{1,0:T(8,128)S(1)}, f32[768,1024]{1,0:T(8,128)}, u32[]{:S(2)}) copy-start(f32[768,1024]{1,0:T(8,128)} %get-tuple-element.12) | copy-start | bytes 9437188
  72.2 10.3 %copy-start.5 = (f32[3072,1024]{0,1:T(8,128)}, f32[3072,1024]{0,1:T(8,128)S(1)}, u32[]{:S(2)}) copy-start(f32[3072,1024]{0,1:T(8,128)S(1)} %get-tuple-element.14) | copy-start | bytes 37748740
  97.3 15.3 %copy-start.3 = (bf16[1,768,768]{2,1,0:T(8,128)(2,1)S(1)}, bf16[1,768,768]{2,1,0:T(8,128)(2,1)}, u32[]{:S(2)}) copy-start(bf16[1,768,768]{2,1,0:T(8,128)(2,1)} %param.6) | copy-start | bytes 3538948
  132.6 17.7 %copy-start.2 = (f32[768]{0:T(1024)S(1)}, f32[768]{0:T(1024)}, u32[]{:S(2)}) copy-start(f32[768]{0:T(1024)} %get-tuple-element.4) | copy-start | bytes 9220
  132.7 101.3 %copy-start.1 = (bf16[768,1024]{1,0:T(8,128)(2,1)S(1)}, bf16[768,1024]{1,0:T(8,128)(2,1)}, u32[]{:S(2)}) copy-start(bf16[768,1024]{1,0:T(8,128)(2,1)} %param.11) | copy-start | bytes 4718596
  132.7 59.7 %reduce-scatter.5.cloned.1.call-start = ((), (), s32[]{:S(2)}) async-start(), calls=%async_computation.4 | async-start | bytes 3932160 | tf_op jit(solution)/shard_map/reduce_scatter | solution.py:86
  152.3 50.9 %collective-permute-start = (f32[2]{0:T(128)S(1)}, f32[2]{0:T(128)S(1)}, u32[]{:S(2)}, u32[]{:S(2)}) collective-permute-start(f32[2]{0:T(128)S(1)} %pad_maximum_fusion.5), channel_id=1, source_target_pairs={{0,4},{4,0},{1,5},{5,1},{2,6},{6,2},{3,7},{7,3},{8,12},{12,8},{9,1... | collective-permute-start | bytes 32 | tf_op jit(solution)/shard_map/ppermute | solution.py:38
  194.9 37.7 %all-to-all-start = ((f32[16,2,24,256]{3,2,1,0:T(8,128)}), f32[16,2,24,256]{3,2,1,0:T(8,128)S(1)}, u32[]{:S(2)}, u32[]{:S(2)}) async-start(f32[16,2,24,256]{3,2,1,0:T(8,128)} %bitcast.28), calls=%async_computation.2 | async-start | bytes 1572864 | tf_op jit(solution)/shard_map/all_to_all | solution.py:90
  203.8 3.6 %collective-permute-start.3 = (f32[2,2]{1,0:T(2,128)S(1)}, f32[2,2]{1,0:T(2,128)S(1)}, u32[]{:S(2)}, u32[]{:S(2)}) collective-permute-start(f32[2,2]{1,0:T(2,128)S(1)} %gather_fusion), channel_id=1, source_target_pairs={{0,24},{8,0},{16,8},{24,16},{1,25},{9,1},{17,9},{25,17},{2,26},{10... | collective-permute-start | bytes 56 | tf_op jit(solution)/shard_map/ppermute | solution.py:38
  204.8 5.1 %collective-permute-start.2 = (f32[2,2]{1,0:T(2,128)S(1)}, f32[2,2]{1,0:T(2,128)S(1)}, u32[]{:S(2)}, u32[]{:S(2)}) collective-permute-start(f32[2,2]{1,0:T(2,128)S(1)} %gather_fusion), channel_id=1, source_target_pairs={{0,16},{8,24},{16,0},{24,8},{1,17},{9,25},{17,1},{25,9},{2,18},{10... | collective-permute-start | bytes 56 | tf_op jit(solution)/shard_map/ppermute | solution.py:38
  206.2 4.8 %collective-permute-start.1 = (f32[2,2]{1,0:T(2,128)S(1)}, f32[2,2]{1,0:T(2,128)S(1)}, u32[]{:S(2)}, u32[]{:S(2)}) collective-permute-start(f32[2,2]{1,0:T(2,128)S(1)} %gather_fusion), channel_id=1, source_target_pairs={{0,8},{8,16},{16,24},{24,0},{1,9},{9,17},{17,25},{25,1},{2,10},{10... | collective-permute-start | bytes 56 | tf_op jit(solution)/shard_map/ppermute | solution.py:38
  211.6 5.0 %collective-permute-start.6 = (f32[4,2,2]{2,1,0:T(2,128)S(1)}, f32[4,2,2]{2,1,0:T(2,128)S(1)}, u32[]{:S(2)}, u32[]{:S(2)}) collective-permute-start(f32[4,2,2]{2,1,0:T(2,128)S(1)} %gather_fusion.1), channel_id=1, source_target_pairs={{0,96},{32,0},{64,32},{96,64},{1,97},{33,1},{65,33},{97,65},{2,98}... | collective-permute-start | bytes 200 | tf_op jit(solution)/shard_map/ppermute | solution.py:38
  214.8 5.1 %collective-permute-start.5 = (f32[4,2,2]{2,1,0:T(2,128)S(1)}, f32[4,2,2]{2,1,0:T(2,128)S(1)}, u32[]{:S(2)}, u32[]{:S(2)}) collective-permute-start(f32[4,2,2]{2,1,0:T(2,128)S(1)} %gather_fusion.1), channel_id=1, source_target_pairs={{0,64},{32,96},{64,0},{96,32},{1,65},{33,97},{65,1},{97,33},{2,66}... | collective-permute-start | bytes 200 | tf_op jit(solution)/shard_map/ppermute | solution.py:38
  215.6 4.8 %collective-permute-start.4 = (f32[4,2,2]{2,1,0:T(2,128)S(1)}, f32[4,2,2]{2,1,0:T(2,128)S(1)}, u32[]{:S(2)}, u32[]{:S(2)}) collective-permute-start(f32[4,2,2]{2,1,0:T(2,128)S(1)} %gather_fusion.1), channel_id=1, source_target_pairs={{0,32},{32,64},{64,96},{96,0},{1,33},{33,65},{65,97},{97,1},{2,34}... | collective-permute-start | bytes 200 | tf_op jit(solution)/shard_map/ppermute | solution.py:38
  221.1 4.5 %collective-permute-start.9 = (f32[4,4,2,2]{1,3,2,0:T(2,128)S(1)}, f32[4,4,2,2]{1,3,2,0:T(2,128)S(1)}, u32[]{:S(2)}, u32[]{:S(2)}) collective-permute-start(f32[4,4,2,2]{1,3,2,0:T(2,128)S(1)} %gather_fusion.2), channel_id=1, source_target_pairs={{0,3},{1,0},{2,1},{3,2},{4,7},{5,4},{6,5},{7,6},{8,11},{9,8},{10,9... | collective-permute-start | bytes 776 | tf_op jit(solution)/shard_map/ppermute | solution.py:38
  223.9 5.2 %collective-permute-start.8 = (f32[4,4,2,2]{1,3,2,0:T(2,128)S(1)}, f32[4,4,2,2]{1,3,2,0:T(2,128)S(1)}, u32[]{:S(2)}, u32[]{:S(2)}) collective-permute-start(f32[4,4,2,2]{1,3,2,0:T(2,128)S(1)} %gather_fusion.2), channel_id=1, source_target_pairs={{0,2},{1,3},{2,0},{3,1},{4,6},{5,7},{6,4},{7,5},{8,10},{9,11},{10,... | collective-permute-start | bytes 776 | tf_op jit(solution)/shard_map/ppermute | solution.py:38
  224.7 4.9 %collective-permute-start.7 = (f32[4,4,2,2]{1,3,2,0:T(2,128)S(1)}, f32[4,4,2,2]{1,3,2,0:T(2,128)S(1)}, u32[]{:S(2)}, u32[]{:S(2)}) collective-permute-start(f32[4,4,2,2]{1,3,2,0:T(2,128)S(1)} %gather_fusion.2), channel_id=1, source_target_pairs={{0,1},{1,2},{2,3},{3,0},{4,5},{5,6},{6,7},{7,4},{8,9},{9,10},{10,1... | collective-permute-start | bytes 776 | tf_op jit(solution)/shard_map/ppermute | solution.py:38
Sparse Core Ops, SparseCore 0:
  9.7 55.3 all-gather.2
  132.8 17.3 reduce-scatter.2
  152.8 39.5 reduce-scatter.4

commit v5 on v2

--- a/solution.py
+++ b/solution.py
@@ -30,6 +30,15 @@
     return ((gradient - unit_vec * projected) / radius).astype(jnp.bfloat16)
 
 
+def gathered_sum(value):
+    axes = ("y", "x", "core", "blk")
+    count = 1
+    for axis in axes:
+        count *= lax.axis_size(axis)
+    spread = jnp.broadcast_to(value.reshape(1, 1), (count, 1))
+    return jnp.sum(lax.all_to_all(spread, axes, 0, 0, tiled=True))
+
+
 def per_device(prod_feat, prec_feat, matched, row_weight, proj_prod, proj_prec):
     feat_prod = prod_feat[0]
     feat_prec = prec_feat[0]
@@ -46,9 +55,8 @@
     losses = LOGIT_SCALE + jnp.log(totals) - positive
     loss_local = jnp.sum(weights * losses)
     weight_local = jnp.sum(weights)
-    scalars = lax.psum(jnp.stack([loss_local, weight_local]), ("y", "x", "core", "blk"))
-    loss_sum = scalars[0]
-    weight_total = scalars[1]
+    loss_sum = gathered_sum(loss_local)
+    weight_total = gathered_sum(weight_local)
     coeffs = coefficient(scores, matches, weights, totals)
     grad_unit_prod = LOGIT_SCALE * jnp.dot(coeffs, unit16_prec, preferred_element_type=jnp.float32)
     grad_prec_part = LOGIT_SCALE * lax.dot_general(
@@ -70,8 +78,11 @@
     heads = heads.reshape(2, y_size, x_size, core_size, feat // (y_size * x_size * core_size), embed)
     heads = lax.psum_scatter(heads, "core", scatter_dimension=3, tiled=False)
     heads = lax.psum_scatter(heads, "x", scatter_dimension=2, tiled=False)
-    heads = lax.psum_scatter(heads, "y", scatter_dimension=1, tiled=False)
-    heads = lax.psum_scatter(heads, "blk", scatter_dimension=2, tiled=True)
+    blk_size = lax.axis_size("blk")
+    heads = heads.reshape(2, y_size, feat // (y_size * x_size * core_size), blk_size, embed // blk_size)
+    heads = heads.transpose(1, 3, 0, 2, 4).reshape((y_size * blk_size, 2) + heads.shape[2:3] + heads.shape[4:])
+    heads = lax.all_to_all(heads, ("y", "blk"), 0, 0, tiled=True)
+    heads = jnp.sum(heads, axis=0)
     heads = heads / weight_total
     return (loss_sum / weight_total, heads[0], heads[1])
 

time: 297 us -> 227 us (0.76)
  blocking collectives: 65 us -> 0 us
  waiting for transfers between devices: 135 us -> 105 us
  starting transfers between devices: 0.19 us -> 22.1 us
  local copies, waits for them, and re-layouts: 4.49 us -> 8.99 us
    psum x1 -> x0, blocking collectives: 65 us -> none  [per_device(): lax.psum(jnp.stack([loss_local, weight_local]), ('y', 'x', 'core', 'blk'))]
    reduce_scatter x1, waiting for transfers between devices: 42.1 us -> 16.3 us  [per_device(): heads = lax.psum_scatter(heads, 'x', scatter_dimension=2, tiled=False)]
    reduce_scatter x2 -> x0, waiting for transfers between devices: 24.6 us -> none  [the longest x1 24.6 us: per_device(): heads = lax.psum_scatter(heads, 'y', scatter_dimension=1, tiled=False)]
    all_to_all x0 -> x3, starting transfers between devices: none -> 21.9 us  [the longest x2 14.9 us: gathered_sum(): return jnp.sum(lax.all_to_all(spread, axes, 0, 0, tiled=True))]
    all_to_all x0 -> x3, waiting for transfers between devices: none -> 20.2 us  [the longest x1 11.7 us: per_device(): heads = lax.all_to_all(heads, ('y', 'blk'), 0, 0, tiled=True)]
  transfers between devices with their start and end apart: 5 -> 6, of which waited for: 4 -> 5; matrix products, arithmetic and copies ran while one was open for 3% -> 6% of each run, Pallas kernels for 0% -> 0%
where the time goes in v5:
time: 227 us; the launch traced here: 226 us
  waiting for transfers between devices  105 us (46%)
  matrix products  68.5 us (30%)
  starting transfers between devices  22.1 us (10%)
  between operations  16.3 us (7%)
  local copies, waits for them, and re-layouts  8.99 us (4%)
  other arithmetic  5.38 us (2%)
    all_gather x1, waiting for transfers between devices, per_device(): feat_prec_all = lax.all_gather(feat_prec, 'blk', axis=0, tiled=True)  50.2 us
    reduce_scatter x1, waiting for transfers between devices, per_device(): heads = lax.psum_scatter(heads, 'core', scatter_dimension=3, tiled=False)  17.5 us
    reduce_scatter x1, waiting for transfers between devices, per_device(): heads = lax.psum_scatter(heads, 'x', scatter_dimension=2, tiled=False)  16.3 us
    dot_general x1, matrix products, per_device(): jnp.dot(coeffs, unit16_prec, preferred_element_type=jnp.float32)  15.3 us
    all_to_all x2, starting transfers between devices, gathered_sum(): return jnp.sum(lax.all_to_all(spread, axes, 0, 0, tiled=True))  14.9 us
    dot_general x1, matrix products, per_device(): lax.dot_general(coeffs, unit16_prod, (((0,), (0,)), ((), ())), preferred_...  14.8 us
    dot_general x1, matrix products, per_device(): lax.dot_general(feat_prec_all, dir_prec, (((0,), (0,)), ((), ())), prefer...  12.5 us
    dot_general x2, matrix products, embed_rows(): jnp.dot(features, weight, preferred_element_type=jnp.float32)  12 us
  transfers between devices with their start and end apart: 6, of which 5 were waited for; matrix products, arithmetic and copies ran while one was open for 6% of the time, Pallas kernels for 0%

profile of v5, /device:TPU:0, one launch (start us, length us, event | category | flops | bytes accessed | tf_op | source)
XLA Modules:
  0.0 226.2 jit_solution(5391245518864547330)
XLA Ops:
  7.2 0.7 all-gather.3.cloned.1.call-update
  7.9 0.0 reduce-scatter.3.cloned.1.call-start
  8.0 0.7 reduce.6
  8.7 1.3 fusion.18
  10.0 4.8 %multiply_reduce_fusion.3 = (f32[768]{0:T(1024)S(1)}, f32[768,1024]{1,0:T(8,128)}) fusion(bf16[768,1024]{1,0:T(8,128)(2,1)} %param.10, bf16[1,768,768]{2,1,0:T(8,128)(2,1)} %param.6), kind=kOutput, calls=%fused_computation.20 | convolution fusion | flops 1209531648 | bytes 5901312 | tf_op jit(solution)/shard_map/dot_general | solution.py:11
  14.8 50.2 %all-gather.3.cloned.1.call-done = bf16[1,3072,768]{2,1,0:T(8,128)(2,1)} async-done(((bf16[1,768,768]{2,1,0:T(8,128)(2,1)}), bf16[1,3072,768]{2,1,0:T(8,128)(2,1)}) %all-gather.3.cloned.1.call-update) | async-done | bytes 4718608 | tf_op jit(solution)/shard_map/all_gather | solution.py:48
  65.0 7.2 %multiply_reduce_fusion.1 = (f32[3072]{0:T(1024)S(1)}, f32[3072,1024]{0,1:T(8,128)S(1)}) fusion(bf16[768,1024]{1,0:T(8,128)(2,1)S(1)} %copy-done, bf16[1,3072,768]{2,1,0:T(8,128)(2,1)} %all-gather.3.cloned.1.call-done), kind=kOutput, calls=%fused_computation.2 | convolution fusion | flops 4838126592 | bytes 18886656 | tf_op jit(solution)/shard_map/dot_general | solution.py:11
  72.3 10.3 %fusion = (f32[768]{0:T(1024)S(1)}, f32[768]{0:T(1024)}, f32[768,3072]{1,0:T(8,128)}) fusion(s32[768]{0:T(1024)S(1)} %reduce.6, f32[3072,1024]{0,1:T(8,128)S(1)} %get-tuple-element.12, f32[3072]{0:T(1024)S(1)} %add_sqrt_fusion, f32[768,1024]{1,0:T(8,128)S(1)} %copy-done.4, f32[768]{0:T(1024)S(1)} %add_sqrt_fusion.1), kind=kOutput, calls=%fused_computation.7 | convolution fusion | flops 4853856256 | bytes 25190400 | tf_op jit(solution)/shard_map/dot_general | solution.py:18
  82.6 14.8 %multiply_reduce_fusion = (f32[3072]{0:T(1024)S(1)}, f32[3072,1024]{0,1:T(8,128)}) fusion(f32[3072,1024]{0,1:T(8,128)} %copy-done.5, f32[3072]{0:T(1024)S(1)} %add_sqrt_fusion, f32[768,1024]{1,0:T(8,128)S(1)} %copy-done.4, f32[768]{0:T(1024)S(1)} %add_sqrt_fusion.1, f32[768,3072]{1,0:T(8,128)} %get-tuple-element.13, f32[768]{0:T(1024)S(1)} %get-tuple-element.3, ...), kind=kOutput, calls=%fused_computation.1 | convolution fusion | flops 4864865280 | bytes 37785600 | tf_op jit(solution)/shard_map/dot_general | solution.py:62
  97.3 15.3 %multiply_reduce_fusion.2 = (f32[768]{0:T(1024)S(1)}, f32[768,1024]{1,0:T(8,128)}) fusion(f32[768,1024]{1,0:T(8,128)S(1)} %copy-done.4, f32[768]{0:T(1024)S(1)} %add_sqrt_fusion.1, f32[3072,1024]{0,1:T(8,128)} %copy-done.5, f32[3072]{0:T(1024)S(1)} %add_sqrt_fusion, f32[768,3072]{1,0:T(8,128)} %get-tuple-element.13, f32[768]{0:T(1024)S(1)} %get-tuple-element.3, ...), kind=kOutput, calls=%fused_computation.15 | convolution fusion | flops 4860148736 | bytes 28339200 | tf_op jit(solution)/shard_map/dot_general | solution.py:61
  112.6 3.7 %fusion.9 = f32[1024,768]{0,1:T(8,128)S(1)} fusion(f32[768,1024]{1,0:T(8,128)} %get-tuple-element.17, f32[768]{0:T(1024)S(1)} %get-tuple-element.16, f32[768]{0:T(1024)S(1)} %add_sqrt_fusion.1, bf16[1,768,768]{2,1,0:T(8,128)(2,1)S(1)} %copy-done.3, f32[768,1024]{1,0:T(8,128)S(1)} %copy-done.4), kind=kOutput, calls=%fused_computation.22 | convolution fusion | flops 1212678144 | bytes 10622976 | tf_op jit(solution)/shard_map/dot_general | solution.py:67
  116.3 12.5 %fusion.1 = f32[1024,768]{0,1:T(8,128)S(1)} fusion(f32[3072,1024]{0,1:T(8,128)} %get-tuple-element.15, f32[3072]{0:T(1024)S(1)} %get-tuple-element.14, f32[3072]{0:T(1024)S(1)} %add_sqrt_fusion, bf16[1,3072,768]{2,1,0:T(8,128)(2,1)} %all-gather.3.cloned.1.call-done, f32[3072,1024]{0,1:T(8,128)} %copy-done.5), kind=kOutput, calls=%fused_computation.10 | convolution fusion | flops 4850712576 | bytes 33054720 | tf_op jit(solution)/shard_map/dot_general | solution.py:70
  128.8 0.6 pad_maximum_fusion
  129.4 3.2 %copy.20 = f32[2,4,4,2,24,1024]{5,4,1,0,2,3:T(8,128)} copy(f32[2,4,4,2,24,1024]{5,4,3,2,1,0:T(8,128)S(1)} %pad_maximum_fusion) | data formatting | bytes 12582912 | tf_op jit(solution)/shard_map/stack | solution.py:73
  132.7 0.0 reduce-scatter.5.cloned.1.call-start
  132.7 17.5 %reduce-scatter.3.cloned.1.call-done = f32[2,4,4,1,24,1024]{5,4,1,0,2,3:T(8,128)} async-done(((f32[2,4,4,2,24,1024]{5,4,1,0,2,3:T(8,128)}), f32[2,4,4,1,24,1024]{5,4,1,0,2,3:T(8,128)}) %reduce-scatter.3.cloned.1.call-update) | async-done | bytes 3145744 | tf_op jit(solution)/shard_map/reduce_scatter | solution.py:79
  150.2 1.3 broadcast_in_dim.10
  151.5 10.1 %all-to-all-start.1 = ((f32[128,1,1]{2,1,0:T(1,128)}), f32[128,1,1]{2,1,0:T(1,128)S(1)}, u32[]{:S(2)}, u32[]{:S(2)}) async-start(f32[128,1,1]{2,1,0:T(1,128)} %broadcast_in_dim.10), calls=%async_computation.1 | async-start | bytes 131072 | tf_op jit(solution)/shard_map/all_to_all | solution.py:39
  161.6 0.6 multiply_reduce_fusion.4
  162.2 8.5 %all-to-all-done.1 = f32[128,1,1]{2,1,0:T(1,128)S(1)} async-done(((f32[128,1,1]{2,1,0:T(1,128)}), f32[128,1,1]{2,1,0:T(1,128)S(1)}, u32[]{:S(2)}, u32[]{:S(2)}) %all-to-all-start.1) | async-done | bytes 544 | tf_op jit(solution)/shard_map/all_to_all | solution.py:39
  170.7 1.3 broadcast_in_dim.9
  172.0 4.8 %all-to-all-start = ((f32[128,1,1]{2,1,0:T(1,128)}), f32[128,1,1]{2,1,0:T(1,128)S(1)}, u32[]{:S(2)}, u32[]{:S(2)}) async-start(f32[128,1,1]{2,1,0:T(1,128)} %broadcast_in_dim.9), calls=%async_computation | async-start | bytes 131072 | tf_op jit(solution)/shard_map/all_to_all | solution.py:39
  176.8 16.3 %reduce-scatter.5.cloned.1.call-done = f32[2,4,1,24,1024]{4,3,1,0,2:T(8,128)} async-done(((f32[2,4,4,24,1024]{4,3,1,0,2:T(8,128)}), f32[2,4,1,24,1024]{4,3,1,0,2:T(8,128)}) %reduce-scatter.5.cloned.1.call-update) | async-done | bytes 786448 | tf_op jit(solution)/shard_map/reduce_scatter | solution.py:80
  193.1 1.5 reshape_reduce_scatter.3
  194.6 1.0 copy.19
  195.6 7.0 %all-to-all-start.2 = ((f32[16,2,24,256]{3,2,1,0:T(8,128)}), f32[16,2,24,256]{3,2,1,0:T(8,128)S(1)}, u32[]{:S(2)}, u32[]{:S(2)}) async-start(f32[16,2,24,256]{3,2,1,0:T(8,128)} %bitcast.8), calls=%async_computation.4 | async-start | bytes 1572864 | tf_op jit(solution)/shard_map/all_to_all | solution.py:84
  202.7 0.7 reduce_sum.106
  203.4 0.7 reduce_sum.104
  205.5 11.7 %all-to-all-done.2 = f32[16,2,24,256]{3,2,1,0:T(8,128)S(1)} async-done(((f32[16,2,24,256]{3,2,1,0:T(8,128)}), f32[16,2,24,256]{3,2,1,0:T(8,128)S(1)}, u32[]{:S(2)}, u32[]{:S(2)}) %all-to-all-start.2) | async-done | bytes 786464 | tf_op jit(solution)/shard_map/all_to_all | solution.py:84
  217.2 0.1 reduce_sum.109
  217.3 0.7 broadcast_divide_fusion.2
  217.9 0.6 slice_bitcast_fusion
  (18 shorter events, 0.1 us)
Async XLA Ops:
  7.2 57.9 %copy-start = (bf16[768,1024]{1,0:T(8,128)(2,1)S(1)}, bf16[768,1024]{1,0:T(8,128)(2,1)}, u32[]{:S(2)}) copy-start(bf16[768,1024]{1,0:T(8,128)(2,1)} %param.11) | copy-start | bytes 4718596
  7.2 57.8 %all-gather.3.cloned.1.call-start = ((), (), s32[]{:S(2)}) async-start(), calls=%async_computation.7 | async-start | bytes 5898240 | tf_op jit(solution)/shard_map/all_gather | solution.py:48
  7.9 142.3 %reduce-scatter.3.cloned.1.call-start = ((), (), s32[]{:S(2)}) async-start(), calls=%async_computation.5 | async-start | bytes 9437184 | tf_op jit(solution)/shard_map/reduce_scatter | solution.py:79
  65.0 7.2 %copy-start.4 = (f32[768,1024]{1,0:T(8,128)S(1)}, f32[768,1024]{1,0:T(8,128)}, u32[]{:S(2)}) copy-start(f32[768,1024]{1,0:T(8,128)} %get-tuple-element.10) | copy-start | bytes 9437188
  72.2 10.3 %copy-start.5 = (f32[3072,1024]{0,1:T(8,128)}, f32[3072,1024]{0,1:T(8,128)S(1)}, u32[]{:S(2)}) copy-start(f32[3072,1024]{0,1:T(8,128)S(1)} %get-tuple-element.12) | copy-start | bytes 37748740
  97.3 15.3 %copy-start.3 = (bf16[1,768,768]{2,1,0:T(8,128)(2,1)S(1)}, bf16[1,768,768]{2,1,0:T(8,128)(2,1)}, u32[]{:S(2)}) copy-start(bf16[1,768,768]{2,1,0:T(8,128)(2,1)} %param.6) | copy-start | bytes 3538948
  132.6 29.0 %copy-start.2 = (f32[768]{0:T(1024)S(1)}, f32[768]{0:T(1024)}, u32[]{:S(2)}) copy-start(f32[768]{0:T(1024)} %get-tuple-element.4) | copy-start | bytes 9220
  132.7 85.9 %copy-start.1 = (bf16[768,1024]{1,0:T(8,128)(2,1)S(1)}, bf16[768,1024]{1,0:T(8,128)(2,1)}, u32[]{:S(2)}) copy-start(bf16[768,1024]{1,0:T(8,128)(2,1)} %param.11) | copy-start | bytes 4718596
  132.7 60.4 %reduce-scatter.5.cloned.1.call-start = ((), (), s32[]{:S(2)}) async-start(), calls=%async_computation.6 | async-start | bytes 3932160 | tf_op jit(solution)/shard_map/reduce_scatter | solution.py:80
  151.5 19.2 %all-to-all-start.1 = ((f32[128,1,1]{2,1,0:T(1,128)}), f32[128,1,1]{2,1,0:T(1,128)S(1)}, u32[]{:S(2)}, u32[]{:S(2)}) async-start(f32[128,1,1]{2,1,0:T(1,128)} %broadcast_in_dim.10), calls=%async_computation.1 | async-start | bytes 131072 | tf_op jit(solution)/shard_map/all_to_all | solution.py:39
  172.0 23.6 %all-to-all-start = ((f32[128,1,1]{2,1,0:T(1,128)}), f32[128,1,1]{2,1,0:T(1,128)S(1)}, u32[]{:S(2)}, u32[]{:S(2)}) async-start(f32[128,1,1]{2,1,0:T(1,128)} %broadcast_in_dim.9), calls=%async_computation | async-start | bytes 131072 | tf_op jit(solution)/shard_map/all_to_all | solution.py:39
  195.6 21.6 %all-to-all-start.2 = ((f32[16,2,24,256]{3,2,1,0:T(8,128)}), f32[16,2,24,256]{3,2,1,0:T(8,128)S(1)}, u32[]{:S(2)}, u32[]{:S(2)}) async-start(f32[16,2,24,256]{3,2,1,0:T(8,128)} %bitcast.8), calls=%async_computation.4 | async-start | bytes 1572864 | tf_op jit(solution)/shard_map/all_to_all | solution.py:84
Sparse Core Ops, SparseCore 0:
  9.7 55.3 all-gather.2
  132.8 17.3 reduce-scatter.2
  152.8 40.2 reduce-scatter.4

commit v6 on v5

--- a/solution.py
+++ b/solution.py
@@ -77,11 +77,12 @@
     core_size = lax.axis_size("core")
     heads = heads.reshape(2, y_size, x_size, core_size, feat // (y_size * x_size * core_size), embed)
     heads = lax.psum_scatter(heads, "core", scatter_dimension=3, tiled=False)
-    heads = lax.psum_scatter(heads, "x", scatter_dimension=2, tiled=False)
     blk_size = lax.axis_size("blk")
-    heads = heads.reshape(2, y_size, feat // (y_size * x_size * core_size), blk_size, embed // blk_size)
-    heads = heads.transpose(1, 3, 0, 2, 4).reshape((y_size * blk_size, 2) + heads.shape[2:3] + heads.shape[4:])
-    heads = lax.all_to_all(heads, ("y", "blk"), 0, 0, tiled=True)
+    block_rows = feat // (y_size * x_size * core_size)
+    heads = heads.reshape(2, y_size, x_size, block_rows, blk_size, embed // blk_size)
+    heads = heads.transpose(1, 2, 4, 0, 3, 5)
+    heads = heads.reshape((y_size * x_size * blk_size, 2, block_rows, embed // blk_size))
+    heads = lax.all_to_all(heads, ("y", "x", "blk"), 0, 0, tiled=True)
     heads = jnp.sum(heads, axis=0)
     heads = heads / weight_total
     return (loss_sum / weight_total, heads[0], heads[1])

time: 227 us -> 232 us (1.022)
  waiting for transfers between devices: 105 us -> 97.5 us
  local copies, waits for them, and re-layouts: 8.99 us -> 15.9 us
    all_to_all x1, waiting for transfers between devices: 11.7 us -> 38 us  [per_device(): heads = lax.all_to_all(heads, ('y', 'x', 'blk'), 0, 0, tiled=True)]
    reduce_scatter x1, waiting for transfers between devices: 17.5 us -> 0.02 us  [per_device(): heads = lax.psum_scatter(heads, 'core', scatter_dimension=3, tiled=False)]
    reduce_scatter x1 -> x0, waiting for transfers between devices: 16.3 us -> none  [per_device(): heads = lax.psum_scatter(heads, 'x', scatter_dimension=2, tiled=False)]
    another operation x1, local copies, waits for them, and re-layouts: 1.49 us -> 5.18 us  [per_device(): heads.reshape(2, y_size, x_size, block_rows, blk_size, embed // blk_size)]
    all_to_all x1, starting transfers between devices: 7.04 us -> 10.3 us  [per_device(): heads = lax.all_to_all(heads, ('y', 'x', 'blk'), 0, 0, tiled=True)]
    transpose x1, local copies, waits for them, and re-layouts: 1.02 us -> 4.22 us  [per_device(): heads = heads.transpose(1, 2, 4, 0, 3, 5)]
  transfers between devices with their start and end apart: 6 -> 5, of which waited for: 5 -> 3; matrix products, arithmetic and copies ran while one was open for 6% -> 9% of each run, Pallas kernels for 0% -> 0%
where the time goes in v6:
time: 232 us; the launch traced here: 230 us
  waiting for transfers between devices  97.5 us (42%)
  matrix products  68.5 us (30%)
  starting transfers between devices  24.2 us (10%)
  between operations  16.6 us (7%)
  local copies, waits for them, and re-layouts  15.9 us (7%)
  other arithmetic  7.4 us (3%)
    all_gather x1, waiting for transfers between devices, per_device(): feat_prec_all = lax.all_gather(feat_prec, 'blk', axis=0, tiled=True)  50.2 us
    all_to_all x1, waiting for transfers between devices, per_device(): heads = lax.all_to_all(heads, ('y', 'x', 'blk'), 0, 0, tiled=True)  38 us
    dot_general x1, matrix products, per_device(): jnp.dot(coeffs, unit16_prec, preferred_element_type=jnp.float32)  15.3 us
    dot_general x1, matrix products, per_device(): lax.dot_general(coeffs, unit16_prod, (((0,), (0,)), ((), ())), preferred_...  14.8 us
    all_to_all x2, starting transfers between devices, gathered_sum(): return jnp.sum(lax.all_to_all(spread, axes, 0, 0, tiled=True))  13.8 us
    dot_general x1, matrix products, per_device(): lax.dot_general(feat_prec_all, dir_prec, (((0,), (0,)), ((), ())), prefer...  12.5 us
    dot_general x2, matrix products, embed_rows(): jnp.dot(features, weight, preferred_element_type=jnp.float32)  12 us
    all_to_all x1, starting transfers between devices, per_device(): heads = lax.all_to_all(heads, ('y', 'x', 'blk'), 0, 0, tiled=True)  10.3 us
  transfers between devices with their start and end apart: 5, of which 3 were waited for; matrix products, arithmetic and copies ran while one was open for 9% of the time, Pallas kernels for 0%

profile of v6, /device:TPU:0, one launch (start us, length us, event | category | flops | bytes accessed | tf_op | source)
XLA Modules:
  0.0 230.1 jit_solution(17575199774920998837)
XLA Ops:
  7.2 0.0 all-gather.3.cloned.1.call-start
  7.2 0.7 all-gather.3.cloned.1.call-update
  7.9 0.0 reduce-scatter.2.cloned.1.call-start
  8.0 0.7 reduce.6
  8.7 1.3 fusion.18
  10.0 4.8 %multiply_reduce_fusion.3 = (f32[768]{0:T(1024)S(1)}, f32[768,1024]{1,0:T(8,128)}) fusion(bf16[768,1024]{1,0:T(8,128)(2,1)} %param.10, bf16[1,768,768]{2,1,0:T(8,128)(2,1)} %param.6), kind=kOutput, calls=%fused_computation.20 | convolution fusion | flops 1209531648 | bytes 5901312 | tf_op jit(solution)/shard_map/dot_general | solution.py:11
  14.8 50.2 %all-gather.3.cloned.1.call-done = bf16[1,3072,768]{2,1,0:T(8,128)(2,1)} async-done(((bf16[1,768,768]{2,1,0:T(8,128)(2,1)}), bf16[1,3072,768]{2,1,0:T(8,128)(2,1)}) %all-gather.3.cloned.1.call-update) | async-done | bytes 4718608 | tf_op jit(solution)/shard_map/all_gather | solution.py:48
  65.0 7.2 %multiply_reduce_fusion.1 = (f32[3072]{0:T(1024)S(1)}, f32[3072,1024]{0,1:T(8,128)S(1)}) fusion(bf16[768,1024]{1,0:T(8,128)(2,1)S(1)} %copy-done, bf16[1,3072,768]{2,1,0:T(8,128)(2,1)} %all-gather.3.cloned.1.call-done), kind=kOutput, calls=%fused_computation.2 | convolution fusion | flops 4838126592 | bytes 18886656 | tf_op jit(solution)/shard_map/dot_general | solution.py:11
  72.3 10.3 %fusion = (f32[768]{0:T(1024)S(1)}, f32[768]{0:T(1024)}, f32[768,3072]{1,0:T(8,128)}) fusion(s32[768]{0:T(1024)S(1)} %reduce.6, f32[3072,1024]{0,1:T(8,128)S(1)} %get-tuple-element.12, f32[3072]{0:T(1024)S(1)} %add_sqrt_fusion, f32[768,1024]{1,0:T(8,128)S(1)} %copy-done.4, f32[768]{0:T(1024)S(1)} %add_sqrt_fusion.1), kind=kOutput, calls=%fused_computation.7 | convolution fusion | flops 4853856256 | bytes 25190400 | tf_op jit(solution)/shard_map/dot_general | solution.py:18
  82.6 14.8 %multiply_reduce_fusion = (f32[3072]{0:T(1024)S(1)}, f32[3072,1024]{0,1:T(8,128)}) fusion(f32[3072,1024]{0,1:T(8,128)} %copy-done.5, f32[3072]{0:T(1024)S(1)} %add_sqrt_fusion, f32[768,1024]{1,0:T(8,128)S(1)} %copy-done.4, f32[768]{0:T(1024)S(1)} %add_sqrt_fusion.1, f32[768,3072]{1,0:T(8,128)} %get-tuple-element.13, f32[768]{0:T(1024)S(1)} %get-tuple-element.3, ...), kind=kOutput, calls=%fused_computation.1 | convolution fusion | flops 4864865280 | bytes 37785600 | tf_op jit(solution)/shard_map/dot_general | solution.py:62
  97.3 15.3 %multiply_reduce_fusion.2 = (f32[768]{0:T(1024)S(1)}, f32[768,1024]{1,0:T(8,128)}) fusion(f32[768,1024]{1,0:T(8,128)S(1)} %copy-done.4, f32[768]{0:T(1024)S(1)} %add_sqrt_fusion.1, f32[3072,1024]{0,1:T(8,128)} %copy-done.5, f32[3072]{0:T(1024)S(1)} %add_sqrt_fusion, f32[768,3072]{1,0:T(8,128)} %get-tuple-element.13, f32[768]{0:T(1024)S(1)} %get-tuple-element.3, ...), kind=kOutput, calls=%fused_computation.15 | convolution fusion | flops 4860148736 | bytes 28339200 | tf_op jit(solution)/shard_map/dot_general | solution.py:61
  112.6 3.7 %fusion.9 = f32[1024,768]{0,1:T(8,128)S(1)} fusion(f32[768,1024]{1,0:T(8,128)} %get-tuple-element.17, f32[768]{0:T(1024)S(1)} %get-tuple-element.16, f32[768]{0:T(1024)S(1)} %add_sqrt_fusion.1, bf16[1,768,768]{2,1,0:T(8,128)(2,1)S(1)} %copy-done.3, f32[768,1024]{1,0:T(8,128)S(1)} %copy-done.4), kind=kOutput, calls=%fused_computation.22 | convolution fusion | flops 1212678144 | bytes 10622976 | tf_op jit(solution)/shard_map/dot_general | solution.py:67
  116.3 12.5 %fusion.1 = f32[1024,768]{0,1:T(8,128)S(1)} fusion(f32[3072,1024]{0,1:T(8,128)} %get-tuple-element.15, f32[3072]{0:T(1024)S(1)} %get-tuple-element.14, f32[3072]{0:T(1024)S(1)} %add_sqrt_fusion, bf16[1,3072,768]{2,1,0:T(8,128)(2,1)} %all-gather.3.cloned.1.call-done, f32[3072,1024]{0,1:T(8,128)} %copy-done.5), kind=kOutput, calls=%fused_computation.10 | convolution fusion | flops 4850712576 | bytes 33054720 | tf_op jit(solution)/shard_map/dot_general | solution.py:70
  128.8 0.6 pad_maximum_fusion
  129.4 3.2 %copy.20 = f32[2,4,4,2,24,1024]{5,4,2,1,0,3:T(8,128)} copy(f32[2,4,4,2,24,1024]{5,4,3,2,1,0:T(8,128)S(1)} %pad_maximum_fusion) | data formatting | bytes 12582912 | tf_op jit(solution)/shard_map/stack | solution.py:73
  132.6 0.0 reduce-scatter.2.cloned.1.call-update
  132.7 1.3 broadcast_in_dim.10
  134.0 8.9 %all-to-all-start.1 = ((f32[128,1,1]{2,1,0:T(1,128)}), f32[128,1,1]{2,1,0:T(1,128)S(1)}, u32[]{:S(2)}, u32[]{:S(2)}) async-start(f32[128,1,1]{2,1,0:T(1,128)} %broadcast_in_dim.10), calls=%async_computation.1 | async-start | bytes 131072 | tf_op jit(solution)/shard_map/all_to_all | solution.py:39
  142.9 0.6 multiply_reduce_fusion.4
  143.5 8.5 %all-to-all-done.1 = f32[128,1,1]{2,1,0:T(1,128)S(1)} async-done(((f32[128,1,1]{2,1,0:T(1,128)}), f32[128,1,1]{2,1,0:T(1,128)S(1)}, u32[]{:S(2)}, u32[]{:S(2)}) %all-to-all-start.1) | async-done | bytes 544 | tf_op jit(solution)/shard_map/all_to_all | solution.py:39
  152.0 1.3 broadcast_in_dim.9
  153.3 4.8 %all-to-all-start = ((f32[128,1,1]{2,1,0:T(1,128)}), f32[128,1,1]{2,1,0:T(1,128)S(1)}, u32[]{:S(2)}, u32[]{:S(2)}) async-start(f32[128,1,1]{2,1,0:T(1,128)} %broadcast_in_dim.9), calls=%async_computation | async-start | bytes 131072 | tf_op jit(solution)/shard_map/all_to_all | solution.py:39
  158.1 0.0 reduce-scatter.2.cloned.1.call-done
  158.2 5.2 %reshape_reduce_scatter.3 = f32[2,4,4,24,4,256]{5,4,3,2,1,0:T(4,128)} reshape(f32[2,4,4,1,24,1024]{5,4,2,1,0,3:T(8,128)} %reduce-scatter.2.cloned.1.call-done) | data formatting | bytes 6291456 | tf_op jit(solution)/shard_map/reshape;reduce_scatter | solution.py:82
  163.4 4.2 %copy.19 = f32[4,4,4,2,24,256]{5,4,3,2,1,0:T(8,128)} copy(f32[4,4,4,2,24,256]{5,2,4,1,0,3:T(4,128)} %bitcast.33) | data formatting | bytes 6291456 | tf_op jit(solution)/shard_map/transpose | solution.py:83
  167.6 10.3 %all-to-all-start.2 = ((f32[64,2,24,256]{3,2,1,0:T(8,128)}), f32[64,2,24,256]{3,2,1,0:T(8,128)}, u32[]{:S(2)}, u32[]{:S(2)}) async-start(f32[64,2,24,256]{3,2,1,0:T(8,128)} %bitcast.32), calls=%async_computation.3 | async-start | bytes 6291456 | tf_op jit(solution)/shard_map/all_to_all | solution.py:85
  177.9 0.7 reduce_sum.106
  178.7 0.7 reduce_sum.104
  180.7 38.0 %all-to-all-done.2 = f32[64,2,24,256]{3,2,1,0:T(8,128)} async-done(((f32[64,2,24,256]{3,2,1,0:T(8,128)}), f32[64,2,24,256]{3,2,1,0:T(8,128)}, u32[]{:S(2)}, u32[]{:S(2)}) %all-to-all-start.2) | async-done | bytes 3145760 | tf_op jit(solution)/shard_map/all_to_all | solution.py:85
  218.8 2.1 reduce_sum.109
  220.9 0.7 broadcast_divide_fusion.2
  221.5 0.6 slice_bitcast_fusion
  (15 shorter events, 0.0 us)
Async XLA Ops:
  7.2 57.9 %copy-start = (bf16[768,1024]{1,0:T(8,128)(2,1)S(1)}, bf16[768,1024]{1,0:T(8,128)(2,1)}, u32[]{:S(2)}) copy-start(bf16[768,1024]{1,0:T(8,128)(2,1)} %param.11) | copy-start | bytes 4718596
  7.2 57.8 %all-gather.3.cloned.1.call-start = ((), (), s32[]{:S(2)}) async-start(), calls=%async_computation.5 | async-start | bytes 5898240 | tf_op jit(solution)/shard_map/all_gather | solution.py:48
  7.9 150.2 %reduce-scatter.2.cloned.1.call-start = ((), (), s32[]{:S(2)}) async-start(), calls=%async_computation.4 | async-start | bytes 9437184 | tf_op jit(solution)/shard_map/reduce_scatter | solution.py:79
  65.0 7.2 %copy-start.4 = (f32[768,1024]{1,0:T(8,128)S(1)}, f32[768,1024]{1,0:T(8,128)}, u32[]{:S(2)}) copy-start(f32[768,1024]{1,0:T(8,128)} %get-tuple-element.10) | copy-start | bytes 9437188
  72.2 10.3 %copy-start.5 = (f32[3072,1024]{0,1:T(8,128)}, f32[3072,1024]{0,1:T(8,128)S(1)}, u32[]{:S(2)}) copy-start(f32[3072,1024]{0,1:T(8,128)S(1)} %get-tuple-element.12) | copy-start | bytes 37748740
  97.3 15.3 %copy-start.3 = (bf16[1,768,768]{2,1,0:T(8,128)(2,1)S(1)}, bf16[1,768,768]{2,1,0:T(8,128)(2,1)}, u32[]{:S(2)}) copy-start(bf16[1,768,768]{2,1,0:T(8,128)(2,1)} %param.6) | copy-start | bytes 3538948
  132.6 10.3 %copy-start.2 = (f32[768]{0:T(1024)S(1)}, f32[768]{0:T(1024)}, u32[]{:S(2)}) copy-start(f32[768]{0:T(1024)} %get-tuple-element.4) | copy-start | bytes 9220
  134.0 18.0 %all-to-all-start.1 = ((f32[128,1,1]{2,1,0:T(1,128)}), f32[128,1,1]{2,1,0:T(1,128)S(1)}, u32[]{:S(2)}, u32[]{:S(2)}) async-start(f32[128,1,1]{2,1,0:T(1,128)} %broadcast_in_dim.10), calls=%async_computation.1 | async-start | bytes 131072 | tf_op jit(solution)/shard_map/all_to_all | solution.py:39
  153.3 14.3 %all-to-all-start = ((f32[128,1,1]{2,1,0:T(1,128)}), f32[128,1,1]{2,1,0:T(1,128)S(1)}, u32[]{:S(2)}, u32[]{:S(2)}) async-start(f32[128,1,1]{2,1,0:T(1,128)} %broadcast_in_dim.9), calls=%async_computation | async-start | bytes 131072 | tf_op jit(solution)/shard_map/all_to_all | solution.py:39
  163.4 58.8 %copy-start.1 = (bf16[768,1024]{1,0:T(8,128)(2,1)S(1)}, bf16[768,1024]{1,0:T(8,128)(2,1)}, u32[]{:S(2)}) copy-start(bf16[768,1024]{1,0:T(8,128)(2,1)} %param.11) | copy-start | bytes 4718596
  167.6 51.2 %all-to-all-start.2 = ((f32[64,2,24,256]{3,2,1,0:T(8,128)}), f32[64,2,24,256]{3,2,1,0:T(8,128)}, u32[]{:S(2)}, u32[]{:S(2)}) async-start(f32[64,2,24,256]{3,2,1,0:T(8,128)} %bitcast.32), calls=%async_computation.3 | async-start | bytes 6291456 | tf_op jit(solution)/shard_map/all_to_all | solution.py:85
Sparse Core Ops, SparseCore 0:
  9.7 55.3 all-gather.2
  132.8 17.3 reduce-scatter.1

commit v7 on v5

--- a/solution.py
+++ b/solution.py
@@ -44,31 +44,49 @@
     feat_prec = prec_feat[0]
     targets = matched[0]
     weights = row_weight[0]
+    row_count = feat_prec.shape[0]
+    blk_size = lax.axis_size("blk")
+    blk_pos = lax.axis_index("blk")
+    from_next = lax.ppermute(feat_prec, "blk", [(i, (i - 1) % blk_size) for i in range(blk_size)])
+    from_prev = lax.ppermute(feat_prec, "blk", [(i, (i + 1) % blk_size) for i in range(blk_size)])
+    half = row_count // 2
+    low_half = lax.ppermute(from_prev[:half], "blk", [(i, (i + 1) % blk_size) for i in range(blk_size)])
+    high_half = lax.ppermute(from_next[half:], "blk", [(i, (i - 1) % blk_size) for i in range(blk_size)])
+    opposite = jnp.concatenate([low_half, high_half], axis=0)
+    blocks = [feat_prec, from_next, from_prev, opposite]
+    sources = [blk_pos, (blk_pos + 1) % blk_size, (blk_pos - 1) % blk_size, (blk_pos + 2) % blk_size]
     unit_prod, unit16_prod, radius_prod = embed_rows(feat_prod, proj_prod)
-    feat_prec_all = lax.all_gather(feat_prec, "blk", axis=0, tiled=True)
-    unit_prec, unit16_prec, radius_prec = embed_rows(feat_prec_all, proj_prec)
-    scores = similarity(unit16_prod, unit16_prec)
-    columns = lax.iota(jnp.int32, unit16_prec.shape[0])
-    matches = targets[:, None] == columns[None, :]
-    totals = jnp.sum(jnp.exp(scores - LOGIT_SCALE), axis=1)
-    positive = jnp.sum(jnp.where(matches, scores, 0.0), axis=1)
+    embedded = [embed_rows(block, proj_prec) for block in blocks]
+    scores = [similarity(unit16_prod, unit16) for (_, unit16, _) in embedded]
+    local_columns = lax.iota(jnp.int32, row_count)
+    matches = [targets[:, None] == (source * row_count + local_columns)[None, :] for source in sources]
+    totals = sum(jnp.sum(jnp.exp(block_scores - LOGIT_SCALE), axis=1) for block_scores in scores)
+    positive = sum(
+        jnp.sum(jnp.where(block_matches, block_scores, 0.0), axis=1)
+        for block_matches, block_scores in zip(matches, scores)
+    )
     losses = LOGIT_SCALE + jnp.log(totals) - positive
     loss_local = jnp.sum(weights * losses)
     weight_local = jnp.sum(weights)
     loss_sum = gathered_sum(loss_local)
     weight_total = gathered_sum(weight_local)
-    coeffs = coefficient(scores, matches, weights, totals)
-    grad_unit_prod = LOGIT_SCALE * jnp.dot(coeffs, unit16_prec, preferred_element_type=jnp.float32)
-    grad_prec_part = LOGIT_SCALE * lax.dot_general(
-        coeffs, unit16_prod, (((0,), (0,)), ((), ())), preferred_element_type=jnp.float32
-    )
-    dir_prod = back_norm(unit_prod, radius_prod, grad_unit_prod)
-    dir_prec = back_norm(unit_prec, radius_prec, grad_prec_part)
+    grad_unit_prod = 0.0
+    head_prec = 0.0
+    for block, (unit_prec, unit16_prec, radius_prec), block_scores, block_matches in zip(
+        blocks, embedded, scores, matches
+    ):
+        coeffs = coefficient(block_scores, block_matches, weights, totals)
+        grad_unit_prod = grad_unit_prod + jnp.dot(coeffs, unit16_prec, preferred_element_type=jnp.float32)
+        grad_prec_part = LOGIT_SCALE * lax.dot_general(
+            coeffs, unit16_prod, (((0,), (0,)), ((), ())), preferred_element_type=jnp.float32
+        )
+        dir_prec = back_norm(unit_prec, radius_prec, grad_prec_part)
+        head_prec = head_prec + lax.dot_general(
+            block, dir_prec, (((0,), (0,)), ((), ())), preferred_element_type=jnp.float32
+        )
+    dir_prod = back_norm(unit_prod, radius_prod, LOGIT_SCALE * grad_unit_prod)
     head_prod = lax.dot_general(
         feat_prod, dir_prod, (((0,), (0,)), ((), ())), preferred_element_type=jnp.float32
-    )
-    head_prec = lax.dot_general(
-        feat_prec_all, dir_prec, (((0,), (0,)), ((), ())), preferred_element_type=jnp.float32
     )
     heads = jnp.stack([head_prod, head_prec])
     feat, embed = head_prod.shape

time: 227 us -> 205 us (0.903)
  waiting for transfers between devices: 105 us -> 71 us
  blocking collectives: 0 us -> 19 us
  matrix products: 68.5 us -> 61.1 us
    all_gather x1 -> x0, waiting for transfers between devices: 50.2 us -> none  [per_device(): feat_prec_all = lax.all_gather(feat_prec, 'blk', axis=0, tiled=True)]
    ppermute x0 -> x4, waiting for transfers between devices: none -> 26.1 us  [the longest x1 16.7 us: per_device(): lax.ppermute(feat_prec, 'blk', [(i, (i - 1) % blk_size) for i in range(bl...]
    all_to_all x0 -> x1, blocking collectives: none -> 19 us  [gathered_sum(): return jnp.sum(lax.all_to_all(spread, axes, 0, 0, tiled=True))]
    all_to_all x2 -> x1, starting transfers between devices: 14.9 us -> 4.87 us  [gathered_sum(): return jnp.sum(lax.all_to_all(spread, axes, 0, 0, tiled=True))]
    all_to_all x2 -> x1, waiting for transfers between devices: 8.49 us -> 0.01 us  [gathered_sum(): return jnp.sum(lax.all_to_all(spread, axes, 0, 0, tiled=True))]
    ppermute x0 -> x4, starting transfers between devices: none -> 8.21 us  [the longest x1 4.19 us: per_device(): lax.ppermute(feat_prec, 'blk', [(i, (i - 1) % blk_size) for i in range(bl...]
    dot_general x1 -> x4, matrix products: 12.5 us -> 9.04 us  [per_device(): lax.dot_general(block, dir_prec, (((0,), (0,)), ((), ())), preferred_elem...]
    dot_general x1 -> x4, matrix products: 10.3 us -> 7.66 us  [similarity(): lax.dot_general(queries, key_rows, (((1,), (1,)), ((), ())), preferred_el...]
  transfers between devices with their start and end apart: 6 -> 8, of which waited for: 5 -> 5; matrix products, arithmetic and copies ran while one was open for 6% -> 11% of each run, Pallas kernels for 0% -> 0%
where the time goes in v7:
time: 205 us; the launch traced here: 204 us
  waiting for transfers between devices  71 us (35%)
  matrix products  61.1 us (30%)
  starting transfers between devices  20.1 us (10%)
  blocking collectives  19 us (9%)
  between operations  16.8 us (8%)
  local copies, waits for them, and re-layouts  9.95 us (5%)
  other arithmetic  6.23 us (3%)
    all_to_all x1, blocking collectives, gathered_sum(): return jnp.sum(lax.all_to_all(spread, axes, 0, 0, tiled=True))  19 us
    reduce_scatter x1, waiting for transfers between devices, per_device(): heads = lax.psum_scatter(heads, 'x', scatter_dimension=2, tiled=False)  17 us
    ppermute x1, waiting for transfers between devices, per_device(): lax.ppermute(feat_prec, 'blk', [(i, (i - 1) % blk_size) for i in range(bl...  16.7 us
    dot_general x4, matrix products, per_device(): jnp.dot(coeffs, unit16_prec, preferred_element_type=jnp.float32)  16.6 us
    reduce_scatter x1, waiting for transfers between devices, per_device(): heads = lax.psum_scatter(heads, 'core', scatter_dimension=3, tiled=False)  16.1 us
    dot_general x4, matrix products, per_device(): lax.dot_general(coeffs, unit16_prod, (((0,), (0,)), ((), ())), preferred_...  13.5 us
    all_to_all x1, waiting for transfers between devices, per_device(): heads = lax.all_to_all(heads, ('y', 'blk'), 0, 0, tiled=True)  11.7 us
    dot_general x5, matrix products, embed_rows(): jnp.dot(features, weight, preferred_element_type=jnp.float32)  10.5 us
  transfers between devices with their start and end apart: 8, of which 5 were waited for; matrix products, arithmetic and copies ran while one was open for 11% of the time, Pallas kernels for 0%

profile of v7, /device:TPU:0, one launch (start us, length us, event | category | flops | bytes accessed | tf_op | source)
XLA Modules:
  0.0 204.2 jit_solution(14685247363533252547)
XLA Ops:
  7.2 4.2 %collective-permute-start = (bf16[768,768]{1,0:T(8,128)(2,1)}, bf16[768,768]{1,0:T(8,128)(2,1)}, u32[]{:S(2)}, u32[]{:S(2)}) collective-permute-start(bf16[768,768]{1,0:T(8,128)(2,1)} %bitcast.54), channel_id=1, source_target_pairs={{0,3},{1,0},{2,1},{3,2},{4,7},{5,4},{6,5},{7,6},{8,11},{9,8},{10,9... | collective-permute-start | bytes 3538952 | tf_op jit(solution)/shard_map/ppermute | solution.py:50
  13.4 3.3 %multiply_reduce_fusion.9 = (f32[768]{0:T(1024)S(1)}, f32[768,1024]{1,0:T(8,128)S(1)}) fusion(bf16[768,1024]{1,0:T(8,128)(2,1)} %param.10, bf16[1,768,768]{2,1,0:T(8,128)(2,1)} %param.6), kind=kOutput, calls=%fused_computation.17 | convolution fusion | flops 1209531648 | bytes 5901312 | tf_op jit(solution)/shard_map/dot_general | solution.py:11
  18.7 1.5 fusion.41
  20.2 16.7 %collective-permute-done = bf16[768,768]{1,0:T(8,128)(2,1)} collective-permute-done((bf16[768,768]{1,0:T(8,128)(2,1)}, bf16[768,768]{1,0:T(8,128)(2,1)}, u32[]{:S(2)}, u32[]{:S(2)}) %collective-permute-start) | collective-permute-done | bytes 1179680 | tf_op jit(solution)/shard_map/ppermute | solution.py:50
  38.1 3.8 %collective-permute-start.3 = (bf16[384,768]{1,0:T(8,128)(2,1)S(1)}, bf16[384,768]{1,0:T(8,128)(2,1)S(1)}, u32[]{:S(2)}, u32[]{:S(2)}) collective-permute-start(bf16[384,768]{1,0:T(8,128)(2,1)S(1)} %slice.17), channel_id=1, source_target_pairs={{0,3},{1,0},{2,1},{3,2},{4,7},{5,4},{6,5},{7,6},{8,11},{9,8},{10,9... | collective-permute-start | bytes 1769480 | tf_op jit(solution)/shard_map/ppermute | solution.py:54
  43.6 2.7 %multiply_reduce_fusion.7 = (f32[768]{0:T(1024)S(1)}, f32[768,1024]{1,0:T(8,128)S(1)}) fusion(bf16[768,768]{1,0:T(8,128)(2,1)} %collective-permute-done, bf16[768,1024]{1,0:T(8,128)(2,1)S(1)} %copy-done), kind=kOutput, calls=%fused_computation.15 | convolution fusion | flops 1209531648 | bytes 5901312 | tf_op jit(solution)/shard_map/dot_general | solution.py:11
  46.4 1.5 fusion.33
  47.9 9.4 %collective-permute-done.2 = bf16[384,768]{1,0:T(8,128)(2,1)S(1)} collective-permute-done((bf16[384,768]{1,0:T(8,128)(2,1)S(1)}, bf16[384,768]{1,0:T(8,128)(2,1)S(1)}, u32[]{:S(2)}, u32[]{:S(2)}) %collective-permute-start.2) | collective-permute-done | bytes 589856 | tf_op jit(solution)/shard_map/ppermute | solution.py:53
  57.4 1.5 multiply_reduce_fusion.5
  58.8 1.5 fusion.29
  60.3 3.2 %fusion.17 = (f32[768]{0:T(1024)S(1)}, f32[768]{0:T(1024)S(1)}, f32[768]{0:T(1024)S(1)}, f32[768]{0:T(1024)S(1)}, f32[768]{0:T(1024)S(1)}, /*index=5*/f32[768]{0...) fusion(s32[768]{0:T(1024)S(1)} %get-tuple-element.46, s32[768]{0:T(1024)S(1)} %reduce.6, ...), kind=kOutput, calls=%fused_computation.47 | convolution fusion | flops 1223682048 | bytes 14198784 | tf_op jit(solution)/shard_map/dot_general | solution.py:18
  64.2 3.4 %fusion.35 = f32[768,1024]{1,0:T(8,128)} fusion(f32[768,768]{0,1:T(8,128)S(1)} %get-tuple-element.33, f32[768]{0:T(1024)S(1)} %get-tuple-element.14, f32[768]{0:T(1024)S(1)} %get-tuple-element.12, s32[768]{0:T(1024)S(1)} %reduce.6, s32[768]{0:T(1024)S(1)} %get-tuple-element.46, f32[768,1024]{1,0:T(8,128)S(1)} %get-tuple-element.26, f32[768]{0:T(1024)S(1)} %add_sqrt_fusion.2), kind=kOutput, calls=%fused_computation.70 | convolution fusion | flops 1214251008 | bytes 8666112 | tf_op jit(solution)/shard_map/dot_general | solution.py:79
  67.5 3.4 %multiply_reduce_fusion.2 = (f32[768]{0:T(1024)S(1)}, f32[768,1024]{1,0:T(8,128)}) fusion(f32[768,1024]{1,0:T(8,128)S(1)} %get-tuple-element.26, f32[768]{0:T(1024)S(1)} %add_sqrt_fusion.2, bf16[768,1024]{1,0:T(8,128)(2,1)S(1)} %fusion.50, f32[768,768]{0,1:T(8,128)S(1)} %get-tuple-element.33, f32[768]{0:T(1024)S(1)} %get-tuple-element.14, ...), kind=kOutput, calls=%fused_computation.7 | convolution fusion | flops 1215823104 | bytes 10242048 | tf_op jit(solution)/shard_map/dot_general | solution.py:80
  70.9 3.4 %fusion.31 = f32[768,1024]{1,0:T(8,128)} fusion(f32[768,768]{0,1:T(8,128)S(1)} %fusion.33, f32[768]{0:T(1024)S(1)} %get-tuple-element.14, f32[768]{0:T(1024)S(1)} %get-tuple-element.12, s32[768]{0:T(1024)S(1)} %reduce.6, s32[768]{0:T(1024)S(1)} %get-tuple-element.45, f32[768,1024]{1,0:T(8,128)S(1)} %get-tuple-element.28, f32[768]{0:T(1024)S(1)} %add_sqrt_fusion.1), kind=kOutput, calls=%fused_computation.66 | convolution fusion | flops 1214251008 | bytes 8666112 | tf_op jit(solution)/shard_map/dot_general | solution.py:79
  74.4 3.4 %multiply_reduce_fusion.1 = (f32[768]{0:T(1024)S(1)}, f32[768,1024]{1,0:T(8,128)}) fusion(f32[768,1024]{1,0:T(8,128)S(1)} %get-tuple-element.28, f32[768]{0:T(1024)S(1)} %add_sqrt_fusion.1, bf16[768,1024]{1,0:T(8,128)(2,1)S(1)} %fusion.50, f32[768,768]{0,1:T(8,128)S(1)} %fusion.33, f32[768]{0:T(1024)S(1)} %get-tuple-element.14, ...), kind=kOutput, calls=%fused_computation.5 | convolution fusion | flops 1215823104 | bytes 10242048 | tf_op jit(solution)/shard_map/dot_general | solution.py:80
  77.7 3.4 %fusion.39 = f32[768,1024]{1,0:T(8,128)} fusion(f32[768,768]{0,1:T(8,128)S(1)} %fusion.41, f32[768]{0:T(1024)S(1)} %get-tuple-element.14, f32[768]{0:T(1024)S(1)} %get-tuple-element.12, s32[768]{0:T(1024)S(1)} %reduce.6, s32[768]{0:T(1024)S(1)} %get-tuple-element.47, f32[768,1024]{1,0:T(8,128)S(1)} %get-tuple-element.32, f32[768]{0:T(1024)S(1)} %add_sqrt_fusion.3), kind=kOutput, calls=%fused_computation.74 | convolution fusion | flops 1214251008 | bytes 8666112 | tf_op jit(solution)/shard_map/dot_general | solution.py:79
  81.1 3.4 %multiply_reduce_fusion = (f32[768]{0:T(1024)S(1)}, f32[768,1024]{1,0:T(8,128)}) fusion(f32[768,1024]{1,0:T(8,128)S(1)} %get-tuple-element.30, f32[768]{0:T(1024)S(1)} %add_sqrt_fusion, bf16[768,1024]{1,0:T(8,128)(2,1)S(1)} %fusion.50, f32[768,768]{0,1:T(8,128)S(1)} %fusion.29, f32[768]{0:T(1024)S(1)} %get-tuple-element.14, f32[768]{0:T(1024)S(1)} %get-tuple-element.12, ...), kind=kOutput, calls=%fused_computation.3 | convolution fusion | flops 1215823104 | bytes 10242048 | tf_op jit(solution)/shard_map/dot_general | solution.py:80
  84.6 3.3 %multiply_reduce_fusion.3 = (f32[768]{0:T(1024)S(1)}, f32[768,1024]{1,0:T(8,128)}) fusion(f32[768,1024]{1,0:T(8,128)S(1)} %get-tuple-element.32, f32[768]{0:T(1024)S(1)} %add_sqrt_fusion.3, bf16[768,1024]{1,0:T(8,128)(2,1)S(1)} %fusion.50, f32[768,768]{0,1:T(8,128)S(1)} %fusion.41, f32[768]{0:T(1024)S(1)} %get-tuple-element.14, ...), kind=kOutput, calls=%fused_computation.9 | convolution fusion | flops 1215823104 | bytes 10242048 | tf_op jit(solution)/shard_map/dot_general | solution.py:80
  87.9 6.3 %multiply_reduce_fusion.4 = (f32[768]{0:T(1024)S(1)}, f32[768,1024]{1,0:T(8,128)}) fusion(f32[768,1024]{1,0:T(8,128)S(1)} %get-tuple-element.24, f32[768]{0:T(1024)S(1)} %add_sqrt_fusion.4, f32[768,1024]{1,0:T(8,128)S(1)} %get-tuple-element.30, f32[768]{0:T(1024)S(1)} %add_sqrt_fusion, f32[768,768]{0,1:T(8,128)S(1)} %fusion.29, ...), kind=kOutput, calls=%fused_computation.11 | convolution fusion | flops 1219755264 | bytes 21255168 | tf_op jit(solution)/shard_map/dot_general | solution.py:79
  94.3 3.8 %fusion.20 = f32[1024,768]{0,1:T(8,128)S(1)} fusion(f32[768,1024]{1,0:T(8,128)} %get-tuple-element.43, f32[768]{0:T(1024)S(1)} %get-tuple-element.42, f32[768]{0:T(1024)S(1)} %add_sqrt_fusion.4, bf16[1,768,768]{2,1,0:T(8,128)(2,1)S(1)} %copy-done.2, f32[768,1024]{1,0:T(8,128)S(1)} %get-tuple-element.24), kind=kOutput, calls=%fused_computation.55 | convolution fusion | flops 1211891712 | bytes 10622976 | tf_op jit(solution)/shard_map/dot_general | solution.py:88
  98.1 1.9 fusion.21
  100.0 3.3 %fusion.22 = f32[1024,768]{0,1:T(8,128)S(1)} fusion(bf16[768,768]{1,0:T(8,128)(2,1)} %collective-permute-done, f32[768,1024]{1,0:T(8,128)S(1)} %copy-done.6, f32[768]{0:T(1024)S(1)} %get-tuple-element.38, f32[768]{0:T(1024)S(1)} %add_sqrt_fusion.2, f32[768,1024]{1,0:T(8,128)S(1)} %get-tuple-element.26), kind=kOutput, calls=%fused_computation.57 | convolution fusion | flops 1212678144 | bytes 10622976 | tf_op jit(solution)/shard_map/dot_general | solution.py:84
  103.4 1.9 fusion.23
  105.2 2.0 bitcast_add_fusion
  108.2 3.5 %copy.20 = f32[2,4,4,2,24,1024]{5,4,1,0,2,3:T(8,128)} copy(f32[2,4,4,2,24,1024]{5,4,3,2,1,0:T(8,128)S(1)} %pad_maximum_fusion) | data formatting | bytes 12582912 | tf_op jit(solution)/shard_map/stack | solution.py:91
  111.8 16.1 %reduce-scatter.3.cloned.1.call-done = f32[2,4,4,1,24,1024]{5,4,1,0,2,3:T(8,128)} async-done(((f32[2,4,4,2,24,1024]{5,4,1,0,2,3:T(8,128)}), f32[2,4,4,1,24,1024]{5,4,1,0,2,3:T(8,128)}) %reduce-scatter.3.cloned.1.call-update) | async-done | bytes 3145744 | tf_op jit(solution)/shard_map/reduce_scatter | solution.py:97
  128.6 19.0 %all_to_all.17 = f32[128,1,1]{2,1,0:T(1,128)S(1)} all-to-all(f32[128,1,1]{2,1,0:T(1,128)S(1)} %broadcast_in_dim.13), channel_id=1, replica_groups=mesh['y'=4,'x'=4,'core'=2,'blk'=4] {'y','x','core','blk'}, dimensions={0} | all-to-all | bytes 1024 | tf_op jit(solution)/shard_map/all_to_all | solution.py:39
  148.9 4.9 %all-to-all-start = ((f32[128,1,1]{2,1,0:T(1,128)}), f32[128,1,1]{2,1,0:T(1,128)S(1)}, u32[]{:S(2)}, u32[]{:S(2)}) async-start(f32[128,1,1]{2,1,0:T(1,128)} %broadcast_in_dim.12), calls=%async_computation | async-start | bytes 131072 | tf_op jit(solution)/shard_map/all_to_all | solution.py:39
  153.8 17.0 %reduce-scatter.5.cloned.1.call-done = f32[2,4,1,24,1024]{4,3,1,0,2:T(8,128)} async-done(((f32[2,4,4,24,1024]{4,3,1,0,2:T(8,128)}), f32[2,4,1,24,1024]{4,3,1,0,2:T(8,128)}) %reduce-scatter.5.cloned.1.call-update) | async-done | bytes 786448 | tf_op jit(solution)/shard_map/reduce_scatter | solution.py:98
  170.8 1.6 reshape_reduce_scatter.3
  173.4 7.0 %all-to-all-start.2 = ((f32[16,2,24,256]{3,2,1,0:T(8,128)}), f32[16,2,24,256]{3,2,1,0:T(8,128)S(1)}, u32[]{:S(2)}, u32[]{:S(2)}) async-start(f32[16,2,24,256]{3,2,1,0:T(8,128)} %bitcast.8), calls=%async_computation.4 | async-start | bytes 1572864 | tf_op jit(solution)/shard_map/all_to_all | solution.py:102
  183.2 11.7 %all-to-all-done.2 = f32[16,2,24,256]{3,2,1,0:T(8,128)S(1)} async-done(((f32[16,2,24,256]{3,2,1,0:T(8,128)}), f32[16,2,24,256]{3,2,1,0:T(8,128)S(1)}, u32[]{:S(2)}, u32[]{:S(2)}) %all-to-all-start.2) | async-done | bytes 786464 | tf_op jit(solution)/shard_map/all_to_all | solution.py:102
  (51 shorter events, 14.4 us)
Async XLA Ops:
  7.2 9.6 %copy-start = (bf16[768,1024]{1,0:T(8,128)(2,1)S(1)}, bf16[768,1024]{1,0:T(8,128)(2,1)}, u32[]{:S(2)}) copy-start(bf16[768,1024]{1,0:T(8,128)(2,1)} %param.11) | copy-start | bytes 4718596
  7.2 120.7 %reduce-scatter.3.cloned.1.call-start = ((), (), s32[]{:S(2)}) async-start(), calls=%async_computation.5 | async-start | bytes 9437184 | tf_op jit(solution)/shard_map/reduce_scatter | solution.py:97
  7.2 29.7 %collective-permute-start = (bf16[768,768]{1,0:T(8,128)(2,1)}, bf16[768,768]{1,0:T(8,128)(2,1)}, u32[]{:S(2)}, u32[]{:S(2)}) collective-permute-start(bf16[768,768]{1,0:T(8,128)(2,1)} %bitcast.54), channel_id=1, source_target_pairs={{0,3},{1,0},{2,1},{3,2},{4,7},{5,4},{6,5},{7,6},{8,11},{9,8},{10,9... | collective-permute-start | bytes 3538952 | tf_op jit(solution)/shard_map/ppermute | solution.py:50
  11.4 30.4 %collective-permute-start.1 = (bf16[768,768]{1,0:T(8,128)(2,1)}, bf16[768,768]{1,0:T(8,128)(2,1)S(1)}, u32[]{:S(2)}, u32[]{:S(2)}) collective-permute-start(bf16[768,768]{1,0:T(8,128)(2,1)} %bitcast.55), channel_id=1, source_target_pairs={{0,1},{1,2},{2,3},{3,0},{4,5},{5,6},{6,7},{7,4},{8,9},{9,10},{10,1... | collective-permute-start | bytes 3538952 | tf_op jit(solution)/shard_map/ppermute | solution.py:51
  13.4 3.3 %copy-start.3 = (bf16[1,768,768]{2,1,0:T(8,128)(2,1)S(1)}, bf16[1,768,768]{2,1,0:T(8,128)(2,1)}, u32[]{:S(2)}) copy-start(bf16[1,768,768]{2,1,0:T(8,128)(2,1)} %param.7) | copy-start | bytes 3538948
  38.1 19.2 %collective-permute-start.3 = (bf16[384,768]{1,0:T(8,128)(2,1)S(1)}, bf16[384,768]{1,0:T(8,128)(2,1)S(1)}, u32[]{:S(2)}, u32[]{:S(2)}) collective-permute-start(bf16[384,768]{1,0:T(8,128)(2,1)S(1)} %slice.17), channel_id=1, source_target_pairs={{0,3},{1,0},{2,1},{3,2},{4,7},{5,4},{6,5},{7,6},{8,11},{9,8},{10,9... | collective-permute-start | bytes 1769480 | tf_op jit(solution)/shard_map/ppermute | solution.py:54
  41.9 15.4 %collective-permute-start.2 = (bf16[384,768]{1,0:T(8,128)(2,1)S(1)}, bf16[384,768]{1,0:T(8,128)(2,1)S(1)}, u32[]{:S(2)}, u32[]{:S(2)}) collective-permute-start(bf16[384,768]{1,0:T(8,128)(2,1)S(1)} %slice.16), channel_id=1, source_target_pairs={{0,1},{1,2},{2,3},{3,0},{4,5},{5,6},{6,7},{7,4},{8,9},{9,10},{10,1... | collective-permute-start | bytes 1769480 | tf_op jit(solution)/shard_map/ppermute | solution.py:53
  87.9 6.3 %copy-start.2 = (bf16[1,768,768]{2,1,0:T(8,128)(2,1)S(1)}, bf16[1,768,768]{2,1,0:T(8,128)(2,1)}, u32[]{:S(2)}) copy-start(bf16[1,768,768]{2,1,0:T(8,128)(2,1)} %param.6) | copy-start | bytes 3538948
  94.3 3.8 %copy-start.7 = (f32[768,1024]{1,0:T(8,128)S(1)}, f32[768,1024]{1,0:T(8,128)}, u32[]{:S(2)}) copy-start(f32[768,1024]{1,0:T(8,128)} %get-tuple-element.37) | copy-start | bytes 9437188
  98.1 1.9 copy-start.6
  100.0 3.3 %copy-start.5 = (f32[768,1024]{1,0:T(8,128)S(1)}, f32[768,1024]{1,0:T(8,128)}, u32[]{:S(2)}) copy-start(f32[768,1024]{1,0:T(8,128)} %get-tuple-element.35) | copy-start | bytes 9437188
  103.3 1.9 copy-start.4
  111.7 59.1 %reduce-scatter.5.cloned.1.call-start = ((), (), s32[]{:S(2)}) async-start(), calls=%async_computation.6 | async-start | bytes 3932160 | tf_op jit(solution)/shard_map/reduce_scatter | solution.py:98
  148.9 24.5 %all-to-all-start = ((f32[128,1,1]{2,1,0:T(1,128)}), f32[128,1,1]{2,1,0:T(1,128)S(1)}, u32[]{:S(2)}, u32[]{:S(2)}) async-start(f32[128,1,1]{2,1,0:T(1,128)} %broadcast_in_dim.12), calls=%async_computation | async-start | bytes 131072 | tf_op jit(solution)/shard_map/all_to_all | solution.py:39
  170.8 25.4 %copy-start.1 = (bf16[768,1024]{1,0:T(8,128)(2,1)S(1)}, bf16[768,1024]{1,0:T(8,128)(2,1)}, u32[]{:S(2)}) copy-start(bf16[768,1024]{1,0:T(8,128)(2,1)} %param.11) | copy-start | bytes 4718596
  173.4 21.5 %all-to-all-start.2 = ((f32[16,2,24,256]{3,2,1,0:T(8,128)}), f32[16,2,24,256]{3,2,1,0:T(8,128)S(1)}, u32[]{:S(2)}, u32[]{:S(2)}) async-start(f32[16,2,24,256]{3,2,1,0:T(8,128)} %bitcast.8), calls=%async_computation.4 | async-start | bytes 1572864 | tf_op jit(solution)/shard_map/all_to_all | solution.py:102
Sparse Core Ops, SparseCore 0:
  111.8 16.0 reduce-scatter.2
  130.4 40.2 reduce-scatter.4

commit v8 on v7

--- a/solution.py
+++ b/solution.py
@@ -30,13 +30,13 @@
     return ((gradient - unit_vec * projected) / radius).astype(jnp.bfloat16)
 
 
-def gathered_sum(value):
+def gathered_sum(values):
     axes = ("y", "x", "core", "blk")
     count = 1
     for axis in axes:
         count *= lax.axis_size(axis)
-    spread = jnp.broadcast_to(value.reshape(1, 1), (count, 1))
-    return jnp.sum(lax.all_to_all(spread, axes, 0, 0, tiled=True))
+    spread = jnp.broadcast_to(values.reshape((1,) + values.shape), (count,) + values.shape)
+    return jnp.sum(lax.all_to_all(spread, axes, 0, 0, tiled=True), axis=0)
 
 
 def per_device(prod_feat, prec_feat, matched, row_weight, proj_prod, proj_prec):
@@ -68,8 +68,7 @@
     losses = LOGIT_SCALE + jnp.log(totals) - positive
     loss_local = jnp.sum(weights * losses)
     weight_local = jnp.sum(weights)
-    loss_sum = gathered_sum(loss_local)
-    weight_total = gathered_sum(weight_local)
+    loss_sum, weight_total = gathered_sum(jnp.stack([loss_local, weight_local]))
     grad_unit_prod = 0.0
     head_prec = 0.0
     for block, (unit_prec, unit16_prec, radius_prec), block_scores, block_matches in zip(

time: 205 us -> 205 us (level)
  blocking collectives: 19 us -> 0 us
  waiting for transfers between devices: 71 us -> 85.3 us
  starting transfers between devices: 20.1 us -> 25.6 us
    all_to_all x1 -> x0, blocking collectives: 19 us -> none  [gathered_sum(): return jnp.sum(lax.all_to_all(spread, axes, 0, 0, tiled=True))]
    reduce_scatter x1, waiting for transfers between devices: 17 us -> 30.2 us  [per_device(): heads = lax.psum_scatter(heads, 'x', scatter_dimension=2, tiled=False)]
    all_to_all x1, starting transfers between devices: 4.87 us -> 10.1 us  [gathered_sum(): return jnp.sum(lax.all_to_all(spread, axes, 0, 0, tiled=True), axis=0)]
    reduce_sum x3 -> x1, other arithmetic: 2.77 us -> 0.15 us  [gathered_sum(): return jnp.sum(lax.all_to_all(spread, axes, 0, 0, tiled=True), axis=0)]
  transfers between devices with their start and end apart: 8 -> 8, of which waited for: 5 -> 5; matrix products, arithmetic and copies ran while one was open for 11% -> 10% of each run, Pallas kernels for 0% -> 0%
where the time goes in v8:
time: 205 us; the launch traced here: 204 us
  waiting for transfers between devices  85.3 us (42%)
  matrix products  61.1 us (30%)
  starting transfers between devices  25.6 us (12%)
  between operations  16.8 us (8%)
  local copies, waits for them, and re-layouts  9.22 us (4%)
  other arithmetic  6.28 us (3%)
    reduce_scatter x1, waiting for transfers between devices, per_device(): heads = lax.psum_scatter(heads, 'x', scatter_dimension=2, tiled=False)  30.2 us
    ppermute x1, waiting for transfers between devices, per_device(): lax.ppermute(feat_prec, 'blk', [(i, (i - 1) % blk_size) for i in range(bl...  16.7 us
    dot_general x4, matrix products, per_device(): jnp.dot(coeffs, unit16_prec, preferred_element_type=jnp.float32)  16.6 us
    reduce_scatter x1, waiting for transfers between devices, per_device(): heads = lax.psum_scatter(heads, 'core', scatter_dimension=3, tiled=False)  16.1 us
    dot_general x4, matrix products, per_device(): lax.dot_general(coeffs, unit16_prod, (((0,), (0,)), ((), ())), preferred_...  13.5 us
    all_to_all x1, waiting for transfers between devices, per_device(): heads = lax.all_to_all(heads, ('y', 'blk'), 0, 0, tiled=True)  12.7 us
    dot_general x5, matrix products, embed_rows(): jnp.dot(features, weight, preferred_element_type=jnp.float32)  10.5 us
    all_to_all x1, starting transfers between devices, gathered_sum(): return jnp.sum(lax.all_to_all(spread, axes, 0, 0, tiled=True), axis=0)  10.1 us
  transfers between devices with their start and end apart: 8, of which 5 were waited for; matrix products, arithmetic and copies ran while one was open for 10% of the time, Pallas kernels for 0%

profile of v8, /device:TPU:0, one launch (start us, length us, event | category | flops | bytes accessed | tf_op | source)
XLA Modules:
  0.0 204.2 jit_solution(16086412592483986836)
XLA Ops:
  7.2 4.2 %collective-permute-start = (bf16[768,768]{1,0:T(8,128)(2,1)}, bf16[768,768]{1,0:T(8,128)(2,1)}, u32[]{:S(2)}, u32[]{:S(2)}) collective-permute-start(bf16[768,768]{1,0:T(8,128)(2,1)} %bitcast.58), channel_id=1, source_target_pairs={{0,3},{1,0},{2,1},{3,2},{4,7},{5,4},{6,5},{7,6},{8,11},{9,8},{10,9... | collective-permute-start | bytes 3538952 | tf_op jit(solution)/shard_map/ppermute | solution.py:50
  13.4 3.3 %multiply_reduce_fusion.9 = (f32[768]{0:T(1024)S(1)}, f32[768,1024]{1,0:T(8,128)S(1)}) fusion(bf16[768,1024]{1,0:T(8,128)(2,1)} %param.10, bf16[1,768,768]{2,1,0:T(8,128)(2,1)} %param.6), kind=kOutput, calls=%fused_computation.17 | convolution fusion | flops 1209531648 | bytes 5901312 | tf_op jit(solution)/shard_map/dot_general | solution.py:11
  16.8 1.5 multiply_reduce_fusion.8
  18.7 1.5 fusion.41
  20.2 16.7 %collective-permute-done = bf16[768,768]{1,0:T(8,128)(2,1)} collective-permute-done((bf16[768,768]{1,0:T(8,128)(2,1)}, bf16[768,768]{1,0:T(8,128)(2,1)}, u32[]{:S(2)}, u32[]{:S(2)}) %collective-permute-start) | collective-permute-done | bytes 1179680 | tf_op jit(solution)/shard_map/ppermute | solution.py:50
  38.1 3.8 %collective-permute-start.3 = (bf16[384,768]{1,0:T(8,128)(2,1)S(1)}, bf16[384,768]{1,0:T(8,128)(2,1)S(1)}, u32[]{:S(2)}, u32[]{:S(2)}) collective-permute-start(bf16[384,768]{1,0:T(8,128)(2,1)S(1)} %slice.17), channel_id=1, source_target_pairs={{0,3},{1,0},{2,1},{3,2},{4,7},{5,4},{6,5},{7,6},{8,11},{9,8},{10,9... | collective-permute-start | bytes 1769480 | tf_op jit(solution)/shard_map/ppermute | solution.py:54
  43.6 2.7 %multiply_reduce_fusion.7 = (f32[768]{0:T(1024)S(1)}, f32[768,1024]{1,0:T(8,128)S(1)}) fusion(bf16[768,768]{1,0:T(8,128)(2,1)} %collective-permute-done, bf16[768,1024]{1,0:T(8,128)(2,1)S(1)} %copy-done), kind=kOutput, calls=%fused_computation.15 | convolution fusion | flops 1209531648 | bytes 5901312 | tf_op jit(solution)/shard_map/dot_general | solution.py:11
  46.4 1.5 fusion.33
  47.9 9.4 %collective-permute-done.2 = bf16[384,768]{1,0:T(8,128)(2,1)S(1)} collective-permute-done((bf16[384,768]{1,0:T(8,128)(2,1)S(1)}, bf16[384,768]{1,0:T(8,128)(2,1)S(1)}, u32[]{:S(2)}, u32[]{:S(2)}) %collective-permute-start.2) | collective-permute-done | bytes 589856 | tf_op jit(solution)/shard_map/ppermute | solution.py:53
  57.4 1.5 multiply_reduce_fusion.5
  58.8 1.5 fusion.29
  60.3 3.2 %fusion.17 = (f32[768]{0:T(1024)S(1)}, f32[768]{0:T(1024)S(1)}, f32[768]{0:T(1024)S(1)}, f32[768]{0:T(1024)S(1)}, f32[768]{0:T(1024)S(1)}, /*index=5*/f32[768]{0...) fusion(s32[768]{0:T(1024)S(1)} %get-tuple-element.48, s32[768]{0:T(1024)S(1)} %reduce.3, ...), kind=kOutput, calls=%fused_computation.47 | convolution fusion | flops 1223682048 | bytes 14198784 | tf_op jit(solution)/shard_map/dot_general | solution.py:18
  64.2 3.4 %fusion.35 = f32[768,1024]{1,0:T(8,128)} fusion(f32[768,768]{0,1:T(8,128)S(1)} %get-tuple-element.35, f32[768]{0:T(1024)S(1)} %get-tuple-element.14, f32[768]{0:T(1024)S(1)} %get-tuple-element.11, s32[768]{0:T(1024)S(1)} %reduce.3, s32[768]{0:T(1024)S(1)} %get-tuple-element.48, f32[768,1024]{1,0:T(8,128)S(1)} %get-tuple-element.28, f32[768]{0:T(1024)S(1)} %add_sqrt_fusion.2), kind=kOutput, calls=%fused_computation.70 | convolution fusion | flops 1214251008 | bytes 8666112 | tf_op jit(solution)/shard_map/dot_general | solution.py:78
  67.5 3.4 %multiply_reduce_fusion.2 = (f32[768]{0:T(1024)S(1)}, f32[768,1024]{1,0:T(8,128)}) fusion(f32[768,1024]{1,0:T(8,128)S(1)} %get-tuple-element.28, f32[768]{0:T(1024)S(1)} %add_sqrt_fusion.2, bf16[768,1024]{1,0:T(8,128)(2,1)S(1)} %fusion.50, f32[768,768]{0,1:T(8,128)S(1)} %get-tuple-element.35, f32[768]{0:T(1024)S(1)} %get-tuple-element.14, ...), kind=kOutput, calls=%fused_computation.7 | convolution fusion | flops 1215823104 | bytes 10242048 | tf_op jit(solution)/shard_map/dot_general | solution.py:79
  70.9 3.4 %fusion.31 = f32[768,1024]{1,0:T(8,128)} fusion(f32[768,768]{0,1:T(8,128)S(1)} %fusion.33, f32[768]{0:T(1024)S(1)} %get-tuple-element.14, f32[768]{0:T(1024)S(1)} %get-tuple-element.11, s32[768]{0:T(1024)S(1)} %reduce.3, s32[768]{0:T(1024)S(1)} %get-tuple-element.47, f32[768,1024]{1,0:T(8,128)S(1)} %get-tuple-element.30, f32[768]{0:T(1024)S(1)} %add_sqrt_fusion.1), kind=kOutput, calls=%fused_computation.66 | convolution fusion | flops 1214251008 | bytes 8666112 | tf_op jit(solution)/shard_map/dot_general | solution.py:78
  74.4 3.4 %multiply_reduce_fusion.1 = (f32[768]{0:T(1024)S(1)}, f32[768,1024]{1,0:T(8,128)}) fusion(f32[768,1024]{1,0:T(8,128)S(1)} %get-tuple-element.30, f32[768]{0:T(1024)S(1)} %add_sqrt_fusion.1, bf16[768,1024]{1,0:T(8,128)(2,1)S(1)} %fusion.50, f32[768,768]{0,1:T(8,128)S(1)} %fusion.33, f32[768]{0:T(1024)S(1)} %get-tuple-element.14, ...), kind=kOutput, calls=%fused_computation.5 | convolution fusion | flops 1215823104 | bytes 10242048 | tf_op jit(solution)/shard_map/dot_general | solution.py:79
  77.7 3.4 %fusion.39 = f32[768,1024]{1,0:T(8,128)} fusion(f32[768,768]{0,1:T(8,128)S(1)} %fusion.41, f32[768]{0:T(1024)S(1)} %get-tuple-element.14, f32[768]{0:T(1024)S(1)} %get-tuple-element.11, s32[768]{0:T(1024)S(1)} %reduce.3, s32[768]{0:T(1024)S(1)} %get-tuple-element.49, f32[768,1024]{1,0:T(8,128)S(1)} %get-tuple-element.34, f32[768]{0:T(1024)S(1)} %add_sqrt_fusion.3), kind=kOutput, calls=%fused_computation.74 | convolution fusion | flops 1214251008 | bytes 8666112 | tf_op jit(solution)/shard_map/dot_general | solution.py:78
  81.1 3.4 %multiply_reduce_fusion = (f32[768]{0:T(1024)S(1)}, f32[768,1024]{1,0:T(8,128)}) fusion(f32[768,1024]{1,0:T(8,128)S(1)} %get-tuple-element.32, f32[768]{0:T(1024)S(1)} %add_sqrt_fusion, bf16[768,1024]{1,0:T(8,128)(2,1)S(1)} %fusion.50, f32[768,768]{0,1:T(8,128)S(1)} %fusion.29, f32[768]{0:T(1024)S(1)} %get-tuple-element.14, f32[768]{0:T(1024)S(1)} %get-tuple-element.11, ...), kind=kOutput, calls=%fused_computation.3 | convolution fusion | flops 1215823104 | bytes 10242048 | tf_op jit(solution)/shard_map/dot_general | solution.py:79
  84.6 3.3 %multiply_reduce_fusion.3 = (f32[768]{0:T(1024)S(1)}, f32[768,1024]{1,0:T(8,128)}) fusion(f32[768,1024]{1,0:T(8,128)S(1)} %get-tuple-element.34, f32[768]{0:T(1024)S(1)} %add_sqrt_fusion.3, bf16[768,1024]{1,0:T(8,128)(2,1)S(1)} %fusion.50, f32[768,768]{0,1:T(8,128)S(1)} %fusion.41, f32[768]{0:T(1024)S(1)} %get-tuple-element.14, ...), kind=kOutput, calls=%fused_computation.9 | convolution fusion | flops 1215823104 | bytes 10242048 | tf_op jit(solution)/shard_map/dot_general | solution.py:79
  87.9 6.3 %multiply_reduce_fusion.4 = (f32[768]{0:T(1024)S(1)}, f32[768,1024]{1,0:T(8,128)}) fusion(f32[768,1024]{1,0:T(8,128)S(1)} %get-tuple-element.26, f32[768]{0:T(1024)S(1)} %add_sqrt_fusion.4, f32[768,1024]{1,0:T(8,128)S(1)} %get-tuple-element.32, f32[768]{0:T(1024)S(1)} %add_sqrt_fusion, f32[768,768]{0,1:T(8,128)S(1)} %fusion.29, ...), kind=kOutput, calls=%fused_computation.11 | convolution fusion | flops 1219755264 | bytes 21255168 | tf_op jit(solution)/shard_map/dot_general | solution.py:78
  94.3 3.8 %fusion.20 = f32[1024,768]{0,1:T(8,128)S(1)} fusion(f32[768,1024]{1,0:T(8,128)} %get-tuple-element.45, f32[768]{0:T(1024)S(1)} %get-tuple-element.44, f32[768]{0:T(1024)S(1)} %add_sqrt_fusion.4, bf16[1,768,768]{2,1,0:T(8,128)(2,1)S(1)} %copy-done.2, f32[768,1024]{1,0:T(8,128)S(1)} %get-tuple-element.26), kind=kOutput, calls=%fused_computation.55 | convolution fusion | flops 1211891712 | bytes 10622976 | tf_op jit(solution)/shard_map/dot_general | solution.py:87
  98.1 1.9 fusion.21
  100.0 3.3 %fusion.22 = f32[1024,768]{0,1:T(8,128)S(1)} fusion(bf16[768,768]{1,0:T(8,128)(2,1)} %collective-permute-done, f32[768,1024]{1,0:T(8,128)S(1)} %copy-done.6, f32[768]{0:T(1024)S(1)} %get-tuple-element.40, f32[768]{0:T(1024)S(1)} %add_sqrt_fusion.2, f32[768,1024]{1,0:T(8,128)S(1)} %get-tuple-element.28), kind=kOutput, calls=%fused_computation.57 | convolution fusion | flops 1212678144 | bytes 10622976 | tf_op jit(solution)/shard_map/dot_general | solution.py:83
  103.4 1.9 fusion.23
  105.2 2.0 bitcast_add_fusion
  108.2 3.5 %copy.19 = f32[2,4,4,2,24,1024]{5,4,1,0,2,3:T(8,128)} copy(f32[2,4,4,2,24,1024]{5,4,3,2,1,0:T(8,128)S(1)} %pad_maximum_fusion) | data formatting | bytes 12582912 | tf_op jit(solution)/shard_map/stack | solution.py:90
  111.8 16.1 %reduce-scatter.3.cloned.1.call-done = f32[2,4,4,1,24,1024]{5,4,1,0,2,3:T(8,128)} async-done(((f32[2,4,4,2,24,1024]{5,4,1,0,2,3:T(8,128)}), f32[2,4,4,1,24,1024]{5,4,1,0,2,3:T(8,128)}) %reduce-scatter.3.cloned.1.call-update) | async-done | bytes 3145744 | tf_op jit(solution)/shard_map/reduce_scatter | solution.py:96
  129.9 10.1 %all-to-all-start = ((f32[128,1,2]{2,1,0:T(1,128)}), f32[128,1,2]{2,1,0:T(1,128)S(1)}, u32[]{:S(2)}, u32[]{:S(2)}) async-start(f32[128,1,2]{2,1,0:T(1,128)} %broadcast_in_dim.9), calls=%async_computation | async-start | bytes 131072 | tf_op jit(solution)/shard_map/all_to_all | solution.py:39
  140.0 30.2 %reduce-scatter.5.cloned.1.call-done = f32[2,4,1,24,1024]{4,3,1,0,2:T(8,128)} async-done(((f32[2,4,4,24,1024]{4,3,1,0,2:T(8,128)}), f32[2,4,1,24,1024]{4,3,1,0,2:T(8,128)}) %reduce-scatter.5.cloned.1.call-update) | async-done | bytes 786448 | tf_op jit(solution)/shard_map/reduce_scatter | solution.py:97
  170.3 1.6 reshape_reduce_scatter.3
  172.9 7.2 %all-to-all-start.1 = ((f32[16,2,24,256]{3,2,1,0:T(8,128)}), f32[16,2,24,256]{3,2,1,0:T(8,128)S(1)}, u32[]{:S(2)}, u32[]{:S(2)}) async-start(f32[16,2,24,256]{3,2,1,0:T(8,128)} %bitcast.12), calls=%async_computation.3 | async-start | bytes 1572864 | tf_op jit(solution)/shard_map/all_to_all | solution.py:101
  182.2 12.7 %all-to-all-done.1 = f32[16,2,24,256]{3,2,1,0:T(8,128)S(1)} async-done(((f32[16,2,24,256]{3,2,1,0:T(8,128)}), f32[16,2,24,256]{3,2,1,0:T(8,128)S(1)}, u32[]{:S(2)}, u32[]{:S(2)}) %all-to-all-start.1) | async-done | bytes 786464 | tf_op jit(solution)/shard_map/all_to_all | solution.py:101
  (50 shorter events, 12.3 us)
Async XLA Ops:
  7.2 9.6 %copy-start = (bf16[768,1024]{1,0:T(8,128)(2,1)S(1)}, bf16[768,1024]{1,0:T(8,128)(2,1)}, u32[]{:S(2)}) copy-start(bf16[768,1024]{1,0:T(8,128)(2,1)} %param.11) | copy-start | bytes 4718596
  7.2 120.7 %reduce-scatter.3.cloned.1.call-start = ((), (), s32[]{:S(2)}) async-start(), calls=%async_computation.4 | async-start | bytes 9437184 | tf_op jit(solution)/shard_map/reduce_scatter | solution.py:96
  7.2 29.7 %collective-permute-start = (bf16[768,768]{1,0:T(8,128)(2,1)}, bf16[768,768]{1,0:T(8,128)(2,1)}, u32[]{:S(2)}, u32[]{:S(2)}) collective-permute-start(bf16[768,768]{1,0:T(8,128)(2,1)} %bitcast.58), channel_id=1, source_target_pairs={{0,3},{1,0},{2,1},{3,2},{4,7},{5,4},{6,5},{7,6},{8,11},{9,8},{10,9... | collective-permute-start | bytes 3538952 | tf_op jit(solution)/shard_map/ppermute | solution.py:50
  11.4 30.4 %collective-permute-start.1 = (bf16[768,768]{1,0:T(8,128)(2,1)}, bf16[768,768]{1,0:T(8,128)(2,1)S(1)}, u32[]{:S(2)}, u32[]{:S(2)}) collective-permute-start(bf16[768,768]{1,0:T(8,128)(2,1)} %bitcast.59), channel_id=1, source_target_pairs={{0,1},{1,2},{2,3},{3,0},{4,5},{5,6},{6,7},{7,4},{8,9},{9,10},{10,1... | collective-permute-start | bytes 3538952 | tf_op jit(solution)/shard_map/ppermute | solution.py:51
  13.4 3.3 %copy-start.3 = (bf16[1,768,768]{2,1,0:T(8,128)(2,1)S(1)}, bf16[1,768,768]{2,1,0:T(8,128)(2,1)}, u32[]{:S(2)}) copy-start(bf16[1,768,768]{2,1,0:T(8,128)(2,1)} %param.7) | copy-start | bytes 3538948
  38.1 19.2 %collective-permute-start.3 = (bf16[384,768]{1,0:T(8,128)(2,1)S(1)}, bf16[384,768]{1,0:T(8,128)(2,1)S(1)}, u32[]{:S(2)}, u32[]{:S(2)}) collective-permute-start(bf16[384,768]{1,0:T(8,128)(2,1)S(1)} %slice.17), channel_id=1, source_target_pairs={{0,3},{1,0},{2,1},{3,2},{4,7},{5,4},{6,5},{7,6},{8,11},{9,8},{10,9... | collective-permute-start | bytes 1769480 | tf_op jit(solution)/shard_map/ppermute | solution.py:54
  41.9 15.4 %collective-permute-start.2 = (bf16[384,768]{1,0:T(8,128)(2,1)S(1)}, bf16[384,768]{1,0:T(8,128)(2,1)S(1)}, u32[]{:S(2)}, u32[]{:S(2)}) collective-permute-start(bf16[384,768]{1,0:T(8,128)(2,1)S(1)} %slice.16), channel_id=1, source_target_pairs={{0,1},{1,2},{2,3},{3,0},{4,5},{5,6},{6,7},{7,4},{8,9},{9,10},{10,1... | collective-permute-start | bytes 1769480 | tf_op jit(solution)/shard_map/ppermute | solution.py:53
  87.9 6.3 %copy-start.2 = (bf16[1,768,768]{2,1,0:T(8,128)(2,1)S(1)}, bf16[1,768,768]{2,1,0:T(8,128)(2,1)}, u32[]{:S(2)}) copy-start(bf16[1,768,768]{2,1,0:T(8,128)(2,1)} %param.6) | copy-start | bytes 3538948
  94.3 3.8 %copy-start.7 = (f32[768,1024]{1,0:T(8,128)S(1)}, f32[768,1024]{1,0:T(8,128)}, u32[]{:S(2)}) copy-start(f32[768,1024]{1,0:T(8,128)} %get-tuple-element.39) | copy-start | bytes 9437188
  98.1 1.9 copy-start.6
  100.0 3.3 %copy-start.5 = (f32[768,1024]{1,0:T(8,128)S(1)}, f32[768,1024]{1,0:T(8,128)}, u32[]{:S(2)}) copy-start(f32[768,1024]{1,0:T(8,128)} %get-tuple-element.37) | copy-start | bytes 9437188
  103.3 1.9 copy-start.4
  111.7 58.6 %reduce-scatter.5.cloned.1.call-start = ((), (), s32[]{:S(2)}) async-start(), calls=%async_computation.5 | async-start | bytes 3932160 | tf_op jit(solution)/shard_map/reduce_scatter | solution.py:97
  129.9 43.0 %all-to-all-start = ((f32[128,1,2]{2,1,0:T(1,128)}), f32[128,1,2]{2,1,0:T(1,128)S(1)}, u32[]{:S(2)}, u32[]{:S(2)}) async-start(f32[128,1,2]{2,1,0:T(1,128)} %broadcast_in_dim.9), calls=%async_computation | async-start | bytes 131072 | tf_op jit(solution)/shard_map/all_to_all | solution.py:39
  170.3 26.0 %copy-start.1 = (bf16[768,1024]{1,0:T(8,128)(2,1)S(1)}, bf16[768,1024]{1,0:T(8,128)(2,1)}, u32[]{:S(2)}) copy-start(bf16[768,1024]{1,0:T(8,128)(2,1)} %param.11) | copy-start | bytes 4718596
  172.9 22.0 %all-to-all-start.1 = ((f32[16,2,24,256]{3,2,1,0:T(8,128)}), f32[16,2,24,256]{3,2,1,0:T(8,128)S(1)}, u32[]{:S(2)}, u32[]{:S(2)}) async-start(f32[16,2,24,256]{3,2,1,0:T(8,128)} %bitcast.12), calls=%async_computation.3 | async-start | bytes 1572864 | tf_op jit(solution)/shard_map/all_to_all | solution.py:101
Sparse Core Ops, SparseCore 0:
  111.8 16.0 reduce-scatter.2
  130.4 39.7 reduce-scatter.4

commit v9 on v8

--- a/solution.py
+++ b/solution.py
@@ -53,13 +53,18 @@
     low_half = lax.ppermute(from_prev[:half], "blk", [(i, (i + 1) % blk_size) for i in range(blk_size)])
     high_half = lax.ppermute(from_next[half:], "blk", [(i, (i - 1) % blk_size) for i in range(blk_size)])
     opposite = jnp.concatenate([low_half, high_half], axis=0)
-    blocks = [feat_prec, from_next, from_prev, opposite]
-    sources = [blk_pos, (blk_pos + 1) % blk_size, (blk_pos - 1) % blk_size, (blk_pos + 2) % blk_size]
+    near = jnp.concatenate([feat_prec, from_next, from_prev], axis=0)
+    blocks = [near, opposite]
+    near_order = jnp.stack([blk_pos, (blk_pos + 1) % blk_size, (blk_pos - 1) % blk_size])
+    sources = [near_order, ((blk_pos + 2) % blk_size).reshape(1)]
     unit_prod, unit16_prod, radius_prod = embed_rows(feat_prod, proj_prod)
     embedded = [embed_rows(block, proj_prec) for block in blocks]
     scores = [similarity(unit16_prod, unit16) for (_, unit16, _) in embedded]
     local_columns = lax.iota(jnp.int32, row_count)
-    matches = [targets[:, None] == (source * row_count + local_columns)[None, :] for source in sources]
+    matches = [
+        targets[:, None] == (source[:, None] * row_count + local_columns[None, :]).reshape(1, -1)
+        for source in sources
+    ]
     totals = sum(jnp.sum(jnp.exp(block_scores - LOGIT_SCALE), axis=1) for block_scores in scores)
     positive = sum(
         jnp.sum(jnp.where(block_matches, block_scores, 0.0), axis=1)

time: 205 us -> 199 us (0.971)
  waiting for transfers between devices: 85.3 us -> 79.3 us
  other arithmetic: 6.28 us -> 8.85 us
    ppermute x1, waiting for transfers between devices: 0.01 us -> 20.2 us  [per_device(): lax.ppermute(feat_prec, 'blk', [(i, (i + 1) % blk_size) for i in range(bl...]
    ppermute x1, waiting for transfers between devices: 16.7 us -> 0.01 us  [per_device(): lax.ppermute(feat_prec, 'blk', [(i, (i - 1) % blk_size) for i in range(bl...]
    ppermute x1, waiting for transfers between devices: 9.38 us -> 0.01 us  [per_device(): lax.ppermute(from_prev[:half], 'blk', [(i, (i + 1) % blk_size) for i in r...]
    dot_general x4 -> x2, matrix products: 16.6 us -> 8.77 us  [per_device(): jnp.dot(coeffs, unit16_prec, preferred_element_type=jnp.float32)]
    dot_general x4 -> x2, matrix products: 9.04 us -> 15 us  [per_device(): lax.dot_general(block, dir_prec, (((0,), (0,)), ((), ())), preferred_elem...]
    dot_general x5 -> x3, matrix products: 10.5 us -> 13.5 us  [embed_rows(): jnp.dot(features, weight, preferred_element_type=jnp.float32)]
    convert_element_type x0 -> x1, other arithmetic: none -> 2.7 us  [coefficient(): (weights[:, None] * (probability - matches.astype(jnp.float32))).astype(j...]
    dot_general x4 -> x2, matrix products: 13.5 us -> 11 us  [per_device(): lax.dot_general(coeffs, unit16_prod, (((0,), (0,)), ((), ())), preferred_...]
  transfers between devices with their start and end apart: 8 -> 8, of which waited for: 5 -> 4; matrix products, arithmetic and copies ran while one was open for 10% -> 15% of each run, Pallas kernels for 0% -> 0%
where the time goes in v9:
time: 199 us
  waiting for transfers between devices  79.3 us (40%)
  matrix products  59.7 us (30%)
  starting transfers between devices  25 us (13%)
  between operations  16.7 us (8%)
  local copies, waits for them, and re-layouts  8.86 us (4%)
  other arithmetic  8.85 us (4%)
    reduce_scatter x1, waiting for transfers between devices, per_device(): heads = lax.psum_scatter(heads, 'x', scatter_dimension=2, tiled=False)  30.2 us
    ppermute x1, waiting for transfers between devices, per_device(): lax.ppermute(feat_prec, 'blk', [(i, (i + 1) % blk_size) for i in range(bl...  20.2 us
    reduce_scatter x1, waiting for transfers between devices, per_device(): heads = lax.psum_scatter(heads, 'core', scatter_dimension=3, tiled=False)  16.1 us
    dot_general x2, matrix products, per_device(): lax.dot_general(block, dir_prec, (((0,), (0,)), ((), ())), preferred_elem...  15 us
    dot_general x3, matrix products, embed_rows(): jnp.dot(features, weight, preferred_element_type=jnp.float32)  13.5 us
    all_to_all x1, waiting for transfers between devices, per_device(): heads = lax.all_to_all(heads, ('y', 'blk'), 0, 0, tiled=True)  12.7 us
    dot_general x2, matrix products, per_device(): lax.dot_general(coeffs, unit16_prod, (((0,), (0,)), ((), ())), preferred_...  11 us
    all_to_all x1, starting transfers between devices, gathered_sum(): return jnp.sum(lax.all_to_all(spread, axes, 0, 0, tiled=True), axis=0)  10.1 us
  transfers between devices with their start and end apart: 8, of which 4 were waited for; matrix products, arithmetic and copies ran while one was open for 15% of the time, Pallas kernels for 0%

profile of v9, /device:TPU:0, one launch (start us, length us, event | category | flops | bytes accessed | tf_op | source)
XLA Modules:
  0.0 198.5 jit_solution(15668455144524704192)
XLA Ops:
  7.2 2.1 %collective-permute-start.1 = (bf16[768,768]{1,0:T(8,128)(2,1)}, bf16[768,768]{1,0:T(8,128)(2,1)S(1)}, u32[]{:S(2)}, u32[]{:S(2)}) collective-permute-start(bf16[768,768]{1,0:T(8,128)(2,1)} %bitcast.45), channel_id=1, source_target_pairs={{0,1},{1,2},{2,3},{3,0},{4,5},{5,6},{6,7},{7,4},{8,9},{9,10},{10,1... | collective-permute-start | bytes 3538952 | tf_op jit(solution)/shard_map/ppermute | solution.py:51
  9.3 2.2 %collective-permute-start = (bf16[768,768]{1,0:T(8,128)(2,1)}, bf16[768,768]{1,0:T(8,128)(2,1)}, u32[]{:S(2)}, u32[]{:S(2)}) collective-permute-start(bf16[768,768]{1,0:T(8,128)(2,1)} %bitcast.46), channel_id=1, source_target_pairs={{0,3},{1,0},{2,1},{3,2},{4,7},{5,4},{6,5},{7,6},{8,11},{9,8},{10,9... | collective-permute-start | bytes 3538952 | tf_op jit(solution)/shard_map/ppermute | solution.py:50
  11.7 0.7 reduce.3
  12.4 1.3 fusion.33
  13.7 3.2 %multiply_reduce_fusion.5 = (f32[768]{0:T(1024)S(1)}, f32[768,1024]{1,0:T(8,128)S(1)}) fusion(bf16[768,1024]{1,0:T(8,128)(2,1)} %param.10, bf16[1,768,768]{2,1,0:T(8,128)(2,1)} %param.6), kind=kOutput, calls=%fused_computation.21 | convolution fusion | flops 1209531648 | bytes 5901312 | tf_op jit(solution)/shard_map/dot_general | solution.py:11
  17.4 20.2 %collective-permute-done.1 = bf16[768,768]{1,0:T(8,128)(2,1)S(1)} collective-permute-done((bf16[768,768]{1,0:T(8,128)(2,1)}, bf16[768,768]{1,0:T(8,128)(2,1)S(1)}, u32[]{:S(2)}, u32[]{:S(2)}) %collective-permute-start.1) | collective-permute-done | bytes 1179680 | tf_op jit(solution)/shard_map/ppermute | solution.py:51
  37.7 1.1 slice.17
  38.8 3.3 %collective-permute-start.3 = (bf16[384,768]{1,0:T(8,128)(2,1)S(1)}, bf16[384,768]{1,0:T(8,128)(2,1)S(1)}, u32[]{:S(2)}, u32[]{:S(2)}) collective-permute-start(bf16[384,768]{1,0:T(8,128)(2,1)S(1)} %slice.17), channel_id=1, source_target_pairs={{0,3},{1,0},{2,1},{3,2},{4,7},{5,4},{6,5},{7,6},{8,11},{9,8},{10,9... | collective-permute-start | bytes 1769480 | tf_op jit(solution)/shard_map/ppermute | solution.py:54
  42.1 8.8 %multiply_reduce_fusion.1 = (f32[2304]{0:T(1024)S(1)}, f32[2304,1024]{0,1:T(8,128)}) fusion(bf16[768,1024]{1,0:T(8,128)(2,1)S(1)} %copy-done, bf16[768,768]{1,0:T(8,128)(2,1)S(1)} %collective-permute-done.1, bf16[768,768]{1,0:T(8,128)(2,1)} %collective-permute-done, bf16[768,768]{1,0:T(8,128)(2,1)S(1)} %bitcast.47), kind=kOutput, calls=%fused_computation.2 | convolution fusion | flops 3639211776 | bytes 14558208 | tf_op jit(solution)/shard_map/dot_general | solution.py:11
  50.9 7.9 %fusion.4 = (f32[768]{0:T(1024)S(1)}, f32[768]{0:T(1024)S(1)}, f32[768,2304]{1,0:T(8,128)S(1)}) fusion(s32[2304]{0:T(1024)S(1)} %add.118, s32[768]{0:T(1024)S(1)} %reduce.3, bf16[768,1024]{1,0:T(8,128)(2,1)S(1)} %fusion.29, f32[2304,1024]{0,1:T(8,128)} %get-tuple-element.18, f32[2304]{0:T(1024)S(1)} %add_sqrt_fusion), kind=kOutput, calls=%fused_computation.11 | convolution fusion | flops 3639212544 | bytes 18115584 | tf_op jit(solution)/shard_map/dot_general | solution.py:18
  58.9 1.5 multiply_reduce_fusion.4
  60.4 1.8 fusion.14
  62.8 2.7 %fusion.3 = bf16[768,2304]{1,0:T(8,128)(2,1)S(1)} fusion(f32[768,2304]{1,0:T(8,128)S(1)} %get-tuple-element.19, f32[768]{0:T(1024)S(1)} %get-tuple-element.10, f32[768]{0:T(1024)S(1)} %get-tuple-element.7, s32[2304]{0:T(1024)S(1)} %add.118, s32[768]{0:T(1024)S(1)} %reduce.3), kind=kLoop, calls=%fused_computation.8 | loop fusion | flops 14155776 | bytes 10635264 | tf_op jit(solution)/shard_map/convert_element_type | solution.py:25
  65.5 6.4 %fusion.10 = f32[768,1024]{1,0:T(8,128)S(1)} fusion(bf16[768,2304]{1,0:T(8,128)(2,1)S(1)} %fusion.3, f32[2304,1024]{0,1:T(8,128)} %get-tuple-element.18, f32[2304]{0:T(1024)S(1)} %add_sqrt_fusion), kind=kOutput, calls=%fused_computation.29 | convolution fusion | flops 3628597248 | bytes 16131072 | tf_op jit(solution)/shard_map/dot_general | solution.py:83
  72.0 9.2 %multiply_reduce_fusion = (f32[2304]{0:T(1024)S(1)}, f32[2304,1024]{0,1:T(8,128)}) fusion(f32[2304,1024]{0,1:T(8,128)} %get-tuple-element.18, f32[2304]{0:T(1024)S(1)} %add_sqrt_fusion, bf16[768,2304]{1,0:T(8,128)(2,1)S(1)} %fusion.3, bf16[768,1024]{1,0:T(8,128)(2,1)S(1)} %fusion.29), kind=kOutput, calls=%fused_computation.1 | convolution fusion | flops 3633313536 | bytes 24004608 | tf_op jit(solution)/shard_map/dot_general | solution.py:84
  81.2 1.8 multiply_reduce_fusion.2
  83.0 2.3 %multiply_reduce_fusion.3 = (f32[768]{0:T(1024)S(1)}, f32[768,1024]{1,0:T(8,128)S(1)}) fusion(f32[768,1024]{1,0:T(8,128)S(1)} %get-tuple-element.16, f32[768]{0:T(1024)S(1)} %add_sqrt_fusion.2, f32[768,1024]{1,0:T(8,128)S(1)} %fusion.10, f32[768,1024]{1,0:T(8,128)S(1)} %get-tuple-element.21, f32[768]{0:T(1024)S(1)} %add_sqrt_fusion.1, ...), kind=kOutput, calls=%fused_computation.18 | convolution fusion | flops 1218182400 | bytes 14963712 | tf_op jit(solution)/shard_map/dot_general | solution.py:83
  85.3 1.8 fusion.16
  87.2 3.4 %fusion.17 = f32[768,1024]{1,0:T(8,128)} fusion(bf16[768,768]{1,0:T(8,128)(2,1)S(1)} %constant_dynamic-update-slice_fusion, f32[768,1024]{1,0:T(8,128)S(1)} %get-tuple-element.24, f32[768]{0:T(1024)S(1)} %get-tuple-element.23, f32[768]{0:T(1024)S(1)} %add_sqrt_fusion.1, f32[768,1024]{1,0:T(8,128)S(1)} %get-tuple-element.21), kind=kOutput, calls=%fused_computation.38 | convolution fusion | flops 1212678144 | bytes 10622976 | tf_op jit(solution)/shard_map/dot_general | solution.py:88
  90.6 11.6 %fusion.15 = f32[768,1024]{1,0:T(8,128)S(1)} fusion(f32[768,1024]{1,0:T(8,128)} %fusion.17, f32[2304,1024]{0,1:T(8,128)} %get-tuple-element.26, f32[2304]{0:T(1024)S(1)} %get-tuple-element.25, f32[2304]{0:T(1024)S(1)} %add_sqrt_fusion, bf16[768,768]{1,0:T(8,128)(2,1)S(1)} %collective-permute-done.1, bf16[768,768]{1,0:T(8,128)(2,1)} %collective-permute-done, ...), kind=kOutput, calls=%fused_computation.34 | convolution fusion | flops 3649437696 | bytes 28723200 | tf_op jit(solution)/shard_map/dot_general | solution.py:88
  102.7 3.2 %copy.19 = f32[2,4,4,2,24,1024]{5,4,1,0,2,3:T(8,128)} copy(f32[2,4,4,2,24,1024]{5,4,3,2,1,0:T(8,128)S(1)} %pad_maximum_fusion) | data formatting | bytes 12582912 | tf_op jit(solution)/shard_map/stack | solution.py:95
  106.1 16.1 %reduce-scatter.3.cloned.1.call-done = f32[2,4,4,1,24,1024]{5,4,1,0,2,3:T(8,128)} async-done(((f32[2,4,4,2,24,1024]{5,4,1,0,2,3:T(8,128)}), f32[2,4,4,1,24,1024]{5,4,1,0,2,3:T(8,128)}) %reduce-scatter.3.cloned.1.call-update) | async-done | bytes 3145744 | tf_op jit(solution)/shard_map/reduce_scatter | solution.py:101
  122.2 1.5 pad_maximum_fusion.4
  123.7 0.7 broadcast_in_dim.12
  124.4 10.1 %all-to-all-start = ((f32[128,1,2]{2,1,0:T(1,128)}), f32[128,1,2]{2,1,0:T(1,128)S(1)}, u32[]{:S(2)}, u32[]{:S(2)}) async-start(f32[128,1,2]{2,1,0:T(1,128)} %broadcast_in_dim.12), calls=%async_computation | async-start | bytes 131072 | tf_op jit(solution)/shard_map/all_to_all | solution.py:39
  134.5 30.2 %reduce-scatter.5.cloned.1.call-done = f32[2,4,1,24,1024]{4,3,1,0,2:T(8,128)} async-done(((f32[2,4,4,24,1024]{4,3,1,0,2:T(8,128)}), f32[2,4,1,24,1024]{4,3,1,0,2:T(8,128)}) %reduce-scatter.5.cloned.1.call-update) | async-done | bytes 786448 | tf_op jit(solution)/shard_map/reduce_scatter | solution.py:102
  164.7 1.5 reshape_reduce_scatter.3
  166.2 1.0 copy.18
  167.2 7.2 %all-to-all-start.1 = ((f32[16,2,24,256]{3,2,1,0:T(8,128)}), f32[16,2,24,256]{3,2,1,0:T(8,128)S(1)}, u32[]{:S(2)}, u32[]{:S(2)}) async-start(f32[16,2,24,256]{3,2,1,0:T(8,128)} %bitcast.14), calls=%async_computation.3 | async-start | bytes 1572864 | tf_op jit(solution)/shard_map/all_to_all | solution.py:106
  176.5 12.7 %all-to-all-done.1 = f32[16,2,24,256]{3,2,1,0:T(8,128)S(1)} async-done(((f32[16,2,24,256]{3,2,1,0:T(8,128)}), f32[16,2,24,256]{3,2,1,0:T(8,128)S(1)}, u32[]{:S(2)}, u32[]{:S(2)}) %all-to-all-start.1) | async-done | bytes 786464 | tf_op jit(solution)/shard_map/all_to_all | solution.py:106
  189.3 0.7 broadcast_divide_fusion.3
  189.9 0.6 slice_bitcast_fusion
  (33 shorter events, 2.9 us)
Async XLA Ops:
  7.2 35.0 %copy-start = (bf16[768,1024]{1,0:T(8,128)(2,1)S(1)}, bf16[768,1024]{1,0:T(8,128)(2,1)}, u32[]{:S(2)}) copy-start(bf16[768,1024]{1,0:T(8,128)(2,1)} %param.11) | copy-start | bytes 4718596
  7.2 115.0 %reduce-scatter.3.cloned.1.call-start = ((), (), s32[]{:S(2)}) async-start(), calls=%async_computation.4 | async-start | bytes 9437184 | tf_op jit(solution)/shard_map/reduce_scatter | solution.py:101
  7.2 30.4 %collective-permute-start.1 = (bf16[768,768]{1,0:T(8,128)(2,1)}, bf16[768,768]{1,0:T(8,128)(2,1)S(1)}, u32[]{:S(2)}, u32[]{:S(2)}) collective-permute-start(bf16[768,768]{1,0:T(8,128)(2,1)} %bitcast.45), channel_id=1, source_target_pairs={{0,1},{1,2},{2,3},{3,0},{4,5},{5,6},{6,7},{7,4},{8,9},{9,10},{10,1... | collective-permute-start | bytes 3538952 | tf_op jit(solution)/shard_map/ppermute | solution.py:51
  9.3 28.4 %collective-permute-start = (bf16[768,768]{1,0:T(8,128)(2,1)}, bf16[768,768]{1,0:T(8,128)(2,1)}, u32[]{:S(2)}, u32[]{:S(2)}) collective-permute-start(bf16[768,768]{1,0:T(8,128)(2,1)} %bitcast.46), channel_id=1, source_target_pairs={{0,3},{1,0},{2,1},{3,2},{4,7},{5,4},{6,5},{7,6},{8,11},{9,8},{10,9... | collective-permute-start | bytes 3538952 | tf_op jit(solution)/shard_map/ppermute | solution.py:50
  16.9 25.2 %copy-start.3 = (bf16[1,768,768]{2,1,0:T(8,128)(2,1)S(1)}, bf16[1,768,768]{2,1,0:T(8,128)(2,1)}, u32[]{:S(2)}) copy-start(bf16[1,768,768]{2,1,0:T(8,128)(2,1)} %param.7) | copy-start | bytes 3538948
  37.6 21.2 %collective-permute-start.2 = (bf16[384,768]{1,0:T(8,128)(2,1)S(1)}, bf16[384,768]{1,0:T(8,128)(2,1)S(1)}, u32[]{:S(2)}, u32[]{:S(2)}) collective-permute-start(bf16[384,768]{1,0:T(8,128)(2,1)S(1)} %slice.16), channel_id=1, source_target_pairs={{0,1},{1,2},{2,3},{3,0},{4,5},{5,6},{6,7},{7,4},{8,9},{9,10},{10,1... | collective-permute-start | bytes 1769480 | tf_op jit(solution)/shard_map/ppermute | solution.py:53
  38.8 20.0 %collective-permute-start.3 = (bf16[384,768]{1,0:T(8,128)(2,1)S(1)}, bf16[384,768]{1,0:T(8,128)(2,1)S(1)}, u32[]{:S(2)}, u32[]{:S(2)}) collective-permute-start(bf16[384,768]{1,0:T(8,128)(2,1)S(1)} %slice.17), channel_id=1, source_target_pairs={{0,3},{1,0},{2,1},{3,2},{4,7},{5,4},{6,5},{7,6},{8,11},{9,8},{10,9... | collective-permute-start | bytes 1769480 | tf_op jit(solution)/shard_map/ppermute | solution.py:54
  83.0 2.3 %copy-start.2 = (bf16[1,768,768]{2,1,0:T(8,128)(2,1)S(1)}, bf16[1,768,768]{2,1,0:T(8,128)(2,1)}, u32[]{:S(2)}) copy-start(bf16[1,768,768]{2,1,0:T(8,128)(2,1)} %param.6) | copy-start | bytes 3538948
  106.0 58.7 %reduce-scatter.5.cloned.1.call-start = ((), (), s32[]{:S(2)}) async-start(), calls=%async_computation.5 | async-start | bytes 3932160 | tf_op jit(solution)/shard_map/reduce_scatter | solution.py:102
  122.2 68.3 %copy-start.1 = (bf16[768,1024]{1,0:T(8,128)(2,1)S(1)}, bf16[768,1024]{1,0:T(8,128)(2,1)}, u32[]{:S(2)}) copy-start(bf16[768,1024]{1,0:T(8,128)(2,1)} %param.11) | copy-start | bytes 4718596
  124.4 42.8 %all-to-all-start = ((f32[128,1,2]{2,1,0:T(1,128)}), f32[128,1,2]{2,1,0:T(1,128)S(1)}, u32[]{:S(2)}, u32[]{:S(2)}) async-start(f32[128,1,2]{2,1,0:T(1,128)} %broadcast_in_dim.12), calls=%async_computation | async-start | bytes 131072 | tf_op jit(solution)/shard_map/all_to_all | solution.py:39
  167.2 22.0 %all-to-all-start.1 = ((f32[16,2,24,256]{3,2,1,0:T(8,128)}), f32[16,2,24,256]{3,2,1,0:T(8,128)S(1)}, u32[]{:S(2)}, u32[]{:S(2)}) async-start(f32[16,2,24,256]{3,2,1,0:T(8,128)} %bitcast.14), calls=%async_computation.3 | async-start | bytes 1572864 | tf_op jit(solution)/shard_map/all_to_all | solution.py:106
Sparse Core Ops, SparseCore 0:
  106.1 16.0 reduce-scatter.2
  124.7 39.8 reduce-scatter.4

commit v10 on v9

--- a/solution.py
+++ b/solution.py
@@ -97,14 +97,20 @@
     y_size = lax.axis_size("y")
     x_size = lax.axis_size("x")
     core_size = lax.axis_size("core")
-    heads = heads.reshape(2, y_size, x_size, core_size, feat // (y_size * x_size * core_size), embed)
+    block_rows = feat // (y_size * x_size * core_size)
+    heads = heads.reshape(2, y_size, x_size, core_size, block_rows, embed)
     heads = lax.psum_scatter(heads, "core", scatter_dimension=3, tiled=False)
-    heads = lax.psum_scatter(heads, "x", scatter_dimension=2, tiled=False)
     blk_size = lax.axis_size("blk")
-    heads = heads.reshape(2, y_size, feat // (y_size * x_size * core_size), blk_size, embed // blk_size)
-    heads = heads.transpose(1, 3, 0, 2, 4).reshape((y_size * blk_size, 2) + heads.shape[2:3] + heads.shape[4:])
-    heads = lax.all_to_all(heads, ("y", "blk"), 0, 0, tiled=True)
-    heads = jnp.sum(heads, axis=0)
+    cols = embed // blk_size
+    heads = heads.reshape(2, y_size, x_size, block_rows, blk_size, cols)
+    prod_part = heads[0].transpose(1, 0, 2, 3, 4)
+    prod_part = jnp.sum(lax.all_to_all(prod_part, "x", 0, 0, tiled=True), axis=0)
+    prod_part = prod_part.transpose(0, 2, 1, 3).reshape(y_size * blk_size, block_rows, cols)
+    prod_part = jnp.sum(lax.all_to_all(prod_part, ("y", "blk"), 0, 0, tiled=True), axis=0)
+    prec_part = lax.psum_scatter(heads[1], "blk", scatter_dimension=3, tiled=False)
+    prec_part = prec_part.reshape(y_size * x_size, block_rows, cols)
+    prec_part = jnp.sum(lax.all_to_all(prec_part, ("y", "x"), 0, 0, tiled=True), axis=0)
+    heads = jnp.stack([prod_part, prec_part])
     heads = heads / weight_total
     return (loss_sum / weight_total, heads[0], heads[1])
 

time: 199 us -> 232 us (1.17)
  blocking collectives: 0 us -> 13.1 us
  waiting for transfers between devices: 79.3 us -> 90.2 us
  local copies, waits for them, and re-layouts: 8.86 us -> 14 us
  other arithmetic: 8.85 us -> 12.8 us
    reduce_scatter x2 -> x1, waiting for transfers between devices: 46.3 us -> 0.01 us  [per_device(): lax.psum_scatter(heads[1], 'blk', scatter_dimension=3, tiled=False)]
    unnamed x2 -> x3, waiting for transfers between devices: 0.03 us -> 35.5 us
    all_to_all x1 -> x2, waiting for transfers between devices: 12.7 us -> 26.1 us  [the longest x1 19.7 us: per_device(): lax.all_to_all(prod_part, 'x', 0, 0, tiled=True)]
    all_to_all x0 -> x1, blocking collectives: none -> 13.1 us  [per_device(): lax.all_to_all(prod_part, ('y', 'blk'), 0, 0, tiled=True)]
    all_to_all x1, waiting for transfers between devices: 0.01 us -> 8.36 us  [gathered_sum(): return jnp.sum(lax.all_to_all(spread, axes, 0, 0, tiled=True), axis=0)]
    squeeze x0 -> x4, local copies, waits for them, and re-layouts: none -> 5.59 us  [the longest x2 3.42 us: per_device(): heads[1]]
    another operation x2 -> x0, local copies, waits for them, and re-layouts: 4.72 us -> none  [the longest x1 3.24 us: per_device(): heads = jnp.stack([head_prod, head_prec])]
    slice x0 -> x1, local copies, waits for them, and re-layouts: none -> 4.09 us  [per_device(): prod_part = heads[0].transpose(1, 0, 2, 3, 4)]
  transfers between devices with their start and end apart: 8 -> 9, of which waited for: 4 -> 5; matrix products, arithmetic and copies ran while one was open for 15% -> 13% of each run, Pallas kernels for 0% -> 0%
where the time goes in v10:
time: 232 us; the launch traced here: 231 us
  waiting for transfers between devices  90.2 us (39%)
  matrix products  59.7 us (26%)
  starting transfers between devices  24.5 us (11%)
  between operations  16.8 us (7%)
  local copies, waits for them, and re-layouts  14 us (6%)
  blocking collectives  13.1 us (6%)
  other arithmetic  12.8 us (6%)
    unnamed x3, waiting for transfers between devices  35.5 us
    ppermute x1, waiting for transfers between devices, per_device(): lax.ppermute(feat_prec, 'blk', [(i, (i + 1) % blk_size) for i in range(bl...  20.2 us
    all_to_all x1, waiting for transfers between devices, per_device(): lax.all_to_all(prod_part, 'x', 0, 0, tiled=True)  19.7 us
    dot_general x2, matrix products, per_device(): lax.dot_general(block, dir_prec, (((0,), (0,)), ((), ())), preferred_elem...  15 us
    dot_general x3, matrix products, embed_rows(): jnp.dot(features, weight, preferred_element_type=jnp.float32)  13.5 us
    all_to_all x1, blocking collectives, per_device(): lax.all_to_all(prod_part, ('y', 'blk'), 0, 0, tiled=True)  13.1 us
    dot_general x2, matrix products, per_device(): lax.dot_general(coeffs, unit16_prod, (((0,), (0,)), ((), ())), preferred_...  11 us
    dot_general x2, matrix products, similarity(): lax.dot_general(queries, key_rows, (((1,), (1,)), ((), ())), preferred_el...  9.63 us
  transfers between devices with their start and end apart: 9, of which 5 were waited for; matrix products, arithmetic and copies ran while one was open for 13% of the time, Pallas kernels for 0%

profile of v10, /device:TPU:0, one launch (start us, length us, event | category | flops | bytes accessed | tf_op | source)
XLA Modules:
  0.0 231.1 jit_solution(10400999979007524791)
XLA Ops:
  7.2 2.1 collective-permute-start.1
  9.3 2.2 collective-permute-start
  12.4 1.3 fusion.33
  13.7 3.2 %multiply_reduce_fusion.5 = (f32[768]{0:T(1024)S(1)}, f32[768,1024]{1,0:T(8,128)S(1)}) fusion(bf16[768,1024]{1,0:T(8,128)(2,1)} %param.10, bf16[1,768,768]{2,1,0:T(8,128)(2,1)} %param.6), kind=kOutput, calls=%fused_computation.21 | convolution fusion | flops 1209531648 | bytes 5901312 | tf_op jit(solution)/shard_map/dot_general | solution.py:11
  17.4 20.2 %collective-permute-done.1 = bf16[768,768]{1,0:T(8,128)(2,1)S(1)} collective-permute-done((bf16[768,768]{1,0:T(8,128)(2,1)}, bf16[768,768]{1,0:T(8,128)(2,1)S(1)}, u32[]{:S(2)}, u32[]{:S(2)}) %collective-permute-start.1) | collective-permute-done | bytes 1179680 | tf_op jit(solution)/shard_map/ppermute | solution.py:51
  38.8 3.3 %collective-permute-start.3 = (bf16[384,768]{1,0:T(8,128)(2,1)S(1)}, bf16[384,768]{1,0:T(8,128)(2,1)S(1)}, u32[]{:S(2)}, u32[]{:S(2)}) collective-permute-start(bf16[384,768]{1,0:T(8,128)(2,1)S(1)} %slice.27), channel_id=1, source_target_pairs={{0,3},{1,0},{2,1},{3,2},{4,7},{5,4},{6,5},{7,6},{8,11},{9,8},{10,9... | collective-permute-start | bytes 1769480 | tf_op jit(solution)/shard_map/ppermute | solution.py:54
  42.1 8.8 %multiply_reduce_fusion.1 = (f32[2304]{0:T(1024)S(1)}, f32[2304,1024]{0,1:T(8,128)}) fusion(bf16[768,1024]{1,0:T(8,128)(2,1)S(1)} %copy-done, bf16[768,768]{1,0:T(8,128)(2,1)S(1)} %collective-permute-done.1, bf16[768,768]{1,0:T(8,128)(2,1)} %collective-permute-done, bf16[768,768]{1,0:T(8,128)(2,1)S(1)} %bitcast.59), kind=kOutput, calls=%fused_computation.2 | convolution fusion | flops 3639211776 | bytes 14558208 | tf_op jit(solution)/shard_map/dot_general | solution.py:11
  50.9 7.9 %fusion.4 = (f32[768]{0:T(1024)S(1)}, f32[768]{0:T(1024)S(1)}, f32[768,2304]{1,0:T(8,128)S(1)}) fusion(s32[2304]{0:T(1024)S(1)} %add.118, s32[768]{0:T(1024)S(1)} %reduce.3, bf16[768,1024]{1,0:T(8,128)(2,1)S(1)} %fusion.29, f32[2304,1024]{0,1:T(8,128)} %get-tuple-element.20, f32[2304]{0:T(1024)S(1)} %add_sqrt_fusion), kind=kOutput, calls=%fused_computation.11 | convolution fusion | flops 3639212544 | bytes 18115584 | tf_op jit(solution)/shard_map/dot_general | solution.py:18
  58.9 1.5 multiply_reduce_fusion.4
  60.4 1.8 fusion.14
  62.8 2.7 %fusion.3 = bf16[768,2304]{1,0:T(8,128)(2,1)S(1)} fusion(f32[768,2304]{1,0:T(8,128)S(1)} %get-tuple-element.21, f32[768]{0:T(1024)S(1)} %get-tuple-element.10, f32[768]{0:T(1024)S(1)} %get-tuple-element.7, s32[2304]{0:T(1024)S(1)} %add.118, s32[768]{0:T(1024)S(1)} %reduce.3), kind=kLoop, calls=%fused_computation.8 | loop fusion | flops 14155776 | bytes 10635264 | tf_op jit(solution)/shard_map/convert_element_type | solution.py:25
  65.5 6.4 %fusion.10 = f32[768,1024]{1,0:T(8,128)S(1)} fusion(bf16[768,2304]{1,0:T(8,128)(2,1)S(1)} %fusion.3, f32[2304,1024]{0,1:T(8,128)} %get-tuple-element.20, f32[2304]{0:T(1024)S(1)} %add_sqrt_fusion), kind=kOutput, calls=%fused_computation.29 | convolution fusion | flops 3628597248 | bytes 16131072 | tf_op jit(solution)/shard_map/dot_general | solution.py:83
  72.0 9.2 %multiply_reduce_fusion = (f32[2304]{0:T(1024)S(1)}, f32[2304,1024]{0,1:T(8,128)}) fusion(f32[2304,1024]{0,1:T(8,128)} %get-tuple-element.20, f32[2304]{0:T(1024)S(1)} %add_sqrt_fusion, bf16[768,2304]{1,0:T(8,128)(2,1)S(1)} %fusion.3, bf16[768,1024]{1,0:T(8,128)(2,1)S(1)} %fusion.29), kind=kOutput, calls=%fused_computation.1 | convolution fusion | flops 3633313536 | bytes 24004608 | tf_op jit(solution)/shard_map/dot_general | solution.py:84
  81.2 1.8 multiply_reduce_fusion.2
  83.0 2.3 %multiply_reduce_fusion.3 = (f32[768]{0:T(1024)S(1)}, f32[768,1024]{1,0:T(8,128)S(1)}) fusion(f32[768,1024]{1,0:T(8,128)S(1)} %get-tuple-element.18, f32[768]{0:T(1024)S(1)} %add_sqrt_fusion.2, f32[768,1024]{1,0:T(8,128)S(1)} %fusion.10, f32[768,1024]{1,0:T(8,128)S(1)} %get-tuple-element.23, f32[768]{0:T(1024)S(1)} %add_sqrt_fusion.1, ...), kind=kOutput, calls=%fused_computation.18 | convolution fusion | flops 1218182400 | bytes 14963712 | tf_op jit(solution)/shard_map/dot_general | solution.py:83
  85.3 1.8 fusion.16
  87.2 3.4 %fusion.17 = f32[768,1024]{1,0:T(8,128)} fusion(bf16[768,768]{1,0:T(8,128)(2,1)S(1)} %constant_dynamic-update-slice_fusion, f32[768,1024]{1,0:T(8,128)S(1)} %get-tuple-element.26, f32[768]{0:T(1024)S(1)} %get-tuple-element.25, f32[768]{0:T(1024)S(1)} %add_sqrt_fusion.1, f32[768,1024]{1,0:T(8,128)S(1)} %get-tuple-element.23), kind=kOutput, calls=%fused_computation.39 | convolution fusion | flops 1212678144 | bytes 10622976 | tf_op jit(solution)/shard_map/dot_general | solution.py:88
  90.6 11.6 %fusion.15 = f32[768,1024]{1,0:T(8,128)S(1)} fusion(f32[768,1024]{1,0:T(8,128)} %fusion.17, f32[2304,1024]{0,1:T(8,128)} %get-tuple-element.28, f32[2304]{0:T(1024)S(1)} %get-tuple-element.27, f32[2304]{0:T(1024)S(1)} %add_sqrt_fusion, bf16[768,768]{1,0:T(8,128)(2,1)S(1)} %collective-permute-done.1, bf16[768,768]{1,0:T(8,128)(2,1)} %collective-permute-done, ...), kind=kOutput, calls=%fused_computation.34 | convolution fusion | flops 3649437696 | bytes 28723200 | tf_op jit(solution)/shard_map/dot_general | solution.py:88
  102.2 3.2 %pad_maximum_fusion = f32[2,4,4,2,24,1024]{5,4,3,2,1,0:T(8,128)} fusion(f32[1,4,4,2,24,1024]{5,4,3,2,1,0:T(8,128)S(1)} %bitcast.51, f32[1,4,4,2,24,1024]{5,4,3,2,1,0:T(8,128)S(1)} %bitcast.50), kind=kLoop, calls=%fused_computation.10 | loop fusion | flops 1572864 | bytes 12582912 | tf_op jit(solution)/shard_map/stack | solution.py:95
  106.6 35.4 %all-reduce.3.cloned.1.call-done = f32[2,4,4,2,24,1024]{5,4,3,2,1,0:T(8,128)} async-done(((f32[2,4,4,2,24,1024]{5,4,3,2,1,0:T(8,128)}), f32[2,4,4,2,24,1024]{5,4,3,2,1,0:T(8,128)}) %all-reduce.3.cloned.1.call-update) | async-done | bytes 6291472
  142.1 4.1 %constant_dynamic-slice_fusion = (f32[1,4,4,1,24,1024]{5,4,3,2,1,0:T(8,128)S(1)}, f32[1,4,4,1,24,1024]{5,4,3,2,1,0:T(8,128)}) fusion(f32[2,4,4,2,24,1024]{5,4,3,2,1,0:T(8,128)} %all-reduce.3.cloned.1.call-done, u32[]{:T(128)} %bitcast.23, u32[]{:T(128)S(6)} %convert), kind=kLoop, calls=%fused_computation.60 | loop fusion | bytes 6291464 | tf_op jit(solution)/shard_map/slice | solution.py:106
  146.2 2.0 squeeze.25
  148.2 1.4 copy.21
  150.4 1.4 copy.29
  151.8 4.3 %all-to-all-start.1 = ((f32[4,4,24,4,256]{4,3,2,1,0:T(4,128)}), f32[4,4,24,4,256]{4,3,2,1,0:T(4,128)S(1)}, u32[]{:S(2)}, u32[]{:S(2)}) async-start(f32[4,4,24,4,256]{4,3,2,1,0:T(4,128)} %bitcast.49), calls=%async_computation.1 | async-start | bytes 3145728 | tf_op jit(solution)/shard_map/all_to_all | solution.py:107
  156.1 1.5 pad_maximum_fusion.4
  157.6 19.7 %all-to-all-done.1 = f32[4,4,24,4,256]{4,3,2,1,0:T(4,128)S(1)} async-done(((f32[4,4,24,4,256]{4,3,2,1,0:T(4,128)}), f32[4,4,24,4,256]{4,3,2,1,0:T(4,128)S(1)}, u32[]{:S(2)}, u32[]{:S(2)}) %all-to-all-start.1) | async-done | bytes 1572896 | tf_op jit(solution)/shard_map/all_to_all | solution.py:107
  178.0 8.7 %all-to-all-start = ((f32[128,1,2]{2,1,0:T(1,128)}), f32[128,1,2]{2,1,0:T(1,128)}, u32[]{:S(2)}, u32[]{:S(2)}) async-start(f32[128,1,2]{2,1,0:T(1,128)} %broadcast_in_dim.12), calls=%async_computation | async-start | bytes 131072 | tf_op jit(solution)/shard_map/all_to_all | solution.py:39
  187.2 8.4 %all-to-all-done = f32[128,1,2]{2,1,0:T(1,128)} async-done(((f32[128,1,2]{2,1,0:T(1,128)}), f32[128,1,2]{2,1,0:T(1,128)}, u32[]{:S(2)}, u32[]{:S(2)}) %all-to-all-start) | async-done | bytes 1056 | tf_op jit(solution)/shard_map/all_to_all | solution.py:39
  195.5 13.1 %all_to_all.21 = f32[16,24,256]{2,1,0:T(8,128)S(1)} all-to-all(f32[16,24,256]{2,1,0:T(8,128)S(1)} %bitcast.52), channel_id=1, replica_groups=mesh['y'=4,'x'=4,'core'=2,'blk'=4] {'y','blk'}, dimensions={0} | all-to-all | bytes 786432 | tf_op jit(solution)/shard_map/all_to_all | solution.py:109
  208.6 3.8 %all-to-all-start.3 = ((f32[16,24,256]{2,1,0:T(8,128)}), f32[16,24,256]{2,1,0:T(8,128)S(1)}, u32[]{:S(2)}, u32[]{:S(2)}) async-start(f32[16,24,256]{2,1,0:T(8,128)} %bitcast.54), calls=%async_computation.4 | async-start | bytes 786432 | tf_op jit(solution)/shard_map/all_to_all | solution.py:112
  215.4 6.4 %all-to-all-done.3 = f32[16,24,256]{2,1,0:T(8,128)S(1)} async-done(((f32[16,24,256]{2,1,0:T(8,128)}), f32[16,24,256]{2,1,0:T(8,128)S(1)}, u32[]{:S(2)}, u32[]{:S(2)}) %all-to-all-start.3) | async-done | bytes 393248 | tf_op jit(solution)/shard_map/all_to_all | solution.py:112
  (44 shorter events, 9.3 us)
Async XLA Ops:
  7.2 35.0 %copy-start = (bf16[768,1024]{1,0:T(8,128)(2,1)S(1)}, bf16[768,1024]{1,0:T(8,128)(2,1)}, u32[]{:S(2)}) copy-start(bf16[768,1024]{1,0:T(8,128)(2,1)} %param.11) | copy-start | bytes 4718596
  7.2 134.9 %all-reduce.3.cloned.1.call-start = ((), (), s32[]{:S(2)}) async-start(), calls=%async_computation.6 | async-start | bytes 12582912
  7.2 30.4 %collective-permute-start.1 = (bf16[768,768]{1,0:T(8,128)(2,1)}, bf16[768,768]{1,0:T(8,128)(2,1)S(1)}, u32[]{:S(2)}, u32[]{:S(2)}) collective-permute-start(bf16[768,768]{1,0:T(8,128)(2,1)} %bitcast.57), channel_id=1, source_target_pairs={{0,1},{1,2},{2,3},{3,0},{4,5},{5,6},{6,7},{7,4},{8,9},{9,10},{10,1... | collective-permute-start | bytes 3538952 | tf_op jit(solution)/shard_map/ppermute | solution.py:51
  9.3 28.4 %collective-permute-start = (bf16[768,768]{1,0:T(8,128)(2,1)}, bf16[768,768]{1,0:T(8,128)(2,1)}, u32[]{:S(2)}, u32[]{:S(2)}) collective-permute-start(bf16[768,768]{1,0:T(8,128)(2,1)} %bitcast.58), channel_id=1, source_target_pairs={{0,3},{1,0},{2,1},{3,2},{4,7},{5,4},{6,5},{7,6},{8,11},{9,8},{10,9... | collective-permute-start | bytes 3538952 | tf_op jit(solution)/shard_map/ppermute | solution.py:50
  16.9 25.2 %copy-start.3 = (bf16[1,768,768]{2,1,0:T(8,128)(2,1)S(1)}, bf16[1,768,768]{2,1,0:T(8,128)(2,1)}, u32[]{:S(2)}) copy-start(bf16[1,768,768]{2,1,0:T(8,128)(2,1)} %param.7) | copy-start | bytes 3538948
  37.6 21.2 %collective-permute-start.2 = (bf16[384,768]{1,0:T(8,128)(2,1)S(1)}, bf16[384,768]{1,0:T(8,128)(2,1)S(1)}, u32[]{:S(2)}, u32[]{:S(2)}) collective-permute-start(bf16[384,768]{1,0:T(8,128)(2,1)S(1)} %slice.26), channel_id=1, source_target_pairs={{0,1},{1,2},{2,3},{3,0},{4,5},{5,6},{6,7},{7,4},{8,9},{9,10},{10,1... | collective-permute-start | bytes 1769480 | tf_op jit(solution)/shard_map/ppermute | solution.py:53
  38.8 20.0 %collective-permute-start.3 = (bf16[384,768]{1,0:T(8,128)(2,1)S(1)}, bf16[384,768]{1,0:T(8,128)(2,1)S(1)}, u32[]{:S(2)}, u32[]{:S(2)}) collective-permute-start(bf16[384,768]{1,0:T(8,128)(2,1)S(1)} %slice.27), channel_id=1, source_target_pairs={{0,3},{1,0},{2,1},{3,2},{4,7},{5,4},{6,5},{7,6},{8,11},{9,8},{10,9... | collective-permute-start | bytes 1769480 | tf_op jit(solution)/shard_map/ppermute | solution.py:54
  83.0 2.3 %copy-start.2 = (bf16[1,768,768]{2,1,0:T(8,128)(2,1)S(1)}, bf16[1,768,768]{2,1,0:T(8,128)(2,1)}, u32[]{:S(2)}) copy-start(bf16[1,768,768]{2,1,0:T(8,128)(2,1)} %param.6) | copy-start | bytes 3538948
  105.4 0.7 copy-start.4
  105.4 103.2 %reduce-scatter.3.cloned.1.call-start = ((), (), s32[]{:S(2)}) async-start(), calls=%async_computation.5 | async-start | bytes 1966080 | tf_op jit(solution)/shard_map/reduce_scatter | solution.py:110
  151.8 25.5 %all-to-all-start.1 = ((f32[4,4,24,4,256]{4,3,2,1,0:T(4,128)}), f32[4,4,24,4,256]{4,3,2,1,0:T(4,128)S(1)}, u32[]{:S(2)}, u32[]{:S(2)}) async-start(f32[4,4,24,4,256]{4,3,2,1,0:T(4,128)} %bitcast.49), calls=%async_computation.1 | async-start | bytes 3145728 | tf_op jit(solution)/shard_map/all_to_all | solution.py:107
  156.1 67.0 %copy-start.1 = (bf16[768,1024]{1,0:T(8,128)(2,1)S(1)}, bf16[768,1024]{1,0:T(8,128)(2,1)}, u32[]{:S(2)}) copy-start(bf16[768,1024]{1,0:T(8,128)(2,1)} %param.11) | copy-start | bytes 4718596
  178.0 17.6 %all-to-all-start = ((f32[128,1,2]{2,1,0:T(1,128)}), f32[128,1,2]{2,1,0:T(1,128)}, u32[]{:S(2)}, u32[]{:S(2)}) async-start(f32[128,1,2]{2,1,0:T(1,128)} %broadcast_in_dim.12), calls=%async_computation | async-start | bytes 131072 | tf_op jit(solution)/shard_map/all_to_all | solution.py:39
  208.6 13.2 %all-to-all-start.3 = ((f32[16,24,256]{2,1,0:T(8,128)}), f32[16,24,256]{2,1,0:T(8,128)S(1)}, u32[]{:S(2)}, u32[]{:S(2)}) async-start(f32[16,24,256]{2,1,0:T(8,128)} %bitcast.54), calls=%async_computation.4 | async-start | bytes 786432 | tf_op jit(solution)/shard_map/all_to_all | solution.py:112
Sparse Core Ops, SparseCore 0:
  105.5 36.4 all-reduce.2
  149.7 27.2 reduce-scatter.2

commit v11 on v9

--- a/solution.py
+++ b/solution.py
@@ -99,12 +99,14 @@
     core_size = lax.axis_size("core")
     heads = heads.reshape(2, y_size, x_size, core_size, feat // (y_size * x_size * core_size), embed)
     heads = lax.psum_scatter(heads, "core", scatter_dimension=3, tiled=False)
-    heads = lax.psum_scatter(heads, "x", scatter_dimension=2, tiled=False)
     blk_size = lax.axis_size("blk")
-    heads = heads.reshape(2, y_size, feat // (y_size * x_size * core_size), blk_size, embed // blk_size)
-    heads = heads.transpose(1, 3, 0, 2, 4).reshape((y_size * blk_size, 2) + heads.shape[2:3] + heads.shape[4:])
-    heads = lax.all_to_all(heads, ("y", "blk"), 0, 0, tiled=True)
-    heads = jnp.sum(heads, axis=0)
+    block_rows = feat // (y_size * x_size * core_size)
+    cols = embed // blk_size
+    heads = heads.reshape(2, y_size, x_size, block_rows, blk_size, cols).transpose(2, 4, 0, 1, 3, 5)
+    heads = heads.reshape((x_size * blk_size, 2, y_size, block_rows, cols))
+    heads = jnp.sum(lax.all_to_all(heads, ("x", "blk"), 0, 0, tiled=True), axis=0)
+    heads = heads.transpose(1, 0, 2, 3)
+    heads = jnp.sum(lax.all_to_all(heads, "y", 0, 0, tiled=True), axis=0)
     heads = heads / weight_total
     return (loss_sum / weight_total, heads[0], heads[1])
 

time: 199 us -> 223 us (1.12)
  waiting for transfers between devices: 79.3 us -> 92.7 us
  local copies, waits for them, and re-layouts: 8.86 us -> 16.3 us
  starting transfers between devices: 25 us -> 32.2 us
  matrix products: 59.7 us -> 53.3 us
    all_to_all x1 -> x2, waiting for transfers between devices: 12.7 us -> 45.4 us  [the longest x1 41.2 us: per_device(): lax.all_to_all(heads, ('x', 'blk'), 0, 0, tiled=True)]
    reduce_scatter x1 -> x0, waiting for transfers between devices: 30.2 us -> none  [per_device(): heads = lax.psum_scatter(heads, 'x', scatter_dimension=2, tiled=False)]
    all_to_all x1, waiting for transfers between devices: 0.01 us -> 6.31 us  [gathered_sum(): return jnp.sum(lax.all_to_all(spread, axes, 0, 0, tiled=True), axis=0)]
    all_to_all x1, starting transfers between devices: 10.1 us -> 13.9 us  [gathered_sum(): return jnp.sum(lax.all_to_all(spread, axes, 0, 0, tiled=True), axis=0)]
    transpose x1 -> x2, local copies, waits for them, and re-layouts: 1.02 us -> 4.83 us  [the longest x1 4.15 us: per_device(): heads.reshape(2, y_size, x_size, block_rows, blk_size, cols)]
    another operation x1, local copies, waits for them, and re-layouts: 1.49 us -> 5.14 us  [per_device(): heads.reshape(2, y_size, x_size, block_rows, blk_size, cols)]
    dot_general x3, matrix products: 13.5 us -> 10.1 us  [embed_rows(): jnp.dot(features, weight, preferred_element_type=jnp.float32)]
    all_to_all x1 -> x2, starting transfers between devices: 7.22 us -> 10.5 us  [the longest x1 7.11 us: per_device(): lax.all_to_all(heads, ('x', 'blk'), 0, 0, tiled=True)]
  transfers between devices with their start and end apart: 8 -> 8, of which waited for: 4 -> 7; matrix products, arithmetic and copies ran while one was open for 15% -> 10% of each run, Pallas kernels for 0% -> 0%
where the time goes in v11:
time: 223 us; the launch traced here: 222 us
  waiting for transfers between devices  92.7 us (42%)
  matrix products  53.3 us (24%)
  starting transfers between devices  32.2 us (14%)
  between operations  16.7 us (7%)
  local copies, waits for them, and re-layouts  16.3 us (7%)
  other arithmetic  10.9 us (5%)
    all_to_all x1, waiting for transfers between devices, per_device(): lax.all_to_all(heads, ('x', 'blk'), 0, 0, tiled=True)  41.2 us
    ppermute x1, waiting for transfers between devices, per_device(): lax.ppermute(feat_prec, 'blk', [(i, (i + 1) % blk_size) for i in range(bl...  20.2 us
    reduce_scatter x1, waiting for transfers between devices, per_device(): heads = lax.psum_scatter(heads, 'core', scatter_dimension=3, tiled=False)  19.3 us
    dot_general x2, matrix products, per_device(): lax.dot_general(block, dir_prec, (((0,), (0,)), ((), ())), preferred_elem...  15 us
    all_to_all x1, starting transfers between devices, gathered_sum(): return jnp.sum(lax.all_to_all(spread, axes, 0, 0, tiled=True), axis=0)  13.9 us
    dot_general x2, matrix products, per_device(): lax.dot_general(coeffs, unit16_prod, (((0,), (0,)), ((), ())), preferred_...  11.1 us
    dot_general x3, matrix products, embed_rows(): jnp.dot(features, weight, preferred_element_type=jnp.float32)  10.1 us
    dot_general x2, matrix products, per_device(): jnp.dot(coeffs, unit16_prec, preferred_element_type=jnp.float32)  8.78 us
  transfers between devices with their start and end apart: 8, of which 7 were waited for; matrix products, arithmetic and copies ran while one was open for 10% of the time, Pallas kernels for 0%

profile of v11, /device:TPU:0, one launch (start us, length us, event | category | flops | bytes accessed | tf_op | source)
XLA Modules:
  0.0 222.3 jit_solution(3707937644642428170)
XLA Ops:
  7.2 2.1 collective-permute-start.1
  9.3 2.2 collective-permute-start
  12.4 1.3 fusion.33
  13.7 3.2 %multiply_reduce_fusion.5 = (f32[768]{0:T(1024)S(1)}, f32[768,1024]{1,0:T(8,128)S(1)}) fusion(bf16[768,1024]{1,0:T(8,128)(2,1)} %param.10, bf16[1,768,768]{2,1,0:T(8,128)(2,1)} %param.6), kind=kOutput, calls=%fused_computation.21 | convolution fusion | flops 1209531648 | bytes 5901312 | tf_op jit(solution)/shard_map/dot_general | solution.py:11
  17.4 20.2 %collective-permute-done.1 = bf16[768,768]{1,0:T(8,128)(2,1)S(1)} collective-permute-done((bf16[768,768]{1,0:T(8,128)(2,1)}, bf16[768,768]{1,0:T(8,128)(2,1)S(1)}, u32[]{:S(2)}, u32[]{:S(2)}) %collective-permute-start.1) | collective-permute-done | bytes 1179680 | tf_op jit(solution)/shard_map/ppermute | solution.py:51
  37.7 1.1 slice.17
  38.8 3.5 %collective-permute-start.3 = (bf16[384,768]{1,0:T(8,128)(2,1)S(1)}, bf16[384,768]{1,0:T(8,128)(2,1)S(1)}, u32[]{:S(2)}, u32[]{:S(2)}) collective-permute-start(bf16[384,768]{1,0:T(8,128)(2,1)S(1)} %slice.17), channel_id=1, source_target_pairs={{0,3},{1,0},{2,1},{3,2},{4,7},{5,4},{6,5},{7,6},{8,11},{9,8},{10,9... | collective-permute-start | bytes 1769480 | tf_op jit(solution)/shard_map/ppermute | solution.py:54
  42.3 5.5 %multiply_reduce_fusion.1 = (f32[2304]{0:T(1024)S(1)}, f32[2304,1024]{0,1:T(8,128)S(1)}) fusion(bf16[768,1024]{1,0:T(8,128)(2,1)S(1)} %copy-done, bf16[768,768]{1,0:T(8,128)(2,1)S(1)} %collective-permute-done.1, bf16[768,768]{1,0:T(8,128)(2,1)} %collective-permute-done, bf16[768,768]{1,0:T(8,128)(2,1)S(1)} %bitcast.48), kind=kOutput, calls=%fused_computation.2 | convolution fusion | flops 3639211776 | bytes 14558208 | tf_op jit(solution)/shard_map/dot_general | solution.py:11
  47.8 4.8 %fusion.4 = (f32[768]{0:T(1024)S(1)}, f32[768]{0:T(1024)S(1)}, f32[768,2304]{1,0:T(8,128)S(1)}) fusion(s32[2304]{0:T(1024)S(1)} %add.116, s32[768]{0:T(1024)S(1)} %reduce.3, bf16[768,1024]{1,0:T(8,128)(2,1)S(1)} %fusion.29, f32[2304,1024]{0,1:T(8,128)S(1)} %get-tuple-element.18, f32[2304]{0:T(1024)S(1)} %add_sqrt_fusion), kind=kOutput, calls=%fused_computation.11 | convolution fusion | flops 3639212544 | bytes 18115584 | tf_op jit(solution)/shard_map/dot_general | solution.py:18
  52.6 0.8 collective-permute-done.2
  54.1 1.5 multiply_reduce_fusion.4
  55.6 1.7 fusion.14
  57.9 2.7 %fusion.3 = bf16[768,2304]{1,0:T(8,128)(2,1)S(1)} fusion(f32[768,2304]{1,0:T(8,128)S(1)} %get-tuple-element.19, f32[768]{0:T(1024)S(1)} %get-tuple-element.10, f32[768]{0:T(1024)S(1)} %get-tuple-element.7, s32[2304]{0:T(1024)S(1)} %add.116, s32[768]{0:T(1024)S(1)} %reduce.3), kind=kLoop, calls=%fused_computation.8 | loop fusion | flops 14155776 | bytes 10635264 | tf_op jit(solution)/shard_map/convert_element_type | solution.py:25
  60.6 6.4 %fusion.10 = f32[768,1024]{1,0:T(8,128)S(1)} fusion(bf16[768,2304]{1,0:T(8,128)(2,1)S(1)} %fusion.3, f32[2304,1024]{0,1:T(8,128)} %copy-done.4, f32[2304]{0:T(1024)S(1)} %add_sqrt_fusion), kind=kOutput, calls=%fused_computation.29 | convolution fusion | flops 3628597248 | bytes 16131072 | tf_op jit(solution)/shard_map/dot_general | solution.py:83
  67.1 9.3 %multiply_reduce_fusion = (f32[2304]{0:T(1024)S(1)}, f32[2304,1024]{0,1:T(8,128)}) fusion(f32[2304,1024]{0,1:T(8,128)} %copy-done.4, f32[2304]{0:T(1024)S(1)} %add_sqrt_fusion, bf16[768,2304]{1,0:T(8,128)(2,1)S(1)} %fusion.3, bf16[768,1024]{1,0:T(8,128)(2,1)S(1)} %fusion.29), kind=kOutput, calls=%fused_computation.1 | convolution fusion | flops 3633313536 | bytes 24004608 | tf_op jit(solution)/shard_map/dot_general | solution.py:84
  76.4 1.8 multiply_reduce_fusion.2
  78.2 2.3 %multiply_reduce_fusion.3 = (f32[768]{0:T(1024)S(1)}, f32[768,1024]{1,0:T(8,128)S(1)}) fusion(f32[768,1024]{1,0:T(8,128)S(1)} %get-tuple-element.16, f32[768]{0:T(1024)S(1)} %add_sqrt_fusion.2, f32[768,1024]{1,0:T(8,128)S(1)} %fusion.10, f32[768,1024]{1,0:T(8,128)S(1)} %get-tuple-element.21, f32[768]{0:T(1024)S(1)} %add_sqrt_fusion.1, ...), kind=kOutput, calls=%fused_computation.18 | convolution fusion | flops 1218182400 | bytes 14963712 | tf_op jit(solution)/shard_map/dot_general | solution.py:83
  80.5 1.8 fusion.16
  82.4 3.4 %fusion.17 = f32[768,1024]{1,0:T(8,128)} fusion(bf16[768,768]{1,0:T(8,128)(2,1)S(1)} %constant_dynamic-update-slice_fusion, f32[768,1024]{1,0:T(8,128)S(1)} %get-tuple-element.24, f32[768]{0:T(1024)S(1)} %get-tuple-element.23, f32[768]{0:T(1024)S(1)} %add_sqrt_fusion.1, f32[768,1024]{1,0:T(8,128)S(1)} %get-tuple-element.21), kind=kOutput, calls=%fused_computation.38 | convolution fusion | flops 1212678144 | bytes 10622976 | tf_op jit(solution)/shard_map/dot_general | solution.py:88
  85.8 11.6 %fusion.15 = f32[768,1024]{1,0:T(8,128)S(1)} fusion(f32[768,1024]{1,0:T(8,128)} %fusion.17, f32[2304,1024]{0,1:T(8,128)} %get-tuple-element.26, f32[2304]{0:T(1024)S(1)} %get-tuple-element.25, f32[2304]{0:T(1024)S(1)} %add_sqrt_fusion, bf16[768,768]{1,0:T(8,128)(2,1)S(1)} %collective-permute-done.1, bf16[768,768]{1,0:T(8,128)(2,1)} %collective-permute-done, ...), kind=kOutput, calls=%fused_computation.34 | convolution fusion | flops 3649437696 | bytes 28723200 | tf_op jit(solution)/shard_map/dot_general | solution.py:88
  97.9 3.2 %copy.28 = f32[2,4,4,2,24,1024]{5,4,2,1,0,3:T(8,128)} copy(f32[2,4,4,2,24,1024]{5,4,3,2,1,0:T(8,128)S(1)} %pad_maximum_fusion) | data formatting | bytes 12582912 | tf_op jit(solution)/shard_map/stack | solution.py:95
  101.2 19.3 %reduce-scatter.2.cloned.1.call-done = f32[2,4,4,1,24,1024]{5,4,2,1,0,3:T(8,128)} async-done(((f32[2,4,4,2,24,1024]{5,4,2,1,0,3:T(8,128)}), f32[2,4,4,1,24,1024]{5,4,2,1,0,3:T(8,128)}) %reduce-scatter.2.cloned.1.call-update) | async-done | bytes 3145744 | tf_op jit(solution)/shard_map/reduce_scatter | solution.py:101
  120.5 5.1 %reshape_reduce_scatter.3 = f32[2,4,4,24,4,256]{5,4,3,2,1,0:T(4,128)} reshape(f32[2,4,4,1,24,1024]{5,4,2,1,0,3:T(8,128)} %reduce-scatter.2.cloned.1.call-done) | data formatting | bytes 6291456 | tf_op jit(solution)/shard_map/reshape;reduce_scatter | solution.py:105
  125.7 4.1 %copy.26 = f32[4,4,2,4,24,256]{5,4,3,2,1,0:T(8,128)} copy(f32[4,4,2,4,24,256]{5,1,4,0,3,2:T(4,128)} %bitcast.42) | data formatting | bytes 6291456 | tf_op jit(solution)/shard_map/transpose | solution.py:105
  129.8 7.1 %all-to-all-start.1 = ((f32[16,2,4,24,256]{4,3,2,1,0:T(8,128)}), f32[16,2,4,24,256]{4,3,2,1,0:T(8,128)}, u32[]{:S(2)}, u32[]{:S(2)}) async-start(f32[16,2,4,24,256]{4,3,2,1,0:T(8,128)} %bitcast.41), calls=%async_computation.2 | async-start | bytes 6291456 | tf_op jit(solution)/shard_map/all_to_all | solution.py:107
  136.9 1.5 pad_maximum_fusion.4
  138.4 41.2 %all-to-all-done.1 = f32[16,2,4,24,256]{4,3,2,1,0:T(8,128)} async-done(((f32[16,2,4,24,256]{4,3,2,1,0:T(8,128)}), f32[16,2,4,24,256]{4,3,2,1,0:T(8,128)}, u32[]{:S(2)}, u32[]{:S(2)}) %all-to-all-start.1) | async-done | bytes 3145760 | tf_op jit(solution)/shard_map/all_to_all | solution.py:107
  180.3 13.9 %all-to-all-start = ((f32[128,1,2]{2,1,0:T(1,128)}), f32[128,1,2]{2,1,0:T(1,128)S(1)}, u32[]{:S(2)}, u32[]{:S(2)}) async-start(f32[128,1,2]{2,1,0:T(1,128)} %broadcast_in_dim.12), calls=%async_computation | async-start | bytes 131072 | tf_op jit(solution)/shard_map/all_to_all | solution.py:39
  194.2 2.1 reduce_sum.148
  197.0 6.3 %all-to-all-done = f32[128,1,2]{2,1,0:T(1,128)S(1)} async-done(((f32[128,1,2]{2,1,0:T(1,128)}), f32[128,1,2]{2,1,0:T(1,128)S(1)}, u32[]{:S(2)}, u32[]{:S(2)}) %all-to-all-start) | async-done | bytes 1056 | tf_op jit(solution)/shard_map/all_to_all | solution.py:39
  203.3 3.4 %all-to-all-start.2 = ((f32[4,2,24,256]{3,2,1,0:T(8,128)}), f32[4,2,24,256]{3,2,1,0:T(8,128)S(1)}, u32[]{:S(2)}, u32[]{:S(2)}) async-start(f32[4,2,24,256]{3,2,1,0:T(8,128)} %copy.27), calls=%async_computation.3 | async-start | bytes 393216 | tf_op jit(solution)/shard_map/all_to_all | solution.py:109
  208.8 4.2 %all-to-all-done.2 = f32[4,2,24,256]{3,2,1,0:T(8,128)S(1)} async-done(((f32[4,2,24,256]{3,2,1,0:T(8,128)}), f32[4,2,24,256]{3,2,1,0:T(8,128)S(1)}, u32[]{:S(2)}, u32[]{:S(2)}) %all-to-all-start.2) | async-done | bytes 196640 | tf_op jit(solution)/shard_map/all_to_all | solution.py:109
  (36 shorter events, 6.7 us)
Async XLA Ops:
  7.2 35.1 %copy-start = (bf16[768,1024]{1,0:T(8,128)(2,1)S(1)}, bf16[768,1024]{1,0:T(8,128)(2,1)}, u32[]{:S(2)}) copy-start(bf16[768,1024]{1,0:T(8,128)(2,1)} %param.11) | copy-start | bytes 4718596
  7.2 113.3 %reduce-scatter.2.cloned.1.call-start = ((), (), s32[]{:S(2)}) async-start(), calls=%async_computation.4 | async-start | bytes 9437184 | tf_op jit(solution)/shard_map/reduce_scatter | solution.py:101
  7.2 30.4 %collective-permute-start.1 = (bf16[768,768]{1,0:T(8,128)(2,1)}, bf16[768,768]{1,0:T(8,128)(2,1)S(1)}, u32[]{:S(2)}, u32[]{:S(2)}) collective-permute-start(bf16[768,768]{1,0:T(8,128)(2,1)} %bitcast.46), channel_id=1, source_target_pairs={{0,1},{1,2},{2,3},{3,0},{4,5},{5,6},{6,7},{7,4},{8,9},{9,10},{10,1... | collective-permute-start | bytes 3538952 | tf_op jit(solution)/shard_map/ppermute | solution.py:51
  9.3 28.4 %collective-permute-start = (bf16[768,768]{1,0:T(8,128)(2,1)}, bf16[768,768]{1,0:T(8,128)(2,1)}, u32[]{:S(2)}, u32[]{:S(2)}) collective-permute-start(bf16[768,768]{1,0:T(8,128)(2,1)} %bitcast.47), channel_id=1, source_target_pairs={{0,3},{1,0},{2,1},{3,2},{4,7},{5,4},{6,5},{7,6},{8,11},{9,8},{10,9... | collective-permute-start | bytes 3538952 | tf_op jit(solution)/shard_map/ppermute | solution.py:50
  16.9 25.4 %copy-start.3 = (bf16[1,768,768]{2,1,0:T(8,128)(2,1)S(1)}, bf16[1,768,768]{2,1,0:T(8,128)(2,1)}, u32[]{:S(2)}) copy-start(bf16[1,768,768]{2,1,0:T(8,128)(2,1)} %param.7) | copy-start | bytes 3538948
  37.6 15.8 %collective-permute-start.2 = (bf16[384,768]{1,0:T(8,128)(2,1)S(1)}, bf16[384,768]{1,0:T(8,128)(2,1)S(1)}, u32[]{:S(2)}, u32[]{:S(2)}) collective-permute-start(bf16[384,768]{1,0:T(8,128)(2,1)S(1)} %slice.16), channel_id=1, source_target_pairs={{0,1},{1,2},{2,3},{3,0},{4,5},{5,6},{6,7},{7,4},{8,9},{9,10},{10,1... | collective-permute-start | bytes 1769480 | tf_op jit(solution)/shard_map/ppermute | solution.py:53
  38.8 15.2 %collective-permute-start.3 = (bf16[384,768]{1,0:T(8,128)(2,1)S(1)}, bf16[384,768]{1,0:T(8,128)(2,1)S(1)}, u32[]{:S(2)}, u32[]{:S(2)}) collective-permute-start(bf16[384,768]{1,0:T(8,128)(2,1)S(1)} %slice.17), channel_id=1, source_target_pairs={{0,3},{1,0},{2,1},{3,2},{4,7},{5,4},{6,5},{7,6},{8,11},{9,8},{10,9... | collective-permute-start | bytes 1769480 | tf_op jit(solution)/shard_map/ppermute | solution.py:54
  47.8 4.8 %copy-start.4 = (f32[2304,1024]{0,1:T(8,128)}, f32[2304,1024]{0,1:T(8,128)S(1)}, u32[]{:S(2)}) copy-start(f32[2304,1024]{0,1:T(8,128)S(1)} %get-tuple-element.18) | copy-start | bytes 28311556
  78.2 2.3 %copy-start.2 = (bf16[1,768,768]{2,1,0:T(8,128)(2,1)S(1)}, bf16[1,768,768]{2,1,0:T(8,128)(2,1)}, u32[]{:S(2)}) copy-start(bf16[1,768,768]{2,1,0:T(8,128)(2,1)} %param.6) | copy-start | bytes 3538948
  129.8 49.8 %all-to-all-start.1 = ((f32[16,2,4,24,256]{4,3,2,1,0:T(8,128)}), f32[16,2,4,24,256]{4,3,2,1,0:T(8,128)}, u32[]{:S(2)}, u32[]{:S(2)}) async-start(f32[16,2,4,24,256]{4,3,2,1,0:T(8,128)} %bitcast.41), calls=%async_computation.2 | async-start | bytes 6291456 | tf_op jit(solution)/shard_map/all_to_all | solution.py:107
  136.9 77.4 %copy-start.1 = (bf16[768,1024]{1,0:T(8,128)(2,1)S(1)}, bf16[768,1024]{1,0:T(8,128)(2,1)}, u32[]{:S(2)}) copy-start(bf16[768,1024]{1,0:T(8,128)(2,1)} %param.11) | copy-start | bytes 4718596
  180.3 23.0 %all-to-all-start = ((f32[128,1,2]{2,1,0:T(1,128)}), f32[128,1,2]{2,1,0:T(1,128)S(1)}, u32[]{:S(2)}, u32[]{:S(2)}) async-start(f32[128,1,2]{2,1,0:T(1,128)} %broadcast_in_dim.12), calls=%async_computation | async-start | bytes 131072 | tf_op jit(solution)/shard_map/all_to_all | solution.py:39
  203.3 9.7 %all-to-all-start.2 = ((f32[4,2,24,256]{3,2,1,0:T(8,128)}), f32[4,2,24,256]{3,2,1,0:T(8,128)S(1)}, u32[]{:S(2)}, u32[]{:S(2)}) async-start(f32[4,2,24,256]{3,2,1,0:T(8,128)} %copy.27), calls=%async_computation.3 | async-start | bytes 393216 | tf_op jit(solution)/shard_map/all_to_all | solution.py:109
Sparse Core Ops, SparseCore 0:
  101.3 19.1 reduce-scatter.1

commit v12 on v9

--- a/solution.py
+++ b/solution.py
@@ -79,7 +79,7 @@
     for block, (unit_prec, unit16_prec, radius_prec), block_scores, block_matches in zip(
         blocks, embedded, scores, matches
     ):
-        coeffs = coefficient(block_scores, block_matches, weights, totals)
+        coeffs = lax.optimization_barrier(coefficient(block_scores, block_matches, weights, totals))
         grad_unit_prod = grad_unit_prod + jnp.dot(coeffs, unit16_prec, preferred_element_type=jnp.float32)
         grad_prec_part = LOGIT_SCALE * lax.dot_general(
             coeffs, unit16_prod, (((0,), (0,)), ((), ())), preferred_element_type=jnp.float32

time: 199 us -> 200 us (level)
  no operation moved by 1% of the time
where the time goes in v12:
time: 200 us
  waiting for transfers between devices  79.4 us (40%)
  matrix products  59 us (30%)
  starting transfers between devices  25 us (12%)
  between operations  16.8 us (8%)
  local copies, waits for them, and re-layouts  10 us (5%)
  other arithmetic  9.58 us (5%)
    reduce_scatter x1, waiting for transfers between devices, per_device(): heads = lax.psum_scatter(heads, 'x', scatter_dimension=2, tiled=False)  30.2 us
    ppermute x1, waiting for transfers between devices, per_device(): lax.ppermute(feat_prec, 'blk', [(i, (i + 1) % blk_size) for i in range(bl...  20.2 us
    reduce_scatter x1, waiting for transfers between devices, per_device(): heads = lax.psum_scatter(heads, 'core', scatter_dimension=3, tiled=False)  16.2 us
    dot_general x2, matrix products, per_device(): lax.dot_general(block, dir_prec, (((0,), (0,)), ((), ())), preferred_elem...  14.9 us
    dot_general x3, matrix products, embed_rows(): jnp.dot(features, weight, preferred_element_type=jnp.float32)  13.5 us
    all_to_all x1, waiting for transfers between devices, per_device(): heads = lax.all_to_all(heads, ('y', 'blk'), 0, 0, tiled=True)  12.7 us
    dot_general x2, matrix products, per_device(): lax.dot_general(coeffs, unit16_prod, (((0,), (0,)), ((), ())), preferred_...  10.8 us
    all_to_all x1, starting transfers between devices, gathered_sum(): return jnp.sum(lax.all_to_all(spread, axes, 0, 0, tiled=True), axis=0)  10.1 us
  transfers between devices with their start and end apart: 8, of which 4 were waited for; matrix products, arithmetic and copies ran while one was open for 15% of the time, Pallas kernels for 0%

profile of v12, /device:TPU:0, one launch (start us, length us, event | category | flops | bytes accessed | tf_op | source)
XLA Modules:
  0.0 199.7 jit_solution(5821869213775969050)
XLA Ops:
  7.2 2.1 %collective-permute-start.1 = (bf16[768,768]{1,0:T(8,128)(2,1)}, bf16[768,768]{1,0:T(8,128)(2,1)S(1)}, u32[]{:S(2)}, u32[]{:S(2)}) collective-permute-start(bf16[768,768]{1,0:T(8,128)(2,1)} %bitcast.47), channel_id=1, source_target_pairs={{0,1},{1,2},{2,3},{3,0},{4,5},{5,6},{6,7},{7,4},{8,9},{9,10},{10,1... | collective-permute-start | bytes 3538952 | tf_op jit(solution)/shard_map/ppermute | solution.py:51
  9.3 2.2 %collective-permute-start = (bf16[768,768]{1,0:T(8,128)(2,1)}, bf16[768,768]{1,0:T(8,128)(2,1)}, u32[]{:S(2)}, u32[]{:S(2)}) collective-permute-start(bf16[768,768]{1,0:T(8,128)(2,1)} %bitcast.48), channel_id=1, source_target_pairs={{0,3},{1,0},{2,1},{3,2},{4,7},{5,4},{6,5},{7,6},{8,11},{9,8},{10,9... | collective-permute-start | bytes 3538952 | tf_op jit(solution)/shard_map/ppermute | solution.py:50
  11.7 0.7 reduce.3
  12.4 1.3 fusion.30
  13.7 3.2 %multiply_reduce_fusion.5 = (f32[768]{0:T(1024)S(1)}, f32[768,1024]{1,0:T(8,128)S(1)}) fusion(bf16[768,1024]{1,0:T(8,128)(2,1)} %param.10, bf16[1,768,768]{2,1,0:T(8,128)(2,1)} %param.6), kind=kOutput, calls=%fused_computation.21 | convolution fusion | flops 1209531648 | bytes 5901312 | tf_op jit(solution)/shard_map/dot_general | solution.py:11
  17.4 20.2 %collective-permute-done.1 = bf16[768,768]{1,0:T(8,128)(2,1)S(1)} collective-permute-done((bf16[768,768]{1,0:T(8,128)(2,1)}, bf16[768,768]{1,0:T(8,128)(2,1)S(1)}, u32[]{:S(2)}, u32[]{:S(2)}) %collective-permute-start.1) | collective-permute-done | bytes 1179680 | tf_op jit(solution)/shard_map/ppermute | solution.py:51
  37.7 1.1 slice.17
  38.8 3.3 %collective-permute-start.3 = (bf16[384,768]{1,0:T(8,128)(2,1)S(1)}, bf16[384,768]{1,0:T(8,128)(2,1)S(1)}, u32[]{:S(2)}, u32[]{:S(2)}) collective-permute-start(bf16[384,768]{1,0:T(8,128)(2,1)S(1)} %slice.17), channel_id=1, source_target_pairs={{0,3},{1,0},{2,1},{3,2},{4,7},{5,4},{6,5},{7,6},{8,11},{9,8},{10,9... | collective-permute-start | bytes 1769480 | tf_op jit(solution)/shard_map/ppermute | solution.py:54
  42.1 8.8 %multiply_reduce_fusion.1 = (f32[2304]{0:T(1024)S(1)}, f32[2304,1024]{0,1:T(8,128)}) fusion(bf16[768,1024]{1,0:T(8,128)(2,1)S(1)} %copy-done, bf16[768,768]{1,0:T(8,128)(2,1)S(1)} %collective-permute-done.1, bf16[768,768]{1,0:T(8,128)(2,1)} %collective-permute-done, bf16[768,768]{1,0:T(8,128)(2,1)S(1)} %bitcast.49), kind=kOutput, calls=%fused_computation.2 | convolution fusion | flops 3639211776 | bytes 14558208 | tf_op jit(solution)/shard_map/dot_general | solution.py:11
  50.9 7.9 %fusion.4 = (f32[768]{0:T(1024)S(1)}, f32[768]{0:T(1024)S(1)}, f32[768,2304]{1,0:T(8,128)S(1)}) fusion(s32[2304]{0:T(1024)S(1)} %add.118, s32[768]{0:T(1024)S(1)} %reduce.3, bf16[768,1024]{1,0:T(8,128)(2,1)S(1)} %fusion.29, f32[2304,1024]{0,1:T(8,128)} %get-tuple-element.18, f32[2304]{0:T(1024)S(1)} %add_sqrt_fusion), kind=kOutput, calls=%fused_computation.11 | convolution fusion | flops 3639212544 | bytes 18115584 | tf_op jit(solution)/shard_map/dot_general | solution.py:18
  58.9 1.5 multiply_reduce_fusion.4
  60.4 1.7 fusion.14
  62.8 2.7 %fusion.3 = bf16[768,2304]{1,0:T(8,128)(2,1)S(1)} fusion(f32[768,2304]{1,0:T(8,128)S(1)} %get-tuple-element.19, f32[768]{0:T(1024)S(1)} %get-tuple-element.10, f32[768]{0:T(1024)S(1)} %get-tuple-element.7, s32[2304]{0:T(1024)S(1)} %add.118, s32[768]{0:T(1024)S(1)} %reduce.3), kind=kLoop, calls=%fused_computation.8 | loop fusion | flops 14155776 | bytes 10635264 | tf_op jit(solution)/shard_map/convert_element_type | solution.py:25
  65.5 6.4 %fusion.10 = f32[768,1024]{1,0:T(8,128)S(1)} fusion(bf16[768,2304]{1,0:T(8,128)(2,1)S(1)} %fusion.3, f32[2304,1024]{0,1:T(8,128)} %get-tuple-element.18, f32[2304]{0:T(1024)S(1)} %add_sqrt_fusion), kind=kOutput, calls=%fused_computation.29 | convolution fusion | flops 3628597248 | bytes 16131072 | tf_op jit(solution)/shard_map/dot_general | solution.py:83
  71.9 9.2 %multiply_reduce_fusion = (f32[2304]{0:T(1024)S(1)}, f32[2304,1024]{0,1:T(8,128)}) fusion(f32[2304,1024]{0,1:T(8,128)} %get-tuple-element.18, f32[2304]{0:T(1024)S(1)} %add_sqrt_fusion, bf16[768,2304]{1,0:T(8,128)(2,1)S(1)} %fusion.3, bf16[768,1024]{1,0:T(8,128)(2,1)S(1)} %fusion.29), kind=kOutput, calls=%fused_computation.1 | convolution fusion | flops 3633313536 | bytes 24004608 | tf_op jit(solution)/shard_map/dot_general | solution.py:84
  81.1 0.7 fusion.9
  81.9 1.1 copy-done.6
  83.0 1.6 multiply_reduce_fusion.2
  84.6 2.0 %multiply_reduce_fusion.3 = (f32[768]{0:T(1024)S(1)}, f32[768,1024]{1,0:T(8,128)S(1)}) fusion(f32[768,1024]{1,0:T(8,128)S(1)} %get-tuple-element.16, f32[768]{0:T(1024)S(1)} %add_sqrt_fusion.2, f32[768,1024]{1,0:T(8,128)S(1)} %fusion.10, bf16[768,768]{0,1:T(8,128)(2,1)S(1)} %fusion.9, f32[768,1024]{1,0:T(8,128)S(1)} %copy-done.6, f32[768]{0:T(1024)S(1)} %add_sqrt_fusion.1), kind=kOutput, calls=%fused_computation.18 | convolution fusion | flops 1213463808 | bytes 13771776 | tf_op jit(solution)/shard_map/dot_general | solution.py:83
  86.7 1.8 fusion.16
  88.5 3.4 %fusion.17 = f32[768,1024]{1,0:T(8,128)} fusion(bf16[768,768]{1,0:T(8,128)(2,1)S(1)} %constant_dynamic-update-slice_fusion, f32[768,1024]{1,0:T(8,128)S(1)} %get-tuple-element.24, f32[768]{0:T(1024)S(1)} %get-tuple-element.23, f32[768]{0:T(1024)S(1)} %add_sqrt_fusion.1, f32[768,1024]{1,0:T(8,128)S(1)} %copy-done.6), kind=kOutput, calls=%fused_computation.38 | convolution fusion | flops 1212678144 | bytes 10622976 | tf_op jit(solution)/shard_map/dot_general | solution.py:88
  91.9 11.5 %fusion.15 = f32[768,1024]{1,0:T(8,128)S(1)} fusion(f32[768,1024]{1,0:T(8,128)} %fusion.17, f32[2304,1024]{0,1:T(8,128)} %get-tuple-element.26, f32[2304]{0:T(1024)S(1)} %get-tuple-element.25, f32[2304]{0:T(1024)S(1)} %add_sqrt_fusion, bf16[768,768]{1,0:T(8,128)(2,1)S(1)} %collective-permute-done.1, bf16[768,768]{1,0:T(8,128)(2,1)} %collective-permute-done, ...), kind=kOutput, calls=%fused_computation.34 | convolution fusion | flops 3649437696 | bytes 28723200 | tf_op jit(solution)/shard_map/dot_general | solution.py:88
  104.0 3.2 %copy.19 = f32[2,4,4,2,24,1024]{5,4,1,0,2,3:T(8,128)} copy(f32[2,4,4,2,24,1024]{5,4,3,2,1,0:T(8,128)S(1)} %pad_maximum_fusion) | data formatting | bytes 12582912 | tf_op jit(solution)/shard_map/stack | solution.py:95
  107.3 16.2 %reduce-scatter.3.cloned.1.call-done = f32[2,4,4,1,24,1024]{5,4,1,0,2,3:T(8,128)} async-done(((f32[2,4,4,2,24,1024]{5,4,1,0,2,3:T(8,128)}), f32[2,4,4,1,24,1024]{5,4,1,0,2,3:T(8,128)}) %reduce-scatter.3.cloned.1.call-update) | async-done | bytes 3145744 | tf_op jit(solution)/shard_map/reduce_scatter | solution.py:101
  123.5 1.5 pad_maximum_fusion.4
  125.6 10.1 %all-to-all-start = ((f32[128,1,2]{2,1,0:T(1,128)}), f32[128,1,2]{2,1,0:T(1,128)S(1)}, u32[]{:S(2)}, u32[]{:S(2)}) async-start(f32[128,1,2]{2,1,0:T(1,128)} %broadcast_in_dim.12), calls=%async_computation | async-start | bytes 131072 | tf_op jit(solution)/shard_map/all_to_all | solution.py:39
  135.7 30.2 %reduce-scatter.5.cloned.1.call-done = f32[2,4,1,24,1024]{4,3,1,0,2:T(8,128)} async-done(((f32[2,4,4,24,1024]{4,3,1,0,2:T(8,128)}), f32[2,4,1,24,1024]{4,3,1,0,2:T(8,128)}) %reduce-scatter.5.cloned.1.call-update) | async-done | bytes 786448 | tf_op jit(solution)/shard_map/reduce_scatter | solution.py:102
  165.9 1.5 reshape_reduce_scatter.3
  167.4 1.0 copy.18
  168.4 7.2 %all-to-all-start.1 = ((f32[16,2,24,256]{3,2,1,0:T(8,128)}), f32[16,2,24,256]{3,2,1,0:T(8,128)S(1)}, u32[]{:S(2)}, u32[]{:S(2)}) async-start(f32[16,2,24,256]{3,2,1,0:T(8,128)} %bitcast.14), calls=%async_computation.3 | async-start | bytes 1572864 | tf_op jit(solution)/shard_map/all_to_all | solution.py:106
  177.7 12.7 %all-to-all-done.1 = f32[16,2,24,256]{3,2,1,0:T(8,128)S(1)} async-done(((f32[16,2,24,256]{3,2,1,0:T(8,128)}), f32[16,2,24,256]{3,2,1,0:T(8,128)S(1)}, u32[]{:S(2)}, u32[]{:S(2)}) %all-to-all-start.1) | async-done | bytes 786464 | tf_op jit(solution)/shard_map/all_to_all | solution.py:106
  190.5 0.7 broadcast_divide_fusion.3
  (40 shorter events, 4.2 us)
Async XLA Ops:
  7.2 35.0 %copy-start = (bf16[768,1024]{1,0:T(8,128)(2,1)S(1)}, bf16[768,1024]{1,0:T(8,128)(2,1)}, u32[]{:S(2)}) copy-start(bf16[768,1024]{1,0:T(8,128)(2,1)} %param.11) | copy-start | bytes 4718596
  7.2 116.2 %reduce-scatter.3.cloned.1.call-start = ((), (), s32[]{:S(2)}) async-start(), calls=%async_computation.4 | async-start | bytes 9437184 | tf_op jit(solution)/shard_map/reduce_scatter | solution.py:101
  7.2 30.4 %collective-permute-start.1 = (bf16[768,768]{1,0:T(8,128)(2,1)}, bf16[768,768]{1,0:T(8,128)(2,1)S(1)}, u32[]{:S(2)}, u32[]{:S(2)}) collective-permute-start(bf16[768,768]{1,0:T(8,128)(2,1)} %bitcast.47), channel_id=1, source_target_pairs={{0,1},{1,2},{2,3},{3,0},{4,5},{5,6},{6,7},{7,4},{8,9},{9,10},{10,1... | collective-permute-start | bytes 3538952 | tf_op jit(solution)/shard_map/ppermute | solution.py:51
  9.3 28.4 %collective-permute-start = (bf16[768,768]{1,0:T(8,128)(2,1)}, bf16[768,768]{1,0:T(8,128)(2,1)}, u32[]{:S(2)}, u32[]{:S(2)}) collective-permute-start(bf16[768,768]{1,0:T(8,128)(2,1)} %bitcast.48), channel_id=1, source_target_pairs={{0,3},{1,0},{2,1},{3,2},{4,7},{5,4},{6,5},{7,6},{8,11},{9,8},{10,9... | collective-permute-start | bytes 3538952 | tf_op jit(solution)/shard_map/ppermute | solution.py:50
  16.9 25.2 %copy-start.3 = (bf16[1,768,768]{2,1,0:T(8,128)(2,1)S(1)}, bf16[1,768,768]{2,1,0:T(8,128)(2,1)}, u32[]{:S(2)}) copy-start(bf16[1,768,768]{2,1,0:T(8,128)(2,1)} %param.7) | copy-start | bytes 3538948
  37.6 21.2 %collective-permute-start.2 = (bf16[384,768]{1,0:T(8,128)(2,1)S(1)}, bf16[384,768]{1,0:T(8,128)(2,1)S(1)}, u32[]{:S(2)}, u32[]{:S(2)}) collective-permute-start(bf16[384,768]{1,0:T(8,128)(2,1)S(1)} %slice.16), channel_id=1, source_target_pairs={{0,1},{1,2},{2,3},{3,0},{4,5},{5,6},{6,7},{7,4},{8,9},{9,10},{10,1... | collective-permute-start | bytes 1769480 | tf_op jit(solution)/shard_map/ppermute | solution.py:53
  38.8 20.0 %collective-permute-start.3 = (bf16[384,768]{1,0:T(8,128)(2,1)S(1)}, bf16[384,768]{1,0:T(8,128)(2,1)S(1)}, u32[]{:S(2)}, u32[]{:S(2)}) collective-permute-start(bf16[384,768]{1,0:T(8,128)(2,1)S(1)} %slice.17), channel_id=1, source_target_pairs={{0,3},{1,0},{2,1},{3,2},{4,7},{5,4},{6,5},{7,6},{8,11},{9,8},{10,9... | collective-permute-start | bytes 1769480 | tf_op jit(solution)/shard_map/ppermute | solution.py:54
  60.4 1.7 copy-start.5
  81.1 1.9 copy-start.6
  84.6 2.0 %copy-start.2 = (bf16[1,768,768]{2,1,0:T(8,128)(2,1)S(1)}, bf16[1,768,768]{2,1,0:T(8,128)(2,1)}, u32[]{:S(2)}) copy-start(bf16[1,768,768]{2,1,0:T(8,128)(2,1)} %param.6) | copy-start | bytes 3538948
  88.5 3.4 %copy-start.4 = (bf16[1,768,768]{2,1,0:T(8,128)(2,1)S(1)}, bf16[1,768,768]{2,1,0:T(8,128)(2,1)}, u32[]{:S(2)}) copy-start(bf16[1,768,768]{2,1,0:T(8,128)(2,1)} %param.7) | copy-start | bytes 3538948
  107.2 58.7 %reduce-scatter.5.cloned.1.call-start = ((), (), s32[]{:S(2)}) async-start(), calls=%async_computation.5 | async-start | bytes 3932160 | tf_op jit(solution)/shard_map/reduce_scatter | solution.py:102
  123.4 68.3 %copy-start.1 = (bf16[768,1024]{1,0:T(8,128)(2,1)S(1)}, bf16[768,1024]{1,0:T(8,128)(2,1)}, u32[]{:S(2)}) copy-start(bf16[768,1024]{1,0:T(8,128)(2,1)} %param.11) | copy-start | bytes 4718596
  125.6 42.8 %all-to-all-start = ((f32[128,1,2]{2,1,0:T(1,128)}), f32[128,1,2]{2,1,0:T(1,128)S(1)}, u32[]{:S(2)}, u32[]{:S(2)}) async-start(f32[128,1,2]{2,1,0:T(1,128)} %broadcast_in_dim.12), calls=%async_computation | async-start | bytes 131072 | tf_op jit(solution)/shard_map/all_to_all | solution.py:39
  168.4 22.0 %all-to-all-start.1 = ((f32[16,2,24,256]{3,2,1,0:T(8,128)}), f32[16,2,24,256]{3,2,1,0:T(8,128)S(1)}, u32[]{:S(2)}, u32[]{:S(2)}) async-start(f32[16,2,24,256]{3,2,1,0:T(8,128)} %bitcast.14), calls=%async_computation.3 | async-start | bytes 1572864 | tf_op jit(solution)/shard_map/all_to_all | solution.py:106
Sparse Core Ops, SparseCore 0:
  107.3 16.0 reduce-scatter.2
  126.0 39.8 reduce-scatter.4

commit v13 on v9

--- a/solution.py
+++ b/solution.py
@@ -86,13 +86,13 @@
         )
         dir_prec = back_norm(unit_prec, radius_prec, grad_prec_part)
         head_prec = head_prec + lax.dot_general(
-            block, dir_prec, (((0,), (0,)), ((), ())), preferred_element_type=jnp.float32
+            dir_prec, block, (((0,), (0,)), ((), ())), preferred_element_type=jnp.float32
         )
     dir_prod = back_norm(unit_prod, radius_prod, LOGIT_SCALE * grad_unit_prod)
     head_prod = lax.dot_general(
         feat_prod, dir_prod, (((0,), (0,)), ((), ())), preferred_element_type=jnp.float32
     )
-    heads = jnp.stack([head_prod, head_prec])
+    heads = jnp.stack([head_prod, head_prec.T])
     feat, embed = head_prod.shape
     y_size = lax.axis_size("y")
     x_size = lax.axis_size("x")

time: 199 us -> 199 us (level)
  no operation moved by 1% of the time
where the time goes in v13:
time: 199 us
  waiting for transfers between devices  79.3 us (40%)
  matrix products  59.7 us (30%)
  starting transfers between devices  25 us (13%)
  between operations  16.7 us (8%)
  local copies, waits for them, and re-layouts  8.86 us (4%)
  other arithmetic  8.85 us (4%)
    reduce_scatter x1, waiting for transfers between devices, per_device(): heads = lax.psum_scatter(heads, 'x', scatter_dimension=2, tiled=False)  30.2 us
    ppermute x1, waiting for transfers between devices, per_device(): lax.ppermute(feat_prec, 'blk', [(i, (i + 1) % blk_size) for i in range(bl...  20.2 us
    reduce_scatter x1, waiting for transfers between devices, per_device(): heads = lax.psum_scatter(heads, 'core', scatter_dimension=3, tiled=False)  16.1 us
    dot_general x2, matrix products, per_device(): lax.dot_general(dir_prec, block, (((0,), (0,)), ((), ())), preferred_elem...  15 us
    dot_general x3, matrix products, embed_rows(): jnp.dot(features, weight, preferred_element_type=jnp.float32)  13.5 us
    all_to_all x1, waiting for transfers between devices, per_device(): heads = lax.all_to_all(heads, ('y', 'blk'), 0, 0, tiled=True)  12.7 us
    dot_general x2, matrix products, per_device(): lax.dot_general(coeffs, unit16_prod, (((0,), (0,)), ((), ())), preferred_...  11 us
    all_to_all x1, starting transfers between devices, gathered_sum(): return jnp.sum(lax.all_to_all(spread, axes, 0, 0, tiled=True), axis=0)  10.1 us
  transfers between devices with their start and end apart: 8, of which 4 were waited for; matrix products, arithmetic and copies ran while one was open for 15% of the time, Pallas kernels for 0%

profile of v13, /device:TPU:0, one launch (start us, length us, event | category | flops | bytes accessed | tf_op | source)
XLA Modules:
  0.0 198.5 jit_solution(15668455144524704192)
XLA Ops:
  7.2 2.1 %collective-permute-start.1 = (bf16[768,768]{1,0:T(8,128)(2,1)}, bf16[768,768]{1,0:T(8,128)(2,1)S(1)}, u32[]{:S(2)}, u32[]{:S(2)}) collective-permute-start(bf16[768,768]{1,0:T(8,128)(2,1)} %bitcast.45), channel_id=1, source_target_pairs={{0,1},{1,2},{2,3},{3,0},{4,5},{5,6},{6,7},{7,4},{8,9},{9,10},{10,1... | collective-permute-start | bytes 3538952 | tf_op jit(solution)/shard_map/ppermute | solution.py:51
  9.3 2.2 %collective-permute-start = (bf16[768,768]{1,0:T(8,128)(2,1)}, bf16[768,768]{1,0:T(8,128)(2,1)}, u32[]{:S(2)}, u32[]{:S(2)}) collective-permute-start(bf16[768,768]{1,0:T(8,128)(2,1)} %bitcast.46), channel_id=1, source_target_pairs={{0,3},{1,0},{2,1},{3,2},{4,7},{5,4},{6,5},{7,6},{8,11},{9,8},{10,9... | collective-permute-start | bytes 3538952 | tf_op jit(solution)/shard_map/ppermute | solution.py:50
  11.7 0.7 reduce.3
  12.4 1.3 fusion.33
  13.7 3.2 %multiply_reduce_fusion.5 = (f32[768]{0:T(1024)S(1)}, f32[768,1024]{1,0:T(8,128)S(1)}) fusion(bf16[768,1024]{1,0:T(8,128)(2,1)} %param.10, bf16[1,768,768]{2,1,0:T(8,128)(2,1)} %param.6), kind=kOutput, calls=%fused_computation.21 | convolution fusion | flops 1209531648 | bytes 5901312 | tf_op jit(solution)/shard_map/dot_general | solution.py:11
  17.4 20.2 %collective-permute-done.1 = bf16[768,768]{1,0:T(8,128)(2,1)S(1)} collective-permute-done((bf16[768,768]{1,0:T(8,128)(2,1)}, bf16[768,768]{1,0:T(8,128)(2,1)S(1)}, u32[]{:S(2)}, u32[]{:S(2)}) %collective-permute-start.1) | collective-permute-done | bytes 1179680 | tf_op jit(solution)/shard_map/ppermute | solution.py:51
  37.7 1.1 slice.17
  38.8 3.3 %collective-permute-start.3 = (bf16[384,768]{1,0:T(8,128)(2,1)S(1)}, bf16[384,768]{1,0:T(8,128)(2,1)S(1)}, u32[]{:S(2)}, u32[]{:S(2)}) collective-permute-start(bf16[384,768]{1,0:T(8,128)(2,1)S(1)} %slice.17), channel_id=1, source_target_pairs={{0,3},{1,0},{2,1},{3,2},{4,7},{5,4},{6,5},{7,6},{8,11},{9,8},{10,9... | collective-permute-start | bytes 1769480 | tf_op jit(solution)/shard_map/ppermute | solution.py:54
  42.1 8.8 %multiply_reduce_fusion.1 = (f32[2304]{0:T(1024)S(1)}, f32[2304,1024]{0,1:T(8,128)}) fusion(bf16[768,1024]{1,0:T(8,128)(2,1)S(1)} %copy-done, bf16[768,768]{1,0:T(8,128)(2,1)S(1)} %collective-permute-done.1, bf16[768,768]{1,0:T(8,128)(2,1)} %collective-permute-done, bf16[768,768]{1,0:T(8,128)(2,1)S(1)} %bitcast.47), kind=kOutput, calls=%fused_computation.2 | convolution fusion | flops 3639211776 | bytes 14558208 | tf_op jit(solution)/shard_map/dot_general | solution.py:11
  50.9 7.9 %fusion.4 = (f32[768]{0:T(1024)S(1)}, f32[768]{0:T(1024)S(1)}, f32[768,2304]{1,0:T(8,128)S(1)}) fusion(s32[2304]{0:T(1024)S(1)} %add.119, s32[768]{0:T(1024)S(1)} %reduce.3, bf16[768,1024]{1,0:T(8,128)(2,1)S(1)} %fusion.29, f32[2304,1024]{0,1:T(8,128)} %get-tuple-element.18, f32[2304]{0:T(1024)S(1)} %add_sqrt_fusion), kind=kOutput, calls=%fused_computation.11 | convolution fusion | flops 3639212544 | bytes 18115584 | tf_op jit(solution)/shard_map/dot_general | solution.py:18
  58.9 1.5 multiply_reduce_fusion.4
  60.4 1.8 fusion.14
  62.8 2.7 %fusion.3 = bf16[768,2304]{1,0:T(8,128)(2,1)S(1)} fusion(f32[768,2304]{1,0:T(8,128)S(1)} %get-tuple-element.19, f32[768]{0:T(1024)S(1)} %get-tuple-element.10, f32[768]{0:T(1024)S(1)} %get-tuple-element.7, s32[2304]{0:T(1024)S(1)} %add.119, s32[768]{0:T(1024)S(1)} %reduce.3), kind=kLoop, calls=%fused_computation.8 | loop fusion | flops 14155776 | bytes 10635264 | tf_op jit(solution)/shard_map/convert_element_type | solution.py:25
  65.5 6.4 %fusion.10 = f32[768,1024]{1,0:T(8,128)S(1)} fusion(bf16[768,2304]{1,0:T(8,128)(2,1)S(1)} %fusion.3, f32[2304,1024]{0,1:T(8,128)} %get-tuple-element.18, f32[2304]{0:T(1024)S(1)} %add_sqrt_fusion), kind=kOutput, calls=%fused_computation.29 | convolution fusion | flops 3628597248 | bytes 16131072 | tf_op jit(solution)/shard_map/dot_general | solution.py:83
  72.0 9.2 %multiply_reduce_fusion = (f32[2304]{0:T(1024)S(1)}, f32[2304,1024]{0,1:T(8,128)}) fusion(f32[2304,1024]{0,1:T(8,128)} %get-tuple-element.18, f32[2304]{0:T(1024)S(1)} %add_sqrt_fusion, bf16[768,2304]{1,0:T(8,128)(2,1)S(1)} %fusion.3, bf16[768,1024]{1,0:T(8,128)(2,1)S(1)} %fusion.29), kind=kOutput, calls=%fused_computation.1 | convolution fusion | flops 3633313536 | bytes 24004608 | tf_op jit(solution)/shard_map/dot_general | solution.py:84
  81.2 1.8 multiply_reduce_fusion.2
  83.0 2.3 %multiply_reduce_fusion.3 = (f32[768]{0:T(1024)S(1)}, f32[768,1024]{1,0:T(8,128)S(1)}) fusion(f32[768,1024]{1,0:T(8,128)S(1)} %get-tuple-element.16, f32[768]{0:T(1024)S(1)} %add_sqrt_fusion.2, f32[768,1024]{1,0:T(8,128)S(1)} %fusion.10, f32[768,1024]{1,0:T(8,128)S(1)} %get-tuple-element.21, f32[768]{0:T(1024)S(1)} %add_sqrt_fusion.1, ...), kind=kOutput, calls=%fused_computation.18 | convolution fusion | flops 1218182400 | bytes 14963712 | tf_op jit(solution)/shard_map/dot_general | solution.py:83
  85.3 1.8 fusion.16
  87.2 3.4 %fusion.17 = f32[768,1024]{1,0:T(8,128)} fusion(bf16[768,768]{1,0:T(8,128)(2,1)S(1)} %constant_dynamic-update-slice_fusion, f32[768,1024]{1,0:T(8,128)S(1)} %get-tuple-element.24, f32[768]{0:T(1024)S(1)} %get-tuple-element.23, f32[768]{0:T(1024)S(1)} %add_sqrt_fusion.1, f32[768,1024]{1,0:T(8,128)S(1)} %get-tuple-element.21), kind=kOutput, calls=%fused_computation.38 | convolution fusion | flops 1212678144 | bytes 10622976 | tf_op jit(solution)/shard_map/dot_general | solution.py:88
  90.6 11.6 %fusion.15 = f32[768,1024]{1,0:T(8,128)S(1)} fusion(f32[768,1024]{1,0:T(8,128)} %fusion.17, f32[2304,1024]{0,1:T(8,128)} %get-tuple-element.26, f32[2304]{0:T(1024)S(1)} %get-tuple-element.25, f32[2304]{0:T(1024)S(1)} %add_sqrt_fusion, bf16[768,768]{1,0:T(8,128)(2,1)S(1)} %collective-permute-done.1, bf16[768,768]{1,0:T(8,128)(2,1)} %collective-permute-done, ...), kind=kOutput, calls=%fused_computation.34 | convolution fusion | flops 3649437696 | bytes 28723200 | tf_op jit(solution)/shard_map/dot_general | solution.py:88
  102.7 3.2 %copy.19 = f32[2,4,4,2,24,1024]{5,4,1,0,2,3:T(8,128)} copy(f32[2,4,4,2,24,1024]{5,4,3,2,1,0:T(8,128)S(1)} %pad_maximum_fusion) | data formatting | bytes 12582912 | tf_op jit(solution)/shard_map/stack | solution.py:95
  106.1 16.1 %reduce-scatter.3.cloned.1.call-done = f32[2,4,4,1,24,1024]{5,4,1,0,2,3:T(8,128)} async-done(((f32[2,4,4,2,24,1024]{5,4,1,0,2,3:T(8,128)}), f32[2,4,4,1,24,1024]{5,4,1,0,2,3:T(8,128)}) %reduce-scatter.3.cloned.1.call-update) | async-done | bytes 3145744 | tf_op jit(solution)/shard_map/reduce_scatter | solution.py:101
  122.2 1.5 pad_maximum_fusion.4
  123.7 0.7 broadcast_in_dim.12
  124.4 10.1 %all-to-all-start = ((f32[128,1,2]{2,1,0:T(1,128)}), f32[128,1,2]{2,1,0:T(1,128)S(1)}, u32[]{:S(2)}, u32[]{:S(2)}) async-start(f32[128,1,2]{2,1,0:T(1,128)} %broadcast_in_dim.12), calls=%async_computation | async-start | bytes 131072 | tf_op jit(solution)/shard_map/all_to_all | solution.py:39
  134.5 30.2 %reduce-scatter.5.cloned.1.call-done = f32[2,4,1,24,1024]{4,3,1,0,2:T(8,128)} async-done(((f32[2,4,4,24,1024]{4,3,1,0,2:T(8,128)}), f32[2,4,1,24,1024]{4,3,1,0,2:T(8,128)}) %reduce-scatter.5.cloned.1.call-update) | async-done | bytes 786448 | tf_op jit(solution)/shard_map/reduce_scatter | solution.py:102
  164.7 1.5 reshape_reduce_scatter.3
  166.2 1.0 copy.18
  167.2 7.2 %all-to-all-start.1 = ((f32[16,2,24,256]{3,2,1,0:T(8,128)}), f32[16,2,24,256]{3,2,1,0:T(8,128)S(1)}, u32[]{:S(2)}, u32[]{:S(2)}) async-start(f32[16,2,24,256]{3,2,1,0:T(8,128)} %bitcast.14), calls=%async_computation.3 | async-start | bytes 1572864 | tf_op jit(solution)/shard_map/all_to_all | solution.py:106
  176.5 12.7 %all-to-all-done.1 = f32[16,2,24,256]{3,2,1,0:T(8,128)S(1)} async-done(((f32[16,2,24,256]{3,2,1,0:T(8,128)}), f32[16,2,24,256]{3,2,1,0:T(8,128)S(1)}, u32[]{:S(2)}, u32[]{:S(2)}) %all-to-all-start.1) | async-done | bytes 786464 | tf_op jit(solution)/shard_map/all_to_all | solution.py:106
  189.3 0.7 broadcast_divide_fusion.3
  189.9 0.6 slice_bitcast_fusion
  (33 shorter events, 2.9 us)
Async XLA Ops:
  7.2 35.0 %copy-start = (bf16[768,1024]{1,0:T(8,128)(2,1)S(1)}, bf16[768,1024]{1,0:T(8,128)(2,1)}, u32[]{:S(2)}) copy-start(bf16[768,1024]{1,0:T(8,128)(2,1)} %param.11) | copy-start | bytes 4718596
  7.2 115.0 %reduce-scatter.3.cloned.1.call-start = ((), (), s32[]{:S(2)}) async-start(), calls=%async_computation.4 | async-start | bytes 9437184 | tf_op jit(solution)/shard_map/reduce_scatter | solution.py:101
  7.2 30.4 %collective-permute-start.1 = (bf16[768,768]{1,0:T(8,128)(2,1)}, bf16[768,768]{1,0:T(8,128)(2,1)S(1)}, u32[]{:S(2)}, u32[]{:S(2)}) collective-permute-start(bf16[768,768]{1,0:T(8,128)(2,1)} %bitcast.45), channel_id=1, source_target_pairs={{0,1},{1,2},{2,3},{3,0},{4,5},{5,6},{6,7},{7,4},{8,9},{9,10},{10,1... | collective-permute-start | bytes 3538952 | tf_op jit(solution)/shard_map/ppermute | solution.py:51
  9.3 28.4 %collective-permute-start = (bf16[768,768]{1,0:T(8,128)(2,1)}, bf16[768,768]{1,0:T(8,128)(2,1)}, u32[]{:S(2)}, u32[]{:S(2)}) collective-permute-start(bf16[768,768]{1,0:T(8,128)(2,1)} %bitcast.46), channel_id=1, source_target_pairs={{0,3},{1,0},{2,1},{3,2},{4,7},{5,4},{6,5},{7,6},{8,11},{9,8},{10,9... | collective-permute-start | bytes 3538952 | tf_op jit(solution)/shard_map/ppermute | solution.py:50
  16.9 25.2 %copy-start.3 = (bf16[1,768,768]{2,1,0:T(8,128)(2,1)S(1)}, bf16[1,768,768]{2,1,0:T(8,128)(2,1)}, u32[]{:S(2)}) copy-start(bf16[1,768,768]{2,1,0:T(8,128)(2,1)} %param.7) | copy-start | bytes 3538948
  37.6 21.2 %collective-permute-start.2 = (bf16[384,768]{1,0:T(8,128)(2,1)S(1)}, bf16[384,768]{1,0:T(8,128)(2,1)S(1)}, u32[]{:S(2)}, u32[]{:S(2)}) collective-permute-start(bf16[384,768]{1,0:T(8,128)(2,1)S(1)} %slice.16), channel_id=1, source_target_pairs={{0,1},{1,2},{2,3},{3,0},{4,5},{5,6},{6,7},{7,4},{8,9},{9,10},{10,1... | collective-permute-start | bytes 1769480 | tf_op jit(solution)/shard_map/ppermute | solution.py:53
  38.8 20.0 %collective-permute-start.3 = (bf16[384,768]{1,0:T(8,128)(2,1)S(1)}, bf16[384,768]{1,0:T(8,128)(2,1)S(1)}, u32[]{:S(2)}, u32[]{:S(2)}) collective-permute-start(bf16[384,768]{1,0:T(8,128)(2,1)S(1)} %slice.17), channel_id=1, source_target_pairs={{0,3},{1,0},{2,1},{3,2},{4,7},{5,4},{6,5},{7,6},{8,11},{9,8},{10,9... | collective-permute-start | bytes 1769480 | tf_op jit(solution)/shard_map/ppermute | solution.py:54
  83.0 2.3 %copy-start.2 = (bf16[1,768,768]{2,1,0:T(8,128)(2,1)S(1)}, bf16[1,768,768]{2,1,0:T(8,128)(2,1)}, u32[]{:S(2)}) copy-start(bf16[1,768,768]{2,1,0:T(8,128)(2,1)} %param.6) | copy-start | bytes 3538948
  106.0 58.7 %reduce-scatter.5.cloned.1.call-start = ((), (), s32[]{:S(2)}) async-start(), calls=%async_computation.5 | async-start | bytes 3932160 | tf_op jit(solution)/shard_map/reduce_scatter | solution.py:102
  122.2 68.3 %copy-start.1 = (bf16[768,1024]{1,0:T(8,128)(2,1)S(1)}, bf16[768,1024]{1,0:T(8,128)(2,1)}, u32[]{:S(2)}) copy-start(bf16[768,1024]{1,0:T(8,128)(2,1)} %param.11) | copy-start | bytes 4718596
  124.4 42.8 %all-to-all-start = ((f32[128,1,2]{2,1,0:T(1,128)}), f32[128,1,2]{2,1,0:T(1,128)S(1)}, u32[]{:S(2)}, u32[]{:S(2)}) async-start(f32[128,1,2]{2,1,0:T(1,128)} %broadcast_in_dim.12), calls=%async_computation | async-start | bytes 131072 | tf_op jit(solution)/shard_map/all_to_all | solution.py:39
  167.2 22.0 %all-to-all-start.1 = ((f32[16,2,24,256]{3,2,1,0:T(8,128)}), f32[16,2,24,256]{3,2,1,0:T(8,128)S(1)}, u32[]{:S(2)}, u32[]{:S(2)}) async-start(f32[16,2,24,256]{3,2,1,0:T(8,128)} %bitcast.14), calls=%async_computation.3 | async-start | bytes 1572864 | tf_op jit(solution)/shard_map/all_to_all | solution.py:106
Sparse Core Ops, SparseCore 0:
  106.1 16.0 reduce-scatter.2
  124.7 39.8 reduce-scatter.4

commit v14 on v13

--- a/solution.py
+++ b/solution.py
@@ -75,24 +75,26 @@
     weight_local = jnp.sum(weights)
     loss_sum, weight_total = gathered_sum(jnp.stack([loss_local, weight_local]))
     grad_unit_prod = 0.0
-    head_prec = 0.0
-    for block, (unit_prec, unit16_prec, radius_prec), block_scores, block_matches in zip(
-        blocks, embedded, scores, matches
-    ):
+    dirs_prec = []
+    for (unit_prec, unit16_prec, radius_prec), block_scores, block_matches in zip(embedded, scores, matches):
         coeffs = coefficient(block_scores, block_matches, weights, totals)
         grad_unit_prod = grad_unit_prod + jnp.dot(coeffs, unit16_prec, preferred_element_type=jnp.float32)
         grad_prec_part = LOGIT_SCALE * lax.dot_general(
             coeffs, unit16_prod, (((0,), (0,)), ((), ())), preferred_element_type=jnp.float32
         )
-        dir_prec = back_norm(unit_prec, radius_prec, grad_prec_part)
-        head_prec = head_prec + lax.dot_general(
-            dir_prec, block, (((0,), (0,)), ((), ())), preferred_element_type=jnp.float32
-        )
+        dirs_prec.append(back_norm(unit_prec, radius_prec, grad_prec_part))
     dir_prod = back_norm(unit_prod, radius_prod, LOGIT_SCALE * grad_unit_prod)
-    head_prod = lax.dot_general(
-        feat_prod, dir_prod, (((0,), (0,)), ((), ())), preferred_element_type=jnp.float32
+    heads = lax.dot_general(
+        jnp.stack([feat_prod, opposite]),
+        jnp.stack([dir_prod, dirs_prec[1]]),
+        (((1,), (1,)), ((0,), (0,))),
+        preferred_element_type=jnp.float32,
     )
-    heads = jnp.stack([head_prod, head_prec.T])
+    near_head = lax.dot_general(
+        dirs_prec[0], near, (((0,), (0,)), ((), ())), preferred_element_type=jnp.float32
+    )
+    heads = heads + jnp.stack([jnp.zeros_like(near_head.T), near_head.T])
+    head_prod = heads[0]
     feat, embed = head_prod.shape
     y_size = lax.axis_size("y")
     x_size = lax.axis_size("x")

time: 199 us -> 201 us (1.010)
  local copies, waits for them, and re-layouts: 8.86 us -> 14 us
  matrix products: 59.7 us -> 56.4 us
    dot_general x3 -> x2, matrix products: 16.8 us -> 11.9 us  [the longest x1 9.31 us: per_device(): lax.dot_general(dirs_prec[0], near, (((0,), (0,)), ((), ())), preferred_e...]
    unnamed x9 -> x17, local copies, waits for them, and re-layouts: 0.07 us -> 4.07 us
    reshape x0 -> x1, local copies, waits for them, and re-layouts: none -> 3.24 us  [per_device(): heads.reshape(2, y_size, x_size, core_size, feat // (y_size * x_size * co...]
    another operation x1 -> x0, local copies, waits for them, and re-layouts: 3.24 us -> none  [per_device(): heads = jnp.stack([head_prod, head_prec.T])]
where the time goes in v14:
time: 201 us; the launch traced here: 200 us
  waiting for transfers between devices  79.1 us (39%)
  matrix products  56.4 us (28%)
  starting transfers between devices  24.8 us (12%)
  between operations  16.8 us (8%)
  local copies, waits for them, and re-layouts  14 us (7%)
  other arithmetic  8.93 us (4%)
    reduce_scatter x1, waiting for transfers between devices, per_device(): heads = lax.psum_scatter(heads, 'x', scatter_dimension=2, tiled=False)  30.2 us
    ppermute x1, waiting for transfers between devices, per_device(): lax.ppermute(feat_prec, 'blk', [(i, (i + 1) % blk_size) for i in range(bl...  20 us
    reduce_scatter x1, waiting for transfers between devices, per_device(): heads = lax.psum_scatter(heads, 'core', scatter_dimension=3, tiled=False)  16.1 us
    dot_general x3, matrix products, embed_rows(): jnp.dot(features, weight, preferred_element_type=jnp.float32)  13.5 us
    all_to_all x1, waiting for transfers between devices, per_device(): heads = lax.all_to_all(heads, ('y', 'blk'), 0, 0, tiled=True)  12.7 us
    dot_general x2, matrix products, per_device(): lax.dot_general(coeffs, unit16_prod, (((0,), (0,)), ((), ())), preferred_...  11.1 us
    dot_general x2, matrix products, similarity(): lax.dot_general(queries, key_rows, (((1,), (1,)), ((), ())), preferred_el...  11 us
    all_to_all x1, starting transfers between devices, gathered_sum(): return jnp.sum(lax.all_to_all(spread, axes, 0, 0, tiled=True), axis=0)  10.1 us
  transfers between devices with their start and end apart: 8, of which 4 were waited for; matrix products, arithmetic and copies ran while one was open for 15% of the time, Pallas kernels for 0%

profile of v14, /device:TPU:0, one launch (start us, length us, event | category | flops | bytes accessed | tf_op | source)
XLA Modules:
  0.0 200.1 jit_solution(16628602190981244076)
XLA Ops:
  7.2 2.5 %copy.21 = bf16[1,768,768]{1,2,0:T(8,128)(2,1)} copy(bf16[1,768,768]{2,1,0:T(8,128)(2,1)} %param.7) | data formatting | bytes 2359296 | tf_op args[1]
  9.8 2.0 collective-permute-start.1
  11.8 2.1 %collective-permute-start = (bf16[768,768]{0,1:T(8,128)(2,1)}, bf16[768,768]{0,1:T(8,128)(2,1)}, u32[]{:S(2)}, u32[]{:S(2)}) collective-permute-start(bf16[768,768]{0,1:T(8,128)(2,1)} %bitcast.46), channel_id=1, source_target_pairs={{0,3},{1,0},{2,1},{3,2},{4,7},{5,4},{6,5},{7,6},{8,11},{9,8},{10,9... | collective-permute-start | bytes 3538952 | tf_op jit(solution)/shard_map/ppermute | solution.py:50
  14.0 0.7 reduce.3
  14.8 1.4 copy.23
  16.8 2.9 %multiply_reduce_fusion.5 = (f32[768]{0:T(1024)S(1)}, f32[768,1024]{1,0:T(8,128)S(1)}) fusion(bf16[768,1024]{1,0:T(8,128)(2,1)} %param.10, bf16[1,768,768]{2,1,0:T(8,128)(2,1)S(1)} %copy-done.2), kind=kOutput, calls=%fused_computation.25 | convolution fusion | flops 1209531648 | bytes 5901312 | tf_op jit(solution)/shard_map/dot_general | solution.py:11
  20.2 20.0 %collective-permute-done.1 = bf16[768,768]{0,1:T(8,128)(2,1)} collective-permute-done((bf16[768,768]{0,1:T(8,128)(2,1)}, bf16[768,768]{0,1:T(8,128)(2,1)}, u32[]{:S(2)}, u32[]{:S(2)}) %collective-permute-start.1) | collective-permute-done | bytes 1179680 | tf_op jit(solution)/shard_map/ppermute | solution.py:51
  40.2 1.1 slice.16
  41.4 1.1 slice.17
  42.5 3.3 %collective-permute-start.3 = (bf16[384,768]{0,1:T(8,128)(2,1)S(1)}, bf16[384,768]{0,1:T(8,128)(2,1)S(1)}, u32[]{:S(2)}, u32[]{:S(2)}) collective-permute-start(bf16[384,768]{0,1:T(8,128)(2,1)S(1)} %slice.17), channel_id=1, source_target_pairs={{0,3},{1,0},{2,1},{3,2},{4,7},{5,4},{6,5},{7,6},{8,11},{9,8},{10,9... | collective-permute-start | bytes 1769480 | tf_op jit(solution)/shard_map/ppermute | solution.py:54
  45.8 9.1 %multiply_reduce_fusion.1 = (f32[2304]{0:T(1024)S(1)}, f32[2304,1024]{0,1:T(8,128)}) fusion(bf16[768,1024]{1,0:T(8,128)(2,1)S(1)} %copy-done, bf16[768,768]{0,1:T(8,128)(2,1)} %collective-permute-done.1, bf16[768,768]{0,1:T(8,128)(2,1)} %collective-permute-done, bf16[768,768]{0,1:T(8,128)(2,1)S(1)} %bitcast.47), kind=kOutput, calls=%fused_computation.2 | convolution fusion | flops 3639211776 | bytes 14558208 | tf_op jit(solution)/shard_map/dot_general | solution.py:11
  55.0 7.9 %fusion.4 = (f32[768]{0:T(1024)S(1)}, f32[768]{0:T(1024)S(1)}, f32[768,2304]{1,0:T(8,128)S(1)}) fusion(s32[2304]{0:T(1024)S(1)} %add.120, s32[768]{0:T(1024)S(1)} %reduce.3, bf16[768,1024]{1,0:T(8,128)(2,1)S(1)} %fusion.39, f32[2304,1024]{0,1:T(8,128)} %get-tuple-element.18, f32[2304]{0:T(1024)S(1)} %add_sqrt_fusion), kind=kOutput, calls=%fused_computation.11 | convolution fusion | flops 3639212544 | bytes 18115584 | tf_op jit(solution)/shard_map/dot_general | solution.py:18
  63.0 1.5 multiply_reduce_fusion.4
  64.6 3.1 %fusion.25 = (f32[768]{0:T(1024)S(1)}, f32[768]{0:T(1024)S(1)}, f32[768,768]{0,1:T(8,128)}) fusion(s32[768]{0:T(1024)S(1)} %iota_add_fusion.1, s32[768]{0:T(1024)S(1)} %reduce.3, bf16[768,1024]{1,0:T(8,128)(2,1)S(1)} %fusion.39, f32[768,1024]{1,0:T(8,128)S(1)} %get-tuple-element.21, f32[768]{0:T(1024)S(1)} %add_sqrt_fusion.1), kind=kOutput, calls=%fused_computation.40 | convolution fusion | flops 1213069824 | bytes 7093248 | tf_op jit(solution)/shard_map/dot_general | solution.py:18
  68.3 2.7 %fusion.3 = bf16[768,2304]{1,0:T(8,128)(2,1)S(1)} fusion(f32[768,2304]{1,0:T(8,128)S(1)} %get-tuple-element.19, f32[768]{0:T(1024)S(1)} %get-tuple-element.10, f32[768]{0:T(1024)S(1)} %get-tuple-element.7, s32[2304]{0:T(1024)S(1)} %add.120, s32[768]{0:T(1024)S(1)} %reduce.3), kind=kLoop, calls=%fused_computation.8 | loop fusion | flops 14155776 | bytes 10635264 | tf_op jit(solution)/shard_map/convert_element_type | solution.py:25
  71.0 6.4 %fusion.17 = f32[768,1024]{1,0:T(8,128)S(1)} fusion(bf16[768,2304]{1,0:T(8,128)(2,1)S(1)} %fusion.3, f32[2304,1024]{0,1:T(8,128)} %get-tuple-element.18, f32[2304]{0:T(1024)S(1)} %add_sqrt_fusion), kind=kOutput, calls=%fused_computation.36 | convolution fusion | flops 3628597248 | bytes 16131072 | tf_op jit(solution)/shard_map/dot_general | solution.py:81
  77.5 9.3 %multiply_reduce_fusion = (f32[2304]{0:T(1024)S(1)}, f32[2304,1024]{0,1:T(8,128)}) fusion(f32[2304,1024]{0,1:T(8,128)} %get-tuple-element.18, f32[2304]{0:T(1024)S(1)} %add_sqrt_fusion, bf16[768,2304]{1,0:T(8,128)(2,1)S(1)} %fusion.3, bf16[768,1024]{1,0:T(8,128)(2,1)S(1)} %fusion.39), kind=kOutput, calls=%fused_computation.1 | convolution fusion | flops 3633313536 | bytes 24004608 | tf_op jit(solution)/shard_map/dot_general | solution.py:82
  86.8 1.8 multiply_reduce_fusion.2
  88.6 2.3 %multiply_reduce_fusion.3 = (f32[768]{0:T(1024)S(1)}, f32[768,1024]{1,0:T(8,128)S(1)}) fusion(f32[768,1024]{1,0:T(8,128)S(1)} %get-tuple-element.16, f32[768]{0:T(1024)S(1)} %add_sqrt_fusion.2, f32[768,1024]{1,0:T(8,128)S(1)} %fusion.17, f32[768,1024]{1,0:T(8,128)S(1)} %get-tuple-element.21, f32[768]{0:T(1024)S(1)} %add_sqrt_fusion.1, ...), kind=kOutput, calls=%fused_computation.22 | convolution fusion | flops 1218182400 | bytes 14963712 | tf_op jit(solution)/shard_map/dot_general | solution.py:81
  91.0 1.4 fusion.27
  92.4 9.3 %fusion.26 = f32[1,768,1024]{2,1,0:T(8,128)S(1)} fusion(f32[2304,1024]{0,1:T(8,128)} %get-tuple-element.24, f32[2304]{0:T(1024)S(1)} %get-tuple-element.23, f32[2304]{0:T(1024)S(1)} %add_sqrt_fusion, bf16[768,768]{0,1:T(8,128)(2,1)} %collective-permute-done.1, bf16[768,768]{0,1:T(8,128)(2,1)} %collective-permute-done, bf16[768,768]{0,1:T(8,128)(2,1)S(1)} %bitcast.48, ...), kind=kOutput, calls=%fused_computation.41 | convolution fusion | flops 3648651264 | bytes 25577472 | tf_op jit(solution)/shard_map/dot_general | solution.py:93
  101.7 2.6 %pad_add_fusion = f32[2,768,1024]{2,1,0:T(8,128)S(1)} fusion(f32[1,768,1024]{2,1,0:T(8,128)S(1)} %fusion.26, bf16[1,768,1024]{2,1,0:T(8,128)(2,1)S(1)} %get-tuple-element.30, bf16[1,768,1024]{2,1,0:T(8,128)(2,1)S(1)} %get-tuple-element.29, bf16[1,768,768]{1,2,0:T(8,128)(2,1)S(1)} %bitcast.49, bf16[1,768,768]{1,2,0:T(8,128)(2,1)S(1)} %copy-done.4), kind=kOutput, calls=%fused_computation.10 | convolution fusion | flops 2420244480 | bytes 14942208 | tf_op jit(solution)/shard_map/dot_general | solution.py:87
  104.3 3.2 %copy.24 = f32[2,4,4,2,24,1024]{5,4,1,0,2,3:T(8,128)} copy(f32[2,4,4,2,24,1024]{5,4,3,2,1,0:T(8,128)S(1)} %bitcast.42) | data formatting | bytes 12582912 | tf_op jit(solution)/shard_map/reshape | solution.py:102
  107.7 16.1 %reduce-scatter.3.cloned.1.call-done = f32[2,4,4,1,24,1024]{5,4,1,0,2,3:T(8,128)} async-done(((f32[2,4,4,2,24,1024]{5,4,1,0,2,3:T(8,128)}), f32[2,4,4,1,24,1024]{5,4,1,0,2,3:T(8,128)}) %reduce-scatter.3.cloned.1.call-update) | async-done | bytes 3145744 | tf_op jit(solution)/shard_map/reduce_scatter | solution.py:103
  123.8 1.5 pad_maximum_fusion.3
  125.9 10.1 %all-to-all-start = ((f32[128,1,2]{2,1,0:T(1,128)}), f32[128,1,2]{2,1,0:T(1,128)S(1)}, u32[]{:S(2)}, u32[]{:S(2)}) async-start(f32[128,1,2]{2,1,0:T(1,128)} %broadcast_in_dim.12), calls=%async_computation | async-start | bytes 131072 | tf_op jit(solution)/shard_map/all_to_all | solution.py:39
  136.0 30.2 %reduce-scatter.5.cloned.1.call-done = f32[2,4,1,24,1024]{4,3,1,0,2:T(8,128)} async-done(((f32[2,4,4,24,1024]{4,3,1,0,2:T(8,128)}), f32[2,4,1,24,1024]{4,3,1,0,2:T(8,128)}) %reduce-scatter.5.cloned.1.call-update) | async-done | bytes 786448 | tf_op jit(solution)/shard_map/reduce_scatter | solution.py:104
  166.2 1.5 reshape_reduce_scatter.3
  167.7 1.0 copy.25
  168.8 7.2 %all-to-all-start.1 = ((f32[16,2,24,256]{3,2,1,0:T(8,128)}), f32[16,2,24,256]{3,2,1,0:T(8,128)S(1)}, u32[]{:S(2)}, u32[]{:S(2)}) async-start(f32[16,2,24,256]{3,2,1,0:T(8,128)} %bitcast.16), calls=%async_computation.3 | async-start | bytes 1572864 | tf_op jit(solution)/shard_map/all_to_all | solution.py:108
  178.1 12.7 %all-to-all-done.1 = f32[16,2,24,256]{3,2,1,0:T(8,128)S(1)} async-done(((f32[16,2,24,256]{3,2,1,0:T(8,128)}), f32[16,2,24,256]{3,2,1,0:T(8,128)S(1)}, u32[]{:S(2)}, u32[]{:S(2)}) %all-to-all-start.1) | async-done | bytes 786464 | tf_op jit(solution)/shard_map/all_to_all | solution.py:108
  190.8 0.7 broadcast_divide_fusion.3
  (40 shorter events, 4.3 us)
Async XLA Ops:
  7.2 38.6 %copy-start = (bf16[768,1024]{1,0:T(8,128)(2,1)S(1)}, bf16[768,1024]{1,0:T(8,128)(2,1)}, u32[]{:S(2)}) copy-start(bf16[768,1024]{1,0:T(8,128)(2,1)} %param.11) | copy-start | bytes 4718596
  7.2 7.6 %copy-start.2 = (bf16[1,768,768]{2,1,0:T(8,128)(2,1)S(1)}, bf16[1,768,768]{2,1,0:T(8,128)(2,1)}, u32[]{:S(2)}) copy-start(bf16[1,768,768]{2,1,0:T(8,128)(2,1)} %param.6) | copy-start | bytes 3538948
  7.2 9.0 %copy-start.5 = (f32[1,768]{1,0:T(1,128)S(1)}, f32[1,768]{1,0:T(1,128)}, u32[]{:S(2)}) copy-start(f32[1,768]{1,0:T(1,128)} %param.9) | copy-start | bytes 9220
  7.2 116.6 %reduce-scatter.3.cloned.1.call-start = ((), (), s32[]{:S(2)}) async-start(), calls=%async_computation.4 | async-start | bytes 9437184 | tf_op jit(solution)/shard_map/reduce_scatter | solution.py:103
  9.8 30.4 %collective-permute-start.1 = (bf16[768,768]{0,1:T(8,128)(2,1)}, bf16[768,768]{0,1:T(8,128)(2,1)}, u32[]{:S(2)}, u32[]{:S(2)}) collective-permute-start(bf16[768,768]{0,1:T(8,128)(2,1)} %bitcast.45), channel_id=1, source_target_pairs={{0,1},{1,2},{2,3},{3,0},{4,5},{5,6},{6,7},{7,4},{8,9},{9,10},{10,1... | collective-permute-start | bytes 3538952 | tf_op jit(solution)/shard_map/ppermute | solution.py:51
  11.8 29.6 %collective-permute-start = (bf16[768,768]{0,1:T(8,128)(2,1)}, bf16[768,768]{0,1:T(8,128)(2,1)}, u32[]{:S(2)}, u32[]{:S(2)}) collective-permute-start(bf16[768,768]{0,1:T(8,128)(2,1)} %bitcast.46), channel_id=1, source_target_pairs={{0,3},{1,0},{2,1},{3,2},{4,7},{5,4},{6,5},{7,6},{8,11},{9,8},{10,9... | collective-permute-start | bytes 3538952 | tf_op jit(solution)/shard_map/ppermute | solution.py:50
  19.7 26.1 %copy-start.3 = (bf16[1,768,768]{1,2,0:T(8,128)(2,1)S(1)}, bf16[1,768,768]{1,2,0:T(8,128)(2,1)}, u32[]{:S(2)}) copy-start(bf16[1,768,768]{1,2,0:T(8,128)(2,1)} %copy.21) | copy-start | bytes 3538948
  41.3 21.5 %collective-permute-start.2 = (bf16[384,768]{0,1:T(8,128)(2,1)S(1)}, bf16[384,768]{0,1:T(8,128)(2,1)S(1)}, u32[]{:S(2)}, u32[]{:S(2)}) collective-permute-start(bf16[384,768]{0,1:T(8,128)(2,1)S(1)} %slice.16), channel_id=1, source_target_pairs={{0,1},{1,2},{2,3},{3,0},{4,5},{5,6},{6,7},{7,4},{8,9},{9,10},{10,1... | collective-permute-start | bytes 1769480 | tf_op jit(solution)/shard_map/ppermute | solution.py:53
  42.5 20.4 %collective-permute-start.3 = (bf16[384,768]{0,1:T(8,128)(2,1)S(1)}, bf16[384,768]{0,1:T(8,128)(2,1)S(1)}, u32[]{:S(2)}, u32[]{:S(2)}) collective-permute-start(bf16[384,768]{0,1:T(8,128)(2,1)S(1)} %slice.17), channel_id=1, source_target_pairs={{0,3},{1,0},{2,1},{3,2},{4,7},{5,4},{6,5},{7,6},{8,11},{9,8},{10,9... | collective-permute-start | bytes 1769480 | tf_op jit(solution)/shard_map/ppermute | solution.py:54
  77.5 9.3 %copy-start.6 = (f32[768,768]{0,1:T(8,128)S(1)}, f32[768,768]{0,1:T(8,128)}, u32[]{:S(2)}) copy-start(f32[768,768]{0,1:T(8,128)} %get-tuple-element.22) | copy-start | bytes 7077892
  92.4 9.3 %copy-start.4 = (bf16[1,768,768]{1,2,0:T(8,128)(2,1)S(1)}, bf16[1,768,768]{1,2,0:T(8,128)(2,1)}, u32[]{:S(2)}) copy-start(bf16[1,768,768]{1,2,0:T(8,128)(2,1)} %copy.23) | copy-start | bytes 3538948
  107.6 58.6 %reduce-scatter.5.cloned.1.call-start = ((), (), s32[]{:S(2)}) async-start(), calls=%async_computation.5 | async-start | bytes 3932160 | tf_op jit(solution)/shard_map/reduce_scatter | solution.py:104
  123.8 68.3 %copy-start.1 = (bf16[768,1024]{1,0:T(8,128)(2,1)S(1)}, bf16[768,1024]{1,0:T(8,128)(2,1)}, u32[]{:S(2)}) copy-start(bf16[768,1024]{1,0:T(8,128)(2,1)} %param.11) | copy-start | bytes 4718596
  125.9 42.8 %all-to-all-start = ((f32[128,1,2]{2,1,0:T(1,128)}), f32[128,1,2]{2,1,0:T(1,128)S(1)}, u32[]{:S(2)}, u32[]{:S(2)}) async-start(f32[128,1,2]{2,1,0:T(1,128)} %broadcast_in_dim.12), calls=%async_computation | async-start | bytes 131072 | tf_op jit(solution)/shard_map/all_to_all | solution.py:39
  168.8 22.0 %all-to-all-start.1 = ((f32[16,2,24,256]{3,2,1,0:T(8,128)}), f32[16,2,24,256]{3,2,1,0:T(8,128)S(1)}, u32[]{:S(2)}, u32[]{:S(2)}) async-start(f32[16,2,24,256]{3,2,1,0:T(8,128)} %bitcast.16), calls=%async_computation.3 | async-start | bytes 1572864 | tf_op jit(solution)/shard_map/all_to_all | solution.py:108
Sparse Core Ops, SparseCore 0:
  107.7 16.0 reduce-scatter.2
  126.3 39.8 reduce-scatter.4
